TPU v7x, 256 devices: a whole 4x4x8 slice. The times are simulated.
256 devices in a mesh: row: 16 (over y, x_lo, core), col: 16 (over x_hi, z).
Axes of the slice: x: 4 (x_hi: 2, x_lo: 2; x = x_hi * 2 + x_lo), y: 4, z: 8, core: 2. Of those that a mesh axis runs over, the one named last changes fastest.
Arguments:
- w_cycle: float32 [2048, 16384], P('col', 'row'), may hold values from -0.125 to 0.125
- amps: float32 [32, 512, 2048], P('col', 'row'), may hold values from -18 to 18
- eps_occ: float32 [32], replicated, may hold values from -3 to -0.3
- eps_vir: float32 [512], replicated, may hold values from 0.3 to 3
- occ_map: int32 [4], replicated, may hold values from 0 to 31
- vir_perm: int32 [512], replicated, may hold values from 0 to 511, each once
Outputs:
- cycle: float32 [16384, 16384], P('row', 'col')
Inputs may be any that keep to these rules, and one draw needn't show every extreme that they name: `occ_map`: each window index names one occupied orbital. `vir_perm`: each virtual orbital appears once.
All inputs are finite; a program needn't handle non-finite values.
Results may differ from a plain program's by a relative error of at most 0.000071.
Values sent between devices are 32-bit elements; how exact they have to be, the bound alone decides.
No kernel may reach another device: no remote copies, remote signals or barrier semaphores. Data moves between devices by JAX's collectives and lax.ppermute only.
A program may use at most 64 MiB of HBM per device.

v0:
```python
import jax
import jax.numpy as jnp
from jax import lax
from jax.sharding import PartitionSpec as P


def lookup(indices, table):
    onehot = (indices[:, None] == jnp.arange(table.shape[0], dtype=jnp.int32)[None, :]).astype(
        jnp.float32
    )
    return jnp.dot(
        onehot, table, precision=lax.Precision.HIGHEST, preferred_element_type=jnp.float32
    )


def body(w_cycle, amps, eps_occ, eps_vir, occ_map, vir_perm):
    virtual_count = eps_vir.shape[0]
    j_local = amps.shape[0]
    b_local = amps.shape[1]
    vir_energy = lookup(vir_perm, eps_vir)
    occ_energy = lookup(occ_map, eps_occ)
    pair_energy = (vir_energy[None, :] - occ_energy[:, None]).reshape(-1)
    j_index = jnp.arange(j_local, dtype=jnp.int32) + lax.axis_index("col") * j_local
    j_energy = lookup(j_index, eps_occ)
    b_energy = lax.dynamic_slice_in_dim(vir_energy, lax.axis_index("row") * b_local, b_local)
    denominator = pair_energy[None, None, :] + b_energy[None, :, None] - j_energy[:, None, None]
    scaled = amps / denominator
    w_whole = lax.all_gather(w_cycle, "col", axis=0, tiled=True)
    regrouped = lax.all_to_all(scaled, "row", split_axis=2, concat_axis=1, tiled=True)
    t_columns = regrouped.reshape(j_local * virtual_count, regrouped.shape[2])
    return lax.dot_general(
        w_whole,
        lax.all_gather(t_columns, "row", axis=1, tiled=True),
        (((0,), (1,)), ((), ())),
        precision=lax.Precision.HIGHEST,
        preferred_element_type=jnp.float32,
    )


def solution(mesh):
    placed = (P("col", "row"), P("col", "row", None), P(), P(), P(), P())
    return jax.shard_map(
        body, mesh=mesh, in_specs=placed, out_specs=P("row", "col"), check_vma=False
    )
```

profile of v0, /device:TPU:28, one launch (start us, length us, event | category | flops | bytes accessed | tf_op | source)
XLA Modules:
  0.0 254.5 jit_solution(9936301855552644138)
XLA Ops:
  6.5 0.0 copy-start
  6.5 0.0 all-gather.5.cloned.1.call-start
  6.5 0.7 all-gather.5.cloned.1.call-update
  7.3 0.0 all-gather.3.cloned.1.call-start
  7.3 0.0 copy-done
  7.3 1.3 fusion
  8.6 0.1 dynamic_slice.3
  8.7 0.9 convolution_bitcast_fusion.2
  9.6 0.1 subtract_bitcast_fusion
  9.7 0.8 convolution_bitcast_fusion.1
  10.5 0.1 broadcast_add_fusion
  10.6 1.2 subtract_divide_fusion
  11.8 1.0 copy.17
  12.9 2.1 reshape.65
  14.9 14.9 %all_to_all.15 = f32[16,1,8192]{2,1,0:T(1,128)S(1)} all-to-all(f32[16,1,8192]{2,1,0:T(1,128)S(1)} %reshape.65), channel_id=1, replica_groups=mesh['row'=16,'col'=16] {'row'}, dimensions={0} | all-to-all | bytes 1048576 | tf_op jit(solution)/shard_map/all_to_all | solution.py:29
  29.9 0.5 broadcast.35
  30.4 1.9 reduce
  32.3 1.8 reshape.66
  34.1 2.0 copy.22
  36.1 0.0 all-gather.3.cloned.1.call-update
  36.1 112.0 %all-gather.5.cloned.1.call-done = f32[2048,1024]{1,0:T(8,128)} async-done(((f32[128,1024]{1,0:T(8,128)}), f32[2048,1024]{1,0:T(8,128)}) %all-gather.5.cloned.1.call-update) | async-done | bytes 8388624 | tf_op jit(solution)/shard_map/all_gather | solution.py:28
  148.1 62.3 %all-gather.3.cloned.1.call-done = f32[1024,2048]{1,0:T(8,128)} async-done(((f32[1024,128]{1,0:T(8,128)}), f32[1024,2048]{1,0:T(8,128)}) %all-gather.3.cloned.1.call-update) | async-done | bytes 8388624 | tf_op jit(solution)/shard_map/all_gather | solution.py:33
  210.4 31.9 %convolution_bitcast_fusion = f32[1024,1024]{0,1:T(8,128)} fusion(f32[1024,2048]{1,0:T(8,128)} %all-gather.3.cloned.1.call-done, f32[2048,1024]{1,0:T(8,128)} %all-gather.5.cloned.1.call-done), kind=kOutput, calls=%fused_computation | convolution fusion | flops 25769803776 | bytes 20971520 | tf_op jit(solution)/shard_map/dot_general | solution.py:31
  242.3 5.3 %copy.20 = f32[1024,1024]{1,0:T(8,128)} copy(f32[1024,1024]{0,1:T(8,128)} %convolution_bitcast_fusion) | data formatting | bytes 8388608 | tf_op jit(solution)/shard_map/dot_general | solution.py:31
  (2 shorter events, 0.0 us)
Async XLA Ops:
  6.5 0.8 copy-start
  6.5 141.6 %all-gather.5.cloned.1.call-start = ((), (), s32[]{:S(2)}) async-start(), calls=%async_computation.2 | async-start | bytes 8912896 | tf_op jit(solution)/shard_map/all_gather | solution.py:28
  7.3 203.2 %all-gather.3.cloned.1.call-start = ((), (), s32[]{:S(2)}) async-start(), calls=%async_computation.1 | async-start | bytes 8912896 | tf_op jit(solution)/shard_map/all_gather | solution.py:33
Sparse Core Ops, SparseCore 0:
  9.9 138.1 all-gather.4
  149.9 60.5 all-gather.2
where the time goes:
time: 258 us; the launch traced here: 254 us
  waiting for transfers between devices  175 us (68%)
  matrix products  34.9 us (14%)
  blocking collectives  14.9 us (6%)
  between operations  13.5 us (5%)
  local copies, waits for them, and re-layouts  12.8 us (5%)
  other arithmetic  3.28 us (1%)
    all_gather x1, waiting for transfers between devices, body(): w_whole = lax.all_gather(w_cycle, 'col', axis=0, tiled=True)  112 us
    all_gather x1, waiting for transfers between devices, body(): lax.all_gather(t_columns, 'row', axis=1, tiled=True)  62.3 us
    dot_general x1, matrix products, body(): lax.dot_general(w_whole, lax.all_gather(t_columns, 'row', axis=1, tiled=T...  31.9 us
    all_to_all x1, blocking collectives, body(): lax.all_to_all(scaled, 'row', split_axis=2, concat_axis=1, tiled=True)  14.9 us
    dot_general x1, local copies, waits for them, and re-layouts, body(): lax.dot_general(w_whole, lax.all_gather(t_columns, 'row', axis=1, tiled=T...  5.34 us
  transfers between devices with their start and end apart: 2, of which 2 were waited for; matrix products, arithmetic and copies ran while one was open for 5% of the time, Pallas kernels for 0%

commit v1 on v0

v1 whole, which is shorter than its diff:
```python
import jax
import jax.numpy as jnp
from jax import lax
from jax.sharding import Mesh
from jax.sharding import PartitionSpec as P

ROW = ("y", "xlo", "core")
COL = ("xhi", "z")


def lookup(indices, table):
    onehot = (indices[:, None] == jnp.arange(table.shape[0], dtype=jnp.int32)[None, :]).astype(
        jnp.float32
    )
    return jnp.dot(
        onehot, table, precision=lax.Precision.HIGHEST, preferred_element_type=jnp.float32
    )


def body(w_cycle, amps, eps_occ, eps_vir, occ_map, vir_perm):
    nz = lax.axis_size("z")
    nxhi = lax.axis_size("xhi")
    z = lax.axis_index("z")
    xhi = lax.axis_index("xhi")
    col = xhi * nz + z
    row = (lax.axis_index("y") * lax.axis_size("xlo") + lax.axis_index("xlo")) * lax.axis_size(
        "core"
    ) + lax.axis_index("core")

    j_local, b_local, ck = amps.shape
    kw = occ_energy_count = occ_map.shape[0]
    del occ_energy_count
    blk = w_cycle.shape[0]

    vir_energy = lookup(vir_perm, eps_vir)
    occ_energy = lookup(occ_map, eps_occ)
    pair_energy = (vir_energy[None, :] - occ_energy[:, None]).reshape(-1)
    j_index = jnp.arange(j_local, dtype=jnp.int32) + col * j_local
    j_energy = lookup(j_index, eps_occ)
    b_energy = lax.dynamic_slice_in_dim(vir_energy, row * b_local, b_local)
    denominator = pair_energy[None, None, :] + b_energy[None, :, None] - j_energy[:, None, None]
    scaled = amps / denominator

    s5 = scaled.reshape(j_local, b_local, nxhi, nz, blk)
    s5 = jnp.where(xhi == 0, s5, s5[:, :, ::-1])
    s5 = jnp.roll(s5, -z, axis=3)
    s_perm = s5.transpose(0, 1, 3, 2, 4).reshape(j_local, b_local, ck)
    s_full = lax.all_gather(s_perm, ROW, axis=1, tiled=True)
    del kw

    w_other = lax.ppermute(w_cycle, "xhi", [(0, 1), (1, 0)])
    fwd = [(k, (k + 1) % nz) for k in range(nz)]
    bwd = [(k, (k - 1) % nz) for k in range(nz)]
    blocks = {0: [w_cycle, w_other]}
    f_own, f_oth = w_cycle, w_other
    b_own, b_oth = w_cycle, w_other
    half = nz // 2
    for s in range(1, half + 1):
        f_own = lax.ppermute(f_own, "z", fwd)
        b_oth = lax.ppermute(b_oth, "z", bwd)
        if s < half:
            f_oth = lax.ppermute(f_oth, "z", fwd)
            b_own = lax.ppermute(b_own, "z", bwd)
            blocks[nz - s] = [f_own, f_oth]
            blocks[s] = [b_own, b_oth]
        else:
            blocks[s] = [f_own, b_oth]
    w_full = jnp.concatenate([blocks[d][t] for d in range(nz) for t in range(nxhi)], axis=0)

    return lax.dot_general(
        w_full,
        s_full.reshape(j_local * s_full.shape[1], ck),
        (((0,), (1,)), ((), ())),
        precision=lax.Precision.HIGH,
        preferred_element_type=jnp.float32,
    )


def solution(mesh):
    nrow, ncol = mesh.devices.shape
    ncore = 2
    nxlo = 2
    nxhi = 2
    devices = mesh.devices.reshape(
        nrow // (nxlo * ncore), nxlo, ncore, nxhi, ncol // nxhi
    )
    fine = Mesh(devices, ("y", "xlo", "core", "xhi", "z"))
    placed = (P(COL, ROW), P(COL, ROW, None), P(), P(), P(), P())
    return jax.shard_map(
        body, mesh=fine, in_specs=placed, out_specs=P(ROW, COL), check_vma=False
    )
```

time: 258 us -> 160 us (0.62); the launches traced: 254 us -> 160 us
  waiting for transfers between devices: 175 us -> 60.1 us
  starting transfers between devices: 0.04 us -> 32.3 us
  blocking collectives: 14.9 us -> 0 us
  local copies, waits for them, and re-layouts: 12.8 us -> 16.5 us
    all_gather x2 -> x1, waiting for transfers between devices: 174 us -> 0.01 us  [body(): s_full = lax.all_gather(s_perm, ROW, axis=1, tiled=True)]
    ppermute x0 -> x15, waiting for transfers between devices: none -> 60.1 us  [the longest x4 27.2 us: body(): b_oth = lax.ppermute(b_oth, 'z', bwd)]
    ppermute x0 -> x15, starting transfers between devices: none -> 32.3 us  [the longest x4 20.3 us: body(): b_oth = lax.ppermute(b_oth, 'z', bwd)]
    all_to_all x1 -> x0, blocking collectives: 14.9 us -> none  [body(): lax.all_to_all(scaled, 'row', split_axis=2, concat_axis=1, tiled=True)]
    unnamed x5 -> x21, local copies, waits for them, and re-layouts: 3.85 us -> 12.8 us
    dot_general x1 -> x0, local copies, waits for them, and re-layouts: 5.34 us -> none  [body(): lax.dot_general(w_whole, lax.all_gather(t_columns, 'row', axis=1, tiled=T...]
  transfers between devices with their start and end apart: 2 -> 16, of which waited for: 2 -> 8; matrix products, arithmetic and copies ran while one was open for 5% -> 8% of each run, Pallas kernels for 0% -> 0%
where the time goes in v1:
time: 160 us
  waiting for transfers between devices  60.1 us (38%)
  matrix products  35.4 us (22%)
  starting transfers between devices  32.3 us (20%)
  local copies, waits for them, and re-layouts  16.5 us (10%)
  between operations  13.5 us (8%)
  other arithmetic  2.11 us (1%)
    dot_general x1, matrix products, body(): lax.dot_general(w_full, s_full.reshape(j_local * s_full.shape[1], ck), ((...  32.3 us
    ppermute x4, waiting for transfers between devices, body(): b_oth = lax.ppermute(b_oth, 'z', bwd)  27.2 us
    ppermute x4, starting transfers between devices, body(): b_oth = lax.ppermute(b_oth, 'z', bwd)  20.3 us
    ppermute x3, waiting for transfers between devices, body(): b_own = lax.ppermute(b_own, 'z', bwd)  20.1 us
    unnamed x21, local copies, waits for them, and re-layouts  12.8 us
    ppermute x1, waiting for transfers between devices, body(): w_other = lax.ppermute(w_cycle, 'xhi', [(0, 1), (1, 0)])  12.7 us
    ppermute x3, starting transfers between devices, body(): b_own = lax.ppermute(b_own, 'z', bwd)  8.03 us
    ppermute x4, starting transfers between devices, body(): f_own = lax.ppermute(f_own, 'z', fwd)  3.3 us
  transfers between devices with their start and end apart: 16, of which 8 were waited for; matrix products, arithmetic and copies ran while one was open for 8% of the time, Pallas kernels for 0%

profile of v1, /device:TPU:28, one launch (start us, length us, event | category | flops | bytes accessed | tf_op | source)
XLA Modules:
  0.0 159.9 jit_solution(4905176820862268753)
XLA Ops:
  6.6 0.9 convolution_bitcast_fusion
  7.5 0.9 convolution_bitcast_fusion.1
  8.3 1.3 fusion
  9.9 1.2 subtract_divide_fusion
  11.5 1.3 rev.3
  13.6 1.2 reshape.64
  15.4 1.9 %collective-permute-start.7 = (f32[128,1024]{1,0:T(8,128)S(1)}, f32[128,1024]{1,0:T(8,128)S(1)}, u32[]{:S(2)}, u32[]{:S(2)}) collective-permute-start(f32[128,1024]{1,0:T(8,128)S(1)} %copy-done.1), channel_id=1, source_target_pairs={{0,1},{1,2},{2,3},{3,4},{4,5},{5,6},{6,7},{7,0},{8,9},{9,10},{10,1... | collective-permute-start | bytes 1572872 | tf_op jit(solution)/shard_map/ppermute | solution.py:59
  17.3 12.7 %collective-permute-done = f32[128,1024]{1,0:T(8,128)S(1)} collective-permute-done((f32[128,1024]{1,0:T(8,128)S(1)}, f32[128,1024]{1,0:T(8,128)S(1)}, u32[]{:S(2)}, u32[]{:S(2)}) %collective-permute-start) | collective-permute-done | bytes 524320 | tf_op jit(solution)/shard_map/ppermute | solution.py:51
  30.1 9.3 %collective-permute-start.2 = (f32[128,1024]{1,0:T(8,128)S(1)}, f32[128,1024]{1,0:T(8,128)S(1)}, u32[]{:S(2)}, u32[]{:S(2)}) collective-permute-start(f32[128,1024]{1,0:T(8,128)S(1)} %collective-permute-done), channel_id=1, source_target_pairs={{0,7},{1,0},{2,1},{3,2},{4,3},{5,4},{6,5},{7,6},{8,15},{9,8},{10,9... | collective-permute-start | bytes 1572872 | tf_op jit(solution)/shard_map/ppermute | solution.py:60
  40.0 1.4 collective-permute-start.8
  41.4 10.3 %collective-permute-done.2 = f32[128,1024]{1,0:T(8,128)S(1)} collective-permute-done((f32[128,1024]{1,0:T(8,128)S(1)}, f32[128,1024]{1,0:T(8,128)S(1)}, u32[]{:S(2)}, u32[]{:S(2)}) %collective-permute-start.2) | collective-permute-done | bytes 524320 | tf_op jit(solution)/shard_map/ppermute | solution.py:60
  51.7 3.7 %collective-permute-start.4 = (f32[128,1024]{1,0:T(8,128)S(1)}, f32[128,1024]{1,0:T(8,128)S(1)}, u32[]{:S(2)}, u32[]{:S(2)}) collective-permute-start(f32[128,1024]{1,0:T(8,128)S(1)} %collective-permute-done.2), channel_id=1, source_target_pairs={{0,7},{1,0},{2,1},{3,2},{4,3},{5,4},{6,5},{7,6},{8,15},{9,8},{10,9... | collective-permute-start | bytes 1572872 | tf_op jit(solution)/shard_map/ppermute | solution.py:60
  55.4 7.5 %collective-permute-done.1 = f32[128,1024]{1,0:T(8,128)S(1)} collective-permute-done((f32[128,1024]{1,0:T(8,128)S(1)}, f32[128,1024]{1,0:T(8,128)S(1)}, u32[]{:S(2)}, u32[]{:S(2)}) %collective-permute-start.1) | collective-permute-done | bytes 524320 | tf_op jit(solution)/shard_map/ppermute | solution.py:63
  62.9 3.7 %collective-permute-start.3 = (f32[128,1024]{1,0:T(8,128)S(1)}, f32[128,1024]{1,0:T(8,128)S(1)}, u32[]{:S(2)}, u32[]{:S(2)}) collective-permute-start(f32[128,1024]{1,0:T(8,128)S(1)} %collective-permute-done.1), channel_id=1, source_target_pairs={{0,7},{1,0},{2,1},{3,2},{4,3},{5,4},{6,5},{7,6},{8,15},{9,8},{10,9... | collective-permute-start | bytes 1572872 | tf_op jit(solution)/shard_map/ppermute | solution.py:63
  66.6 7.5 %collective-permute-done.4 = f32[128,1024]{1,0:T(8,128)S(1)} collective-permute-done((f32[128,1024]{1,0:T(8,128)S(1)}, f32[128,1024]{1,0:T(8,128)S(1)}, u32[]{:S(2)}, u32[]{:S(2)}) %collective-permute-start.4) | collective-permute-done | bytes 524320 | tf_op jit(solution)/shard_map/ppermute | solution.py:60
  74.2 3.7 %collective-permute-start.6 = (f32[128,1024]{1,0:T(8,128)S(1)}, f32[128,1024]{1,0:T(8,128)S(1)}, u32[]{:S(2)}, u32[]{:S(2)}) collective-permute-start(f32[128,1024]{1,0:T(8,128)S(1)} %collective-permute-done.4), channel_id=1, source_target_pairs={{0,7},{1,0},{2,1},{3,2},{4,3},{5,4},{6,5},{7,6},{8,15},{9,8},{10,9... | collective-permute-start | bytes 1572872 | tf_op jit(solution)/shard_map/ppermute | solution.py:60
  77.8 0.9 constant_dynamic-update-slice_fusion.15
  78.7 6.7 %collective-permute-done.3 = f32[128,1024]{1,0:T(8,128)S(1)} collective-permute-done((f32[128,1024]{1,0:T(8,128)S(1)}, f32[128,1024]{1,0:T(8,128)S(1)}, u32[]{:S(2)}, u32[]{:S(2)}) %collective-permute-start.3) | collective-permute-done | bytes 524320 | tf_op jit(solution)/shard_map/ppermute | solution.py:63
  85.4 3.7 %collective-permute-start.5 = (f32[128,1024]{1,0:T(8,128)S(1)}, f32[128,1024]{1,0:T(8,128)S(1)}, u32[]{:S(2)}, u32[]{:S(2)}) collective-permute-start(f32[128,1024]{1,0:T(8,128)S(1)} %collective-permute-done.3), channel_id=1, source_target_pairs={{0,7},{1,0},{2,1},{3,2},{4,3},{5,4},{6,5},{7,6},{8,15},{9,8},{10,9... | collective-permute-start | bytes 1572872 | tf_op jit(solution)/shard_map/ppermute | solution.py:63
  89.1 0.9 constant_dynamic-update-slice_fusion.14
  90.8 0.8 constant_dynamic-update-slice_fusion.12
  91.6 5.0 %collective-permute-done.6 = f32[128,1024]{1,0:T(8,128)S(1)} collective-permute-done((f32[128,1024]{1,0:T(8,128)S(1)}, f32[128,1024]{1,0:T(8,128)S(1)}, u32[]{:S(2)}, u32[]{:S(2)}) %collective-permute-start.6) | collective-permute-done | bytes 524320 | tf_op jit(solution)/shard_map/ppermute | solution.py:60
  96.6 3.7 %collective-permute-start.11 = (f32[128,1024]{1,0:T(8,128)S(1)}, f32[128,1024]{1,0:T(8,128)S(1)}, u32[]{:S(2)}, u32[]{:S(2)}) collective-permute-start(f32[128,1024]{1,0:T(8,128)S(1)} %collective-permute-done.6), channel_id=1, source_target_pairs={{0,7},{1,0},{2,1},{3,2},{4,3},{5,4},{6,5},{7,6},{8,15},{9,8},{10,9... | collective-permute-start | bytes 1572872 | tf_op jit(solution)/shard_map/ppermute | solution.py:60
  102.0 5.9 %collective-permute-done.5 = f32[128,1024]{1,0:T(8,128)S(1)} collective-permute-done((f32[128,1024]{1,0:T(8,128)S(1)}, f32[128,1024]{1,0:T(8,128)S(1)}, u32[]{:S(2)}, u32[]{:S(2)}) %collective-permute-start.5) | collective-permute-done | bytes 524320 | tf_op jit(solution)/shard_map/ppermute | solution.py:63
  109.5 0.9 constant_dynamic-update-slice_fusion.7
  110.4 4.4 %collective-permute-done.11 = f32[128,1024]{1,0:T(8,128)S(1)} collective-permute-done((f32[128,1024]{1,0:T(8,128)S(1)}, f32[128,1024]{1,0:T(8,128)S(1)}, u32[]{:S(2)}, u32[]{:S(2)}) %collective-permute-start.11) | collective-permute-done | bytes 524320 | tf_op jit(solution)/shard_map/ppermute | solution.py:60
  115.7 0.9 constant_dynamic-update-slice_fusion.5
  116.5 0.8 constant_dynamic-update-slice_fusion.4
  118.2 0.8 constant_dynamic-update-slice_fusion.2
  119.1 0.8 constant_dynamic-update-slice_fusion.1
  119.9 0.8 constant_dynamic-update-slice_fusion
  120.8 32.3 %fusion.10 = f32[1024,1024]{1,0:T(8,128)} fusion(f32[2048,1024]{1,0:T(8,128)} %constant_dynamic-update-slice_fusion, f32[1024,2048]{1,0:T(8,128)} %bitcast.32), kind=kOutput, calls=%fused_computation.37 | convolution fusion | flops 12884901888 | bytes 20971520 | tf_op jit(solution)/shard_map/dot_general | solution.py:70
  (37 shorter events, 8.5 us)
Async XLA Ops:
  6.5 1.8 %copy-start = (f32[512]{0:T(512)S(1)}, f32[512]{0:T(512)}, u32[]{:S(2)}) copy-start(f32[512]{0:T(512)} %param.9) | copy-start | bytes 6148
  6.5 8.3 %copy-start.1 = (f32[128,1024]{1,0:T(8,128)S(1)}, f32[128,1024]{1,0:T(8,128)}, u32[]{:S(2)}) copy-start(f32[128,1024]{1,0:T(8,128)} %param.6) | copy-start | bytes 1572868
  6.5 114.2 %all-gather.2.cloned.1.call-start = ((), (), s32[]{:S(2)}) async-start(), calls=%async_computation | async-start | bytes 8912896 | tf_op jit(solution)/shard_map/all_gather | solution.py:48
  14.8 15.3 %collective-permute-start = (f32[128,1024]{1,0:T(8,128)S(1)}, f32[128,1024]{1,0:T(8,128)S(1)}, u32[]{:S(2)}, u32[]{:S(2)}) collective-permute-start(f32[128,1024]{1,0:T(8,128)S(1)} %copy-done.1), channel_id=1, source_target_pairs={{0,8},{8,0},{1,9},{9,1},{2,10},{10,2},{3,11},{11,3},{4,12},{12,4},... | collective-permute-start | bytes 1572872 | tf_op jit(solution)/shard_map/ppermute | solution.py:51
  15.4 24.6 %collective-permute-start.7 = (f32[128,1024]{1,0:T(8,128)S(1)}, f32[128,1024]{1,0:T(8,128)S(1)}, u32[]{:S(2)}, u32[]{:S(2)}) collective-permute-start(f32[128,1024]{1,0:T(8,128)S(1)} %copy-done.1), channel_id=1, source_target_pairs={{0,1},{1,2},{2,3},{3,4},{4,5},{5,6},{6,7},{7,0},{8,9},{9,10},{10,1... | collective-permute-start | bytes 1572872 | tf_op jit(solution)/shard_map/ppermute | solution.py:59
  30.1 21.6 %collective-permute-start.2 = (f32[128,1024]{1,0:T(8,128)S(1)}, f32[128,1024]{1,0:T(8,128)S(1)}, u32[]{:S(2)}, u32[]{:S(2)}) collective-permute-start(f32[128,1024]{1,0:T(8,128)S(1)} %collective-permute-done), channel_id=1, source_target_pairs={{0,7},{1,0},{2,1},{3,2},{4,3},{5,4},{6,5},{7,6},{8,15},{9,8},{10,9... | collective-permute-start | bytes 1572872 | tf_op jit(solution)/shard_map/ppermute | solution.py:60
  39.4 23.5 %collective-permute-start.1 = (f32[128,1024]{1,0:T(8,128)S(1)}, f32[128,1024]{1,0:T(8,128)S(1)}, u32[]{:S(2)}, u32[]{:S(2)}) collective-permute-start(f32[128,1024]{1,0:T(8,128)S(1)} %copy-done.1), channel_id=1, source_target_pairs={{0,7},{1,0},{2,1},{3,2},{4,3},{5,4},{6,5},{7,6},{8,15},{9,8},{10,9... | collective-permute-start | bytes 1572872 | tf_op jit(solution)/shard_map/ppermute | solution.py:63
  40.0 26.6 %collective-permute-start.8 = (f32[128,1024]{1,0:T(8,128)S(1)}, f32[128,1024]{1,0:T(8,128)S(1)}, u32[]{:S(2)}, u32[]{:S(2)}) collective-permute-start(f32[128,1024]{1,0:T(8,128)S(1)} %collective-permute-done.7), channel_id=1, source_target_pairs={{0,1},{1,2},{2,3},{3,4},{4,5},{5,6},{6,7},{7,0},{8,9},{9,10},{10,1... | collective-permute-start | bytes 1572872 | tf_op jit(solution)/shard_map/ppermute | solution.py:59
  51.7 22.5 %collective-permute-start.4 = (f32[128,1024]{1,0:T(8,128)S(1)}, f32[128,1024]{1,0:T(8,128)S(1)}, u32[]{:S(2)}, u32[]{:S(2)}) collective-permute-start(f32[128,1024]{1,0:T(8,128)S(1)} %collective-permute-done.2), channel_id=1, source_target_pairs={{0,7},{1,0},{2,1},{3,2},{4,3},{5,4},{6,5},{7,6},{8,15},{9,8},{10,9... | collective-permute-start | bytes 1572872 | tf_op jit(solution)/shard_map/ppermute | solution.py:60
  55.4 22.5 %collective-permute-start.12 = (f32[128,1024]{1,0:T(8,128)S(1)}, f32[128,1024]{1,0:T(8,128)S(1)}, u32[]{:S(2)}, u32[]{:S(2)}) collective-permute-start(f32[128,1024]{1,0:T(8,128)S(1)} %collective-permute-done), channel_id=1, source_target_pairs={{0,1},{1,2},{2,3},{3,4},{4,5},{5,6},{6,7},{7,0},{8,9},{9,10},{10,1... | collective-permute-start | bytes 1572872 | tf_op jit(solution)/shard_map/ppermute | solution.py:62
  62.9 22.5 %collective-permute-start.3 = (f32[128,1024]{1,0:T(8,128)S(1)}, f32[128,1024]{1,0:T(8,128)S(1)}, u32[]{:S(2)}, u32[]{:S(2)}) collective-permute-start(f32[128,1024]{1,0:T(8,128)S(1)} %collective-permute-done.1), channel_id=1, source_target_pairs={{0,7},{1,0},{2,1},{3,2},{4,3},{5,4},{6,5},{7,6},{8,15},{9,8},{10,9... | collective-permute-start | bytes 1572872 | tf_op jit(solution)/shard_map/ppermute | solution.py:63
  66.6 24.2 %collective-permute-start.9 = (f32[128,1024]{1,0:T(8,128)S(1)}, f32[128,1024]{1,0:T(8,128)S(1)}, u32[]{:S(2)}, u32[]{:S(2)}) collective-permute-start(f32[128,1024]{1,0:T(8,128)S(1)} %collective-permute-done.8), channel_id=1, source_target_pairs={{0,1},{1,2},{2,3},{3,4},{4,5},{5,6},{6,7},{7,0},{8,9},{9,10},{10,1... | collective-permute-start | bytes 1572872 | tf_op jit(solution)/shard_map/ppermute | solution.py:59
  74.2 22.5 %collective-permute-start.6 = (f32[128,1024]{1,0:T(8,128)S(1)}, f32[128,1024]{1,0:T(8,128)S(1)}, u32[]{:S(2)}, u32[]{:S(2)}) collective-permute-start(f32[128,1024]{1,0:T(8,128)S(1)} %collective-permute-done.4), channel_id=1, source_target_pairs={{0,7},{1,0},{2,1},{3,2},{4,3},{5,4},{6,5},{7,6},{8,15},{9,8},{10,9... | collective-permute-start | bytes 1572872 | tf_op jit(solution)/shard_map/ppermute | solution.py:60
  77.8 23.3 %collective-permute-start.13 = (f32[128,1024]{1,0:T(8,128)S(1)}, f32[128,1024]{1,0:T(8,128)S(1)}, u32[]{:S(2)}, u32[]{:S(2)}) collective-permute-start(f32[128,1024]{1,0:T(8,128)S(1)} %collective-permute-done.12), channel_id=1, source_target_pairs={{0,1},{1,2},{2,3},{3,4},{4,5},{5,6},{6,7},{7,0},{8,9},{9,10},{10,1... | collective-permute-start | bytes 1572872 | tf_op jit(solution)/shard_map/ppermute | solution.py:62
  85.4 22.5 %collective-permute-start.5 = (f32[128,1024]{1,0:T(8,128)S(1)}, f32[128,1024]{1,0:T(8,128)S(1)}, u32[]{:S(2)}, u32[]{:S(2)}) collective-permute-start(f32[128,1024]{1,0:T(8,128)S(1)} %collective-permute-done.3), channel_id=1, source_target_pairs={{0,7},{1,0},{2,1},{3,2},{4,3},{5,4},{6,5},{7,6},{8,15},{9,8},{10,9... | collective-permute-start | bytes 1572872 | tf_op jit(solution)/shard_map/ppermute | solution.py:63
  90.8 18.8 %collective-permute-start.10 = (f32[128,1024]{1,0:T(8,128)S(1)}, f32[128,1024]{1,0:T(8,128)S(1)}, u32[]{:S(2)}, u32[]{:S(2)}) collective-permute-start(f32[128,1024]{1,0:T(8,128)S(1)} %collective-permute-done.9), channel_id=1, source_target_pairs={{0,1},{1,2},{2,3},{3,4},{4,5},{5,6},{6,7},{7,0},{8,9},{9,10},{10,1... | collective-permute-start | bytes 1572872 | tf_op jit(solution)/shard_map/ppermute | solution.py:59
  96.6 18.2 %collective-permute-start.11 = (f32[128,1024]{1,0:T(8,128)S(1)}, f32[128,1024]{1,0:T(8,128)S(1)}, u32[]{:S(2)}, u32[]{:S(2)}) collective-permute-start(f32[128,1024]{1,0:T(8,128)S(1)} %collective-permute-done.6), channel_id=1, source_target_pairs={{0,7},{1,0},{2,1},{3,2},{4,3},{5,4},{6,5},{7,6},{8,15},{9,8},{10,9... | collective-permute-start | bytes 1572872 | tf_op jit(solution)/shard_map/ppermute | solution.py:60
  101.1 15.4 %collective-permute-start.14 = (f32[128,1024]{1,0:T(8,128)S(1)}, f32[128,1024]{1,0:T(8,128)S(1)}, u32[]{:S(2)}, u32[]{:S(2)}) collective-permute-start(f32[128,1024]{1,0:T(8,128)S(1)} %collective-permute-done.13), channel_id=1, source_target_pairs={{0,1},{1,2},{2,3},{3,4},{4,5},{5,6},{6,7},{7,0},{8,9},{9,10},{10,1... | collective-permute-start | bytes 1572872 | tf_op jit(solution)/shard_map/ppermute | solution.py:62
Sparse Core Ops, SparseCore 0:
  14.9 56.9 all-gather.1

commit v2 on v1

--- a/solution.py
+++ b/solution.py
@@ -15,6 +15,11 @@
     return jnp.dot(
         onehot, table, precision=lax.Precision.HIGHEST, preferred_element_type=jnp.float32
     )
+
+
+def split_bf16(x):
+    hi = lax.reduce_precision(x, exponent_bits=8, mantissa_bits=7)
+    return hi.astype(jnp.bfloat16), (x - hi).astype(jnp.bfloat16)
 
 
 def body(w_cycle, amps, eps_occ, eps_vir, occ_map, vir_perm):
@@ -65,15 +70,23 @@
             blocks[s] = [b_own, b_oth]
         else:
             blocks[s] = [f_own, b_oth]
-    w_full = jnp.concatenate([blocks[d][t] for d in range(nz) for t in range(nxhi)], axis=0)
-
-    return lax.dot_general(
-        w_full,
-        s_full.reshape(j_local * s_full.shape[1], ck),
-        (((0,), (1,)), ((), ())),
-        precision=lax.Precision.HIGH,
-        preferred_element_type=jnp.float32,
-    )
+    s_cols = s_full.reshape(j_local * s_full.shape[1], ck)
+    s_hi, s_lo = split_bf16(s_cols)
+    width = nxhi * blk
+    out = None
+    for group in ([0], [1, nz - 1], [2, nz - 2], [3, nz - 3], [half]):
+        w_g = jnp.concatenate([blocks[d][t] for d in group for t in range(nxhi)], axis=0)
+        w_hi, w_lo = split_bf16(w_g)
+        sl = [slice(d * width, (d + 1) * width) for d in group]
+        sh_g = jnp.concatenate([s_hi[:, c] for c in sl], axis=1)
+        sl_g = jnp.concatenate([s_lo[:, c] for c in sl], axis=1)
+        lhs = jnp.concatenate([w_hi, w_hi, w_lo], axis=0)
+        rhs = jnp.concatenate([sh_g, sl_g, sh_g], axis=1)
+        part = lax.dot_general(
+            lhs, rhs, (((0,), (1,)), ((), ())), preferred_element_type=jnp.float32
+        )
+        out = part if out is None else out + part
+    return out
 
 
 def solution(mesh):

time: 160 us -> 141 us (0.88)
  matrix products: 35.4 us -> 19.7 us
  other arithmetic: 2.11 us -> 12.7 us
  local copies, waits for them, and re-layouts: 16.5 us -> 6.45 us
  waiting for transfers between devices: 60.1 us -> 54.4 us
    ppermute x4, waiting for transfers between devices: 0.01 us -> 21.8 us  [body(): f_own = lax.ppermute(f_own, 'z', fwd)]
    dot_general x1 -> x5, matrix products: 32.3 us -> 16.7 us  [body(): lax.dot_general(lhs, rhs, (((0,), (1,)), ((), ())), preferred_element_typ...]
    ppermute x3, waiting for transfers between devices: 20.1 us -> 7.54 us  [body(): b_own = lax.ppermute(b_own, 'z', bwd)]
    ppermute x4, waiting for transfers between devices: 27.2 us -> 16.3 us  [body(): b_oth = lax.ppermute(b_oth, 'z', bwd)]
    convert_element_type x0 -> x6, other arithmetic: none -> 10.6 us  [split_bf16(): return (hi.astype(jnp.bfloat16), (x - hi).astype(jnp.bfloat16))]
    unnamed x21 -> x34, local copies, waits for them, and re-layouts: 12.8 us -> 2.88 us
    ppermute x3, starting transfers between devices: 8.03 us -> 12.8 us  [body(): b_own = lax.ppermute(b_own, 'z', bwd)]
    ppermute x1, waiting for transfers between devices: 12.7 us -> 8.75 us  [body(): w_other = lax.ppermute(w_cycle, 'xhi', [(0, 1), (1, 0)])]
  transfers between devices with their start and end apart: 16 -> 16, of which waited for: 8 -> 7; matrix products, arithmetic and copies ran while one was open for 8% -> 4% of each run, Pallas kernels for 0% -> 0%
where the time goes in v2:
time: 141 us
  waiting for transfers between devices  54.4 us (39%)
  starting transfers between devices  33.7 us (24%)
  matrix products  19.7 us (14%)
  between operations  13.8 us (10%)
  other arithmetic  12.7 us (9%)
  local copies, waits for them, and re-layouts  6.45 us (5%)
    ppermute x4, waiting for transfers between devices, body(): f_own = lax.ppermute(f_own, 'z', fwd)  21.8 us
    ppermute x4, starting transfers between devices, body(): b_oth = lax.ppermute(b_oth, 'z', bwd)  20.3 us
    dot_general x5, matrix products, body(): lax.dot_general(lhs, rhs, (((0,), (1,)), ((), ())), preferred_element_typ...  16.7 us
    ppermute x4, waiting for transfers between devices, body(): b_oth = lax.ppermute(b_oth, 'z', bwd)  16.3 us
    ppermute x3, starting transfers between devices, body(): b_own = lax.ppermute(b_own, 'z', bwd)  12.8 us
    convert_element_type x6, other arithmetic, split_bf16(): return (hi.astype(jnp.bfloat16), (x - hi).astype(jnp.bfloat16))  10.6 us
    ppermute x1, waiting for transfers between devices, body(): w_other = lax.ppermute(w_cycle, 'xhi', [(0, 1), (1, 0)])  8.75 us
    ppermute x3, waiting for transfers between devices, body(): b_own = lax.ppermute(b_own, 'z', bwd)  7.54 us
  transfers between devices with their start and end apart: 16, of which 7 were waited for; matrix products, arithmetic and copies ran while one was open for 4% of the time, Pallas kernels for 0%

profile of v2, /device:TPU:28, one launch (start us, length us, event | category | flops | bytes accessed | tf_op | source)
XLA Modules:
  0.0 140.9 jit_solution(3453443945678285630)
XLA Ops:
  6.5 0.7 copy-done
  7.2 1.3 fusion.50
  8.6 0.9 convolution_bitcast_fusion.1
  9.6 0.8 convolution_bitcast_fusion
  10.5 1.2 subtract_divide_fusion
  12.1 1.3 rev.3
  14.2 1.2 reshape.64
  15.5 0.6 collective-permute-start
  16.1 5.9 %collective-permute-start.1 = (f32[128,1024]{1,0:T(8,128)S(1)}, f32[128,1024]{1,0:T(8,128)S(1)}, u32[]{:S(2)}, u32[]{:S(2)}) collective-permute-start(f32[128,1024]{1,0:T(8,128)S(1)} %copy-done.6), channel_id=1, source_target_pairs={{0,7},{1,0},{2,1},{3,2},{4,3},{5,4},{6,5},{7,6},{8,15},{9,8},{10,9... | collective-permute-start | bytes 1572872 | tf_op jit(solution)/shard_map/ppermute | solution.py:68
  22.0 8.8 %collective-permute-done = f32[128,1024]{1,0:T(8,128)S(1)} collective-permute-done((f32[128,1024]{1,0:T(8,128)S(1)}, f32[128,1024]{1,0:T(8,128)S(1)}, u32[]{:S(2)}, u32[]{:S(2)}) %collective-permute-start) | collective-permute-done | bytes 524320 | tf_op jit(solution)/shard_map/ppermute | solution.py:56
  30.7 9.3 %collective-permute-start.2 = (f32[128,1024]{1,0:T(8,128)S(1)}, f32[128,1024]{1,0:T(8,128)S(1)}, u32[]{:S(2)}, u32[]{:S(2)}) collective-permute-start(f32[128,1024]{1,0:T(8,128)S(1)} %collective-permute-done), channel_id=1, source_target_pairs={{0,7},{1,0},{2,1},{3,2},{4,3},{5,4},{6,5},{7,6},{8,15},{9,8},{10,9... | collective-permute-start | bytes 1572872 | tf_op jit(solution)/shard_map/ppermute | solution.py:65
  40.0 3.2 %collective-permute-start.5 = (f32[128,1024]{1,0:T(8,128)S(1)}, f32[128,1024]{1,0:T(8,128)S(1)}, u32[]{:S(2)}, u32[]{:S(2)}) collective-permute-start(f32[128,1024]{1,0:T(8,128)S(1)} %collective-permute-done.1), channel_id=1, source_target_pairs={{0,7},{1,0},{2,1},{3,2},{4,3},{5,4},{6,5},{7,6},{8,15},{9,8},{10,9... | collective-permute-start | bytes 1572872 | tf_op jit(solution)/shard_map/ppermute | solution.py:68
  43.3 1.2 reduce-precision_convert_fusion.5
  44.6 7.8 %collective-permute-done.2 = f32[128,1024]{1,0:T(8,128)S(1)} collective-permute-done((f32[128,1024]{1,0:T(8,128)S(1)}, f32[128,1024]{1,0:T(8,128)S(1)}, u32[]{:S(2)}, u32[]{:S(2)}) %collective-permute-start.2) | collective-permute-done | bytes 524320 | tf_op jit(solution)/shard_map/ppermute | solution.py:65
  52.3 3.7 %collective-permute-start.6 = (f32[128,1024]{1,0:T(8,128)S(1)}, f32[128,1024]{1,0:T(8,128)S(1)}, u32[]{:S(2)}, u32[]{:S(2)}) collective-permute-start(f32[128,1024]{1,0:T(8,128)S(1)} %collective-permute-done.2), channel_id=1, source_target_pairs={{0,7},{1,0},{2,1},{3,2},{4,3},{5,4},{6,5},{7,6},{8,15},{9,8},{10,9... | collective-permute-start | bytes 1572872 | tf_op jit(solution)/shard_map/ppermute | solution.py:65
  56.0 7.5 %collective-permute-done.5 = f32[128,1024]{1,0:T(8,128)S(1)} collective-permute-done((f32[128,1024]{1,0:T(8,128)S(1)}, f32[128,1024]{1,0:T(8,128)S(1)}, u32[]{:S(2)}, u32[]{:S(2)}) %collective-permute-start.5) | collective-permute-done | bytes 524320 | tf_op jit(solution)/shard_map/ppermute | solution.py:68
  63.6 3.7 %collective-permute-start.9 = (f32[128,1024]{1,0:T(8,128)S(1)}, f32[128,1024]{1,0:T(8,128)S(1)}, u32[]{:S(2)}, u32[]{:S(2)}) collective-permute-start(f32[128,1024]{1,0:T(8,128)S(1)} %collective-permute-done.5), channel_id=1, source_target_pairs={{0,7},{1,0},{2,1},{3,2},{4,3},{5,4},{6,5},{7,6},{8,15},{9,8},{10,9... | collective-permute-start | bytes 1572872 | tf_op jit(solution)/shard_map/ppermute | solution.py:68
  67.9 6.9 %collective-permute-done.6 = f32[128,1024]{1,0:T(8,128)S(1)} collective-permute-done((f32[128,1024]{1,0:T(8,128)S(1)}, f32[128,1024]{1,0:T(8,128)S(1)}, u32[]{:S(2)}, u32[]{:S(2)}) %collective-permute-start.6) | collective-permute-done | bytes 524320 | tf_op jit(solution)/shard_map/ppermute | solution.py:65
  74.8 3.7 %collective-permute-start.10 = (f32[128,1024]{1,0:T(8,128)S(1)}, f32[128,1024]{1,0:T(8,128)S(1)}, u32[]{:S(2)}, u32[]{:S(2)}) collective-permute-start(f32[128,1024]{1,0:T(8,128)S(1)} %collective-permute-done.6), channel_id=1, source_target_pairs={{0,7},{1,0},{2,1},{3,2},{4,3},{5,4},{6,5},{7,6},{8,15},{9,8},{10,9... | collective-permute-start | bytes 1572872 | tf_op jit(solution)/shard_map/ppermute | solution.py:65
  78.5 11.2 %collective-permute-done.11 = f32[128,1024]{1,0:T(8,128)S(1)} collective-permute-done((f32[128,1024]{1,0:T(8,128)S(1)}, f32[128,1024]{1,0:T(8,128)S(1)}, u32[]{:S(2)}, u32[]{:S(2)}) %collective-permute-start.11) | collective-permute-done | bytes 524320 | tf_op jit(solution)/shard_map/ppermute | solution.py:64
  89.9 1.8 %reduce-precision_convert_fusion.2 = (bf16[512,1024]{1,0:T(8,128)(2,1)}, bf16[512,1024]{1,0:T(8,128)(2,1)}) fusion(f32[512,1024]{1,0:T(8,128)S(1)} %constant_dynamic-update-slice_fusion.6), kind=kLoop, calls=%fused_computation.25 | loop fusion | flops 2097152 | bytes 4194304 | tf_op jit(solution)/shard_map/convert_element_type | solution.py:22
  91.7 1.7 %collective-permute-done.10 = f32[128,1024]{1,0:T(8,128)S(1)} collective-permute-done((f32[128,1024]{1,0:T(8,128)S(1)}, f32[128,1024]{1,0:T(8,128)S(1)}, u32[]{:S(2)}, u32[]{:S(2)}) %collective-permute-start.10) | collective-permute-done | bytes 524320 | tf_op jit(solution)/shard_map/ppermute | solution.py:65
  93.3 3.7 %collective-permute-start.14 = (f32[128,1024]{1,0:T(8,128)S(1)}, f32[128,1024]{1,0:T(8,128)S(1)}, u32[]{:S(2)}, u32[]{:S(2)}) collective-permute-start(f32[128,1024]{1,0:T(8,128)S(1)} %collective-permute-done.10), channel_id=1, source_target_pairs={{0,7},{1,0},{2,1},{3,2},{4,3},{5,4},{6,5},{7,6},{8,15},{9,8},{10,9... | collective-permute-start | bytes 1572872 | tf_op jit(solution)/shard_map/ppermute | solution.py:65
  97.1 10.5 %collective-permute-done.13 = f32[128,1024]{1,0:T(8,128)S(1)} collective-permute-done((f32[128,1024]{1,0:T(8,128)S(1)}, f32[128,1024]{1,0:T(8,128)S(1)}, u32[]{:S(2)}, u32[]{:S(2)}) %collective-permute-start.13) | collective-permute-done | bytes 524320 | tf_op jit(solution)/shard_map/ppermute | solution.py:64
  107.8 1.8 %reduce-precision_convert_fusion.1 = (bf16[512,1024]{1,0:T(8,128)(2,1)}, bf16[512,1024]{1,0:T(8,128)(2,1)}) fusion(f32[512,1024]{1,0:T(8,128)S(1)} %constant_dynamic-update-slice_fusion.10), kind=kLoop, calls=%fused_computation.23 | loop fusion | flops 2097152 | bytes 4194304 | tf_op jit(solution)/shard_map/convert_element_type | solution.py:22
  109.8 5.2 %fusion = (bf16[1024,2048]{1,0:T(8,128)(2,1)S(1)}, bf16[1024,2048]{1,0:T(8,128)(2,1)S(1)}) fusion(f32[2,512,2048]{2,1,0:T(8,128)} %all-gather.2.cloned.1.call-done), kind=kLoop, calls=%fused_computation.2 | loop fusion | flops 8388608 | bytes 16777216 | tf_op jit(solution)/shard_map/convert_element_type | solution.py:22
  115.9 1.0 copy-done.2
  117.2 3.5 %fusion.7 = f32[1024,1024]{1,0:T(8,128)S(1)} fusion(bf16[1024,1536]{1,0:T(8,128)(2,1)S(1)} %get-tuple-element.19, bf16[512,1024]{1,0:T(8,128)(2,1)S(1)} %copy-done.3, bf16[512,1024]{1,0:T(8,128)(2,1)S(1)} %copy-done.2), kind=kOutput, calls=%fused_computation.10 | convolution fusion | flops 3230662656 | bytes 9437184 | tf_op jit(solution)/shard_map/dot_general | solution.py:85
  120.7 3.5 %fusion.1 = f32[1024,1024]{1,0:T(8,128)S(1)} fusion(bf16[1024,1536]{1,0:T(8,128)(2,1)S(1)} %get-tuple-element.17, bf16[512,1024]{1,0:T(8,128)(2,1)S(1)} %get-tuple-element.30, bf16[512,1024]{1,0:T(8,128)(2,1)S(1)} %get-tuple-element.29), kind=kOutput, calls=%fused_computation.4 | convolution fusion | flops 3230662656 | bytes 9437184 | tf_op jit(solution)/shard_map/dot_general | solution.py:85
  124.2 3.8 %fusion.13 = f32[1024,1024]{1,0:T(8,128)S(1)} fusion(bf16[1024,1536]{1,0:T(8,128)(2,1)S(1)} %get-tuple-element.18, bf16[512,1024]{1,0:T(8,128)(2,1)S(1)} %copy-done.5, bf16[512,1024]{1,0:T(8,128)(2,1)S(1)} %copy-done.4), kind=kOutput, calls=%fused_computation.16 | convolution fusion | flops 3230662656 | bytes 9437184 | tf_op jit(solution)/shard_map/dot_general | solution.py:85
  128.0 1.9 %fusion.22 = f32[1024,1024]{1,0:T(8,128)S(1)} fusion(bf16[256,1024]{1,0:T(8,128)(2,1)S(1)} %copy-done.8, bf16[256,1024]{1,0:T(8,128)(2,1)S(1)} %copy-done.7, bf16[1024,256]{1,0:T(8,128)(2,1)S(1)} %get-tuple-element.16, bf16[1024,256]{1,0:T(8,128)(2,1)S(1)} %get-tuple-element.11), kind=kOutput, calls=%fused_computation.31 | convolution fusion | flops 1620049920 | bytes 6291456 | tf_op jit(solution)/shard_map/dot_general | solution.py:85
  129.9 4.1 %add_add_fusion = f32[1024,1024]{1,0:T(8,128)} fusion(f32[1024,1024]{1,0:T(8,128)S(1)} %fusion.13, f32[1024,1024]{1,0:T(8,128)S(1)} %fusion.7, f32[1024,1024]{1,0:T(8,128)S(1)} %fusion.22, f32[1024,1024]{1,0:T(8,128)S(1)} %fusion.1, bf16[1024,256]{1,0:T(8,128)(2,1)S(1)} %get-tuple-element.12, bf16[256,1024]{1,0:T(8,128)(2,1)S(1)} %get-tuple-element.36, ...), kind=kOutput, calls=%fused_computation.3 | convolution fusion | flops 1624244224 | bytes 23068672 | tf_op jit(solution)/shard_map/dot_general | solution.py:85
  (67 shorter events, 3.9 us)
Async XLA Ops:
  6.5 0.7 copy-start
  6.5 103.3 %all-gather.2.cloned.1.call-start = ((), (), s32[]{:S(2)}) async-start(), calls=%async_computation | async-start | bytes 8912896 | tf_op jit(solution)/shard_map/all_gather | solution.py:53
  11.8 3.7 %copy-start.6 = (f32[128,1024]{1,0:T(8,128)S(1)}, f32[128,1024]{1,0:T(8,128)}, u32[]{:S(2)}) copy-start(f32[128,1024]{1,0:T(8,128)} %param.6) | copy-start | bytes 1572868
  15.5 15.3 %collective-permute-start = (f32[128,1024]{1,0:T(8,128)S(1)}, f32[128,1024]{1,0:T(8,128)S(1)}, u32[]{:S(2)}, u32[]{:S(2)}) collective-permute-start(f32[128,1024]{1,0:T(8,128)S(1)} %copy-done.6), channel_id=1, source_target_pairs={{0,8},{8,0},{1,9},{9,1},{2,10},{10,2},{3,11},{11,3},{4,12},{12,4},... | collective-permute-start | bytes 1572872 | tf_op jit(solution)/shard_map/ppermute | solution.py:56
  16.1 23.9 %collective-permute-start.1 = (f32[128,1024]{1,0:T(8,128)S(1)}, f32[128,1024]{1,0:T(8,128)S(1)}, u32[]{:S(2)}, u32[]{:S(2)}) collective-permute-start(f32[128,1024]{1,0:T(8,128)S(1)} %copy-done.6), channel_id=1, source_target_pairs={{0,7},{1,0},{2,1},{3,2},{4,3},{5,4},{6,5},{7,6},{8,15},{9,8},{10,9... | collective-permute-start | bytes 1572872 | tf_op jit(solution)/shard_map/ppermute | solution.py:68
  21.9 21.3 %collective-permute-start.3 = (f32[128,1024]{1,0:T(8,128)S(1)}, f32[128,1024]{1,0:T(8,128)S(1)}, u32[]{:S(2)}, u32[]{:S(2)}) collective-permute-start(f32[128,1024]{1,0:T(8,128)S(1)} %copy-done.6), channel_id=1, source_target_pairs={{0,1},{1,2},{2,3},{3,4},{4,5},{5,6},{6,7},{7,0},{8,9},{9,10},{10,1... | collective-permute-start | bytes 1572872 | tf_op jit(solution)/shard_map/ppermute | solution.py:64
  30.7 21.6 %collective-permute-start.2 = (f32[128,1024]{1,0:T(8,128)S(1)}, f32[128,1024]{1,0:T(8,128)S(1)}, u32[]{:S(2)}, u32[]{:S(2)}) collective-permute-start(f32[128,1024]{1,0:T(8,128)S(1)} %collective-permute-done), channel_id=1, source_target_pairs={{0,7},{1,0},{2,1},{3,2},{4,3},{5,4},{6,5},{7,6},{8,15},{9,8},{10,9... | collective-permute-start | bytes 1572872 | tf_op jit(solution)/shard_map/ppermute | solution.py:65
  40.0 16.0 %collective-permute-start.4 = (f32[128,1024]{1,0:T(8,128)S(1)}, f32[128,1024]{1,0:T(8,128)S(1)}, u32[]{:S(2)}, u32[]{:S(2)}) collective-permute-start(f32[128,1024]{1,0:T(8,128)S(1)} %collective-permute-done), channel_id=1, source_target_pairs={{0,1},{1,2},{2,3},{3,4},{4,5},{5,6},{6,7},{7,0},{8,9},{9,10},{10,1... | collective-permute-start | bytes 1572872 | tf_op jit(solution)/shard_map/ppermute | solution.py:67
  40.0 23.5 %collective-permute-start.5 = (f32[128,1024]{1,0:T(8,128)S(1)}, f32[128,1024]{1,0:T(8,128)S(1)}, u32[]{:S(2)}, u32[]{:S(2)}) collective-permute-start(f32[128,1024]{1,0:T(8,128)S(1)} %collective-permute-done.1), channel_id=1, source_target_pairs={{0,7},{1,0},{2,1},{3,2},{4,3},{5,4},{6,5},{7,6},{8,15},{9,8},{10,9... | collective-permute-start | bytes 1572872 | tf_op jit(solution)/shard_map/ppermute | solution.py:68
  43.2 24.0 %collective-permute-start.7 = (f32[128,1024]{1,0:T(8,128)S(1)}, f32[128,1024]{1,0:T(8,128)S(1)}, u32[]{:S(2)}, u32[]{:S(2)}) collective-permute-start(f32[128,1024]{1,0:T(8,128)S(1)} %collective-permute-done.3), channel_id=1, source_target_pairs={{0,1},{1,2},{2,3},{3,4},{4,5},{5,6},{6,7},{7,0},{8,9},{9,10},{10,1... | collective-permute-start | bytes 1572872 | tf_op jit(solution)/shard_map/ppermute | solution.py:64
  52.3 22.5 %collective-permute-start.6 = (f32[128,1024]{1,0:T(8,128)S(1)}, f32[128,1024]{1,0:T(8,128)S(1)}, u32[]{:S(2)}, u32[]{:S(2)}) collective-permute-start(f32[128,1024]{1,0:T(8,128)S(1)} %collective-permute-done.2), channel_id=1, source_target_pairs={{0,7},{1,0},{2,1},{3,2},{4,3},{5,4},{6,5},{7,6},{8,15},{9,8},{10,9... | collective-permute-start | bytes 1572872 | tf_op jit(solution)/shard_map/ppermute | solution.py:65
  56.0 22.5 %collective-permute-start.8 = (f32[128,1024]{1,0:T(8,128)S(1)}, f32[128,1024]{1,0:T(8,128)S(1)}, u32[]{:S(2)}, u32[]{:S(2)}) collective-permute-start(f32[128,1024]{1,0:T(8,128)S(1)} %collective-permute-done.4), channel_id=1, source_target_pairs={{0,1},{1,2},{2,3},{3,4},{4,5},{5,6},{6,7},{7,0},{8,9},{9,10},{10,1... | collective-permute-start | bytes 1572872 | tf_op jit(solution)/shard_map/ppermute | solution.py:67
  63.6 28.1 %collective-permute-start.9 = (f32[128,1024]{1,0:T(8,128)S(1)}, f32[128,1024]{1,0:T(8,128)S(1)}, u32[]{:S(2)}, u32[]{:S(2)}) collective-permute-start(f32[128,1024]{1,0:T(8,128)S(1)} %collective-permute-done.5), channel_id=1, source_target_pairs={{0,7},{1,0},{2,1},{3,2},{4,3},{5,4},{6,5},{7,6},{8,15},{9,8},{10,9... | collective-permute-start | bytes 1572872 | tf_op jit(solution)/shard_map/ppermute | solution.py:68
  67.2 22.5 %collective-permute-start.11 = (f32[128,1024]{1,0:T(8,128)S(1)}, f32[128,1024]{1,0:T(8,128)S(1)}, u32[]{:S(2)}, u32[]{:S(2)}) collective-permute-start(f32[128,1024]{1,0:T(8,128)S(1)} %collective-permute-done.7), channel_id=1, source_target_pairs={{0,1},{1,2},{2,3},{3,4},{4,5},{5,6},{6,7},{7,0},{8,9},{9,10},{10,1... | collective-permute-start | bytes 1572872 | tf_op jit(solution)/shard_map/ppermute | solution.py:64
  74.8 18.6 %collective-permute-start.10 = (f32[128,1024]{1,0:T(8,128)S(1)}, f32[128,1024]{1,0:T(8,128)S(1)}, u32[]{:S(2)}, u32[]{:S(2)}) collective-permute-start(f32[128,1024]{1,0:T(8,128)S(1)} %collective-permute-done.6), channel_id=1, source_target_pairs={{0,7},{1,0},{2,1},{3,2},{4,3},{5,4},{6,5},{7,6},{8,15},{9,8},{10,9... | collective-permute-start | bytes 1572872 | tf_op jit(solution)/shard_map/ppermute | solution.py:65
  78.5 29.2 %collective-permute-start.12 = (f32[128,1024]{1,0:T(8,128)S(1)}, f32[128,1024]{1,0:T(8,128)S(1)}, u32[]{:S(2)}, u32[]{:S(2)}) collective-permute-start(f32[128,1024]{1,0:T(8,128)S(1)} %collective-permute-done.8), channel_id=1, source_target_pairs={{0,1},{1,2},{2,3},{3,4},{4,5},{5,6},{6,7},{7,0},{8,9},{9,10},{10,1... | collective-permute-start | bytes 1572872 | tf_op jit(solution)/shard_map/ppermute | solution.py:67
  89.7 17.9 %collective-permute-start.13 = (f32[128,1024]{1,0:T(8,128)S(1)}, f32[128,1024]{1,0:T(8,128)S(1)}, u32[]{:S(2)}, u32[]{:S(2)}) collective-permute-start(f32[128,1024]{1,0:T(8,128)S(1)} %collective-permute-done.11), channel_id=1, source_target_pairs={{0,1},{1,2},{2,3},{3,4},{4,5},{5,6},{6,7},{7,0},{8,9},{9,10},{10,1... | collective-permute-start | bytes 1572872 | tf_op jit(solution)/shard_map/ppermute | solution.py:64
  93.3 16.2 %collective-permute-start.14 = (f32[128,1024]{1,0:T(8,128)S(1)}, f32[128,1024]{1,0:T(8,128)S(1)}, u32[]{:S(2)}, u32[]{:S(2)}) collective-permute-start(f32[128,1024]{1,0:T(8,128)S(1)} %collective-permute-done.10), channel_id=1, source_target_pairs={{0,7},{1,0},{2,1},{3,2},{4,3},{5,4},{6,5},{7,6},{8,15},{9,8},{10,9... | collective-permute-start | bytes 1572872 | tf_op jit(solution)/shard_map/ppermute | solution.py:65
  115.7 1.2 copy-start.2
  115.7 1.5 %copy-start.3 = (bf16[512,1024]{1,0:T(8,128)(2,1)S(1)}, bf16[512,1024]{1,0:T(8,128)(2,1)}, u32[]{:S(2)}) copy-start(bf16[512,1024]{1,0:T(8,128)(2,1)} %get-tuple-element.32) | copy-start | bytes 3145732
  120.7 3.5 %copy-start.4 = (bf16[512,1024]{1,0:T(8,128)(2,1)S(1)}, bf16[512,1024]{1,0:T(8,128)(2,1)}, u32[]{:S(2)}) copy-start(bf16[512,1024]{1,0:T(8,128)(2,1)} %get-tuple-element.33) | copy-start | bytes 3145732
  120.7 3.5 %copy-start.5 = (bf16[512,1024]{1,0:T(8,128)(2,1)S(1)}, bf16[512,1024]{1,0:T(8,128)(2,1)}, u32[]{:S(2)}) copy-start(bf16[512,1024]{1,0:T(8,128)(2,1)} %get-tuple-element.34) | copy-start | bytes 3145732
  124.2 3.8 %copy-start.7 = (bf16[256,1024]{1,0:T(8,128)(2,1)S(1)}, bf16[256,1024]{1,0:T(8,128)(2,1)}, u32[]{:S(2)}) copy-start(bf16[256,1024]{1,0:T(8,128)(2,1)} %get-tuple-element.37) | copy-start | bytes 1572868
  124.2 3.8 %copy-start.8 = (bf16[256,1024]{1,0:T(8,128)(2,1)S(1)}, bf16[256,1024]{1,0:T(8,128)(2,1)}, u32[]{:S(2)}) copy-start(bf16[256,1024]{1,0:T(8,128)(2,1)} %get-tuple-element.38) | copy-start | bytes 1572868
  129.9 4.1 %copy-start.1 = (f32[512]{0:T(512)S(1)}, f32[512]{0:T(512)}, u32[]{:S(2)}) copy-start(f32[512]{0:T(512)} %param.9) | copy-start | bytes 6148
Sparse Core Ops, SparseCore 0:
  15.6 56.9 all-gather.1

commit v3 on v2

--- a/solution.py
+++ b/solution.py
@@ -3,6 +3,7 @@
 from jax import lax
 from jax.sharding import Mesh
 from jax.sharding import PartitionSpec as P
+
 
 ROW = ("y", "xlo", "core")
 COL = ("xhi", "z")
@@ -22,7 +23,7 @@
     return hi.astype(jnp.bfloat16), (x - hi).astype(jnp.bfloat16)
 
 
-def body(w_cycle, amps, eps_occ, eps_vir, occ_map, vir_perm):
+def layer(w_cycle, amps, eps_occ, eps_vir, occ_map, vir_perm):
     nz = lax.axis_size("z")
     nxhi = lax.axis_size("xhi")
     z = lax.axis_index("z")
@@ -31,11 +32,28 @@
     row = (lax.axis_index("y") * lax.axis_size("xlo") + lax.axis_index("xlo")) * lax.axis_size(
         "core"
     ) + lax.axis_index("core")
+    j_local, b_local, ck = amps.shape
+    blk = w_cycle.shape[0]
+    half = nz // 2
+    fwd = [(k, (k + 1) % nz) for k in range(nz)]
+    bwd = [(k, (k - 1) % nz) for k in range(nz)]
 
-    j_local, b_local, ck = amps.shape
-    kw = occ_energy_count = occ_map.shape[0]
-    del occ_energy_count
-    blk = w_cycle.shape[0]
+    w_other = lax.ppermute(w_cycle, "xhi", [(0, 1), (1, 0)])
+    blocks = {0: [w_cycle, w_other]}
+    f_own, f_oth = w_cycle, w_other
+    b_own, b_oth = w_cycle, w_other
+    for s in range(1, half + 1):
+        if s < half:
+            f_own = lax.ppermute(f_own, "z", fwd)
+            b_own = lax.ppermute(b_own, "z", bwd)
+            f_oth = lax.ppermute(f_oth, "z", fwd)
+            b_oth = lax.ppermute(b_oth, "z", bwd)
+            blocks[nz - s] = [f_own, f_oth]
+            blocks[s] = [b_own, b_oth]
+        else:
+            f_own = lax.ppermute(f_own, "z", fwd)
+            b_oth = lax.ppermute(b_oth, "z", bwd)
+            blocks[s] = [f_own, b_oth]
 
     vir_energy = lookup(vir_perm, eps_vir)
     occ_energy = lookup(occ_map, eps_occ)
@@ -45,31 +63,12 @@
     b_energy = lax.dynamic_slice_in_dim(vir_energy, row * b_local, b_local)
     denominator = pair_energy[None, None, :] + b_energy[None, :, None] - j_energy[:, None, None]
     scaled = amps / denominator
-
     s5 = scaled.reshape(j_local, b_local, nxhi, nz, blk)
     s5 = jnp.where(xhi == 0, s5, s5[:, :, ::-1])
     s5 = jnp.roll(s5, -z, axis=3)
     s_perm = s5.transpose(0, 1, 3, 2, 4).reshape(j_local, b_local, ck)
     s_full = lax.all_gather(s_perm, ROW, axis=1, tiled=True)
-    del kw
 
-    w_other = lax.ppermute(w_cycle, "xhi", [(0, 1), (1, 0)])
-    fwd = [(k, (k + 1) % nz) for k in range(nz)]
-    bwd = [(k, (k - 1) % nz) for k in range(nz)]
-    blocks = {0: [w_cycle, w_other]}
-    f_own, f_oth = w_cycle, w_other
-    b_own, b_oth = w_cycle, w_other
-    half = nz // 2
-    for s in range(1, half + 1):
-        f_own = lax.ppermute(f_own, "z", fwd)
-        b_oth = lax.ppermute(b_oth, "z", bwd)
-        if s < half:
-            f_oth = lax.ppermute(f_oth, "z", fwd)
-            b_own = lax.ppermute(b_own, "z", bwd)
-            blocks[nz - s] = [f_own, f_oth]
-            blocks[s] = [b_own, b_oth]
-        else:
-            blocks[s] = [f_own, b_oth]
     s_cols = s_full.reshape(j_local * s_full.shape[1], ck)
     s_hi, s_lo = split_bf16(s_cols)
     width = nxhi * blk
@@ -99,6 +98,4 @@
     )
     fine = Mesh(devices, ("y", "xlo", "core", "xhi", "z"))
     placed = (P(COL, ROW), P(COL, ROW, None), P(), P(), P(), P())
-    return jax.shard_map(
-        body, mesh=fine, in_specs=placed, out_specs=P(ROW, COL), check_vma=False
-    )
+    return jax.shard_map(layer, mesh=fine, in_specs=placed, out_specs=P(ROW, COL), check_vma=False)

time: 141 us -> 141 us (level)
  no operation moved by 1% of the time
where the time goes in v3:
time: 141 us
  waiting for transfers between devices  54.4 us (39%)
  starting transfers between devices  33.7 us (24%)
  matrix products  19.7 us (14%)
  between operations  13.8 us (10%)
  other arithmetic  12.7 us (9%)
  local copies, waits for them, and re-layouts  6.45 us (5%)
    ppermute x4, waiting for transfers between devices, layer(): f_own = lax.ppermute(f_own, 'z', fwd)  21.8 us
    ppermute x4, starting transfers between devices, layer(): b_oth = lax.ppermute(b_oth, 'z', bwd)  20.3 us
    dot_general x5, matrix products, layer(): lax.dot_general(lhs, rhs, (((0,), (1,)), ((), ())), preferred_element_typ...  16.7 us
    ppermute x4, waiting for transfers between devices, layer(): b_oth = lax.ppermute(b_oth, 'z', bwd)  16.3 us
    ppermute x3, starting transfers between devices, layer(): b_own = lax.ppermute(b_own, 'z', bwd)  12.8 us
    convert_element_type x6, other arithmetic, split_bf16(): return (hi.astype(jnp.bfloat16), (x - hi).astype(jnp.bfloat16))  10.6 us
    ppermute x1, waiting for transfers between devices, layer(): w_other = lax.ppermute(w_cycle, 'xhi', [(0, 1), (1, 0)])  8.75 us
    ppermute x3, waiting for transfers between devices, layer(): b_own = lax.ppermute(b_own, 'z', bwd)  7.54 us
  transfers between devices with their start and end apart: 16, of which 7 were waited for; matrix products, arithmetic and copies ran while one was open for 4% of the time, Pallas kernels for 0%

profile of v3, /device:TPU:28, one launch (start us, length us, event | category | flops | bytes accessed | tf_op | source)
XLA Modules:
  0.0 140.9 jit_solution(3453443945678285630)
XLA Ops:
  6.5 0.7 copy-done
  7.2 1.3 fusion.50
  8.6 0.9 convolution_bitcast_fusion.1
  9.6 0.8 convolution_bitcast_fusion
  10.5 1.2 subtract_divide_fusion
  12.1 1.3 rev.3
  14.2 1.2 reshape.64
  15.5 0.6 collective-permute-start
  16.1 5.9 %collective-permute-start.1 = (f32[128,1024]{1,0:T(8,128)S(1)}, f32[128,1024]{1,0:T(8,128)S(1)}, u32[]{:S(2)}, u32[]{:S(2)}) collective-permute-start(f32[128,1024]{1,0:T(8,128)S(1)} %copy-done.6), channel_id=1, source_target_pairs={{0,7},{1,0},{2,1},{3,2},{4,3},{5,4},{6,5},{7,6},{8,15},{9,8},{10,9... | collective-permute-start | bytes 1572872 | tf_op jit(solution)/shard_map/ppermute | solution.py:48
  22.0 8.8 %collective-permute-done = f32[128,1024]{1,0:T(8,128)S(1)} collective-permute-done((f32[128,1024]{1,0:T(8,128)S(1)}, f32[128,1024]{1,0:T(8,128)S(1)}, u32[]{:S(2)}, u32[]{:S(2)}) %collective-permute-start) | collective-permute-done | bytes 524320 | tf_op jit(solution)/shard_map/ppermute | solution.py:41
  30.7 9.3 %collective-permute-start.2 = (f32[128,1024]{1,0:T(8,128)S(1)}, f32[128,1024]{1,0:T(8,128)S(1)}, u32[]{:S(2)}, u32[]{:S(2)}) collective-permute-start(f32[128,1024]{1,0:T(8,128)S(1)} %collective-permute-done), channel_id=1, source_target_pairs={{0,7},{1,0},{2,1},{3,2},{4,3},{5,4},{6,5},{7,6},{8,15},{9,8},{10,9... | collective-permute-start | bytes 1572872 | tf_op jit(solution)/shard_map/ppermute | solution.py:50
  40.0 3.2 %collective-permute-start.5 = (f32[128,1024]{1,0:T(8,128)S(1)}, f32[128,1024]{1,0:T(8,128)S(1)}, u32[]{:S(2)}, u32[]{:S(2)}) collective-permute-start(f32[128,1024]{1,0:T(8,128)S(1)} %collective-permute-done.1), channel_id=1, source_target_pairs={{0,7},{1,0},{2,1},{3,2},{4,3},{5,4},{6,5},{7,6},{8,15},{9,8},{10,9... | collective-permute-start | bytes 1572872 | tf_op jit(solution)/shard_map/ppermute | solution.py:48
  43.3 1.2 reduce-precision_convert_fusion.5
  44.6 7.8 %collective-permute-done.2 = f32[128,1024]{1,0:T(8,128)S(1)} collective-permute-done((f32[128,1024]{1,0:T(8,128)S(1)}, f32[128,1024]{1,0:T(8,128)S(1)}, u32[]{:S(2)}, u32[]{:S(2)}) %collective-permute-start.2) | collective-permute-done | bytes 524320 | tf_op jit(solution)/shard_map/ppermute | solution.py:50
  52.3 3.7 %collective-permute-start.6 = (f32[128,1024]{1,0:T(8,128)S(1)}, f32[128,1024]{1,0:T(8,128)S(1)}, u32[]{:S(2)}, u32[]{:S(2)}) collective-permute-start(f32[128,1024]{1,0:T(8,128)S(1)} %collective-permute-done.2), channel_id=1, source_target_pairs={{0,7},{1,0},{2,1},{3,2},{4,3},{5,4},{6,5},{7,6},{8,15},{9,8},{10,9... | collective-permute-start | bytes 1572872 | tf_op jit(solution)/shard_map/ppermute | solution.py:50
  56.0 7.5 %collective-permute-done.5 = f32[128,1024]{1,0:T(8,128)S(1)} collective-permute-done((f32[128,1024]{1,0:T(8,128)S(1)}, f32[128,1024]{1,0:T(8,128)S(1)}, u32[]{:S(2)}, u32[]{:S(2)}) %collective-permute-start.5) | collective-permute-done | bytes 524320 | tf_op jit(solution)/shard_map/ppermute | solution.py:48
  63.6 3.7 %collective-permute-start.9 = (f32[128,1024]{1,0:T(8,128)S(1)}, f32[128,1024]{1,0:T(8,128)S(1)}, u32[]{:S(2)}, u32[]{:S(2)}) collective-permute-start(f32[128,1024]{1,0:T(8,128)S(1)} %collective-permute-done.5), channel_id=1, source_target_pairs={{0,7},{1,0},{2,1},{3,2},{4,3},{5,4},{6,5},{7,6},{8,15},{9,8},{10,9... | collective-permute-start | bytes 1572872 | tf_op jit(solution)/shard_map/ppermute | solution.py:48
  67.9 6.9 %collective-permute-done.6 = f32[128,1024]{1,0:T(8,128)S(1)} collective-permute-done((f32[128,1024]{1,0:T(8,128)S(1)}, f32[128,1024]{1,0:T(8,128)S(1)}, u32[]{:S(2)}, u32[]{:S(2)}) %collective-permute-start.6) | collective-permute-done | bytes 524320 | tf_op jit(solution)/shard_map/ppermute | solution.py:50
  74.8 3.7 %collective-permute-start.10 = (f32[128,1024]{1,0:T(8,128)S(1)}, f32[128,1024]{1,0:T(8,128)S(1)}, u32[]{:S(2)}, u32[]{:S(2)}) collective-permute-start(f32[128,1024]{1,0:T(8,128)S(1)} %collective-permute-done.6), channel_id=1, source_target_pairs={{0,7},{1,0},{2,1},{3,2},{4,3},{5,4},{6,5},{7,6},{8,15},{9,8},{10,9... | collective-permute-start | bytes 1572872 | tf_op jit(solution)/shard_map/ppermute | solution.py:50
  78.5 11.2 %collective-permute-done.11 = f32[128,1024]{1,0:T(8,128)S(1)} collective-permute-done((f32[128,1024]{1,0:T(8,128)S(1)}, f32[128,1024]{1,0:T(8,128)S(1)}, u32[]{:S(2)}, u32[]{:S(2)}) %collective-permute-start.11) | collective-permute-done | bytes 524320 | tf_op jit(solution)/shard_map/ppermute | solution.py:47
  89.9 1.8 %reduce-precision_convert_fusion.2 = (bf16[512,1024]{1,0:T(8,128)(2,1)}, bf16[512,1024]{1,0:T(8,128)(2,1)}) fusion(f32[512,1024]{1,0:T(8,128)S(1)} %constant_dynamic-update-slice_fusion.6), kind=kLoop, calls=%fused_computation.25 | loop fusion | flops 2097152 | bytes 4194304 | tf_op jit(solution)/shard_map/convert_element_type | solution.py:23
  91.7 1.7 %collective-permute-done.10 = f32[128,1024]{1,0:T(8,128)S(1)} collective-permute-done((f32[128,1024]{1,0:T(8,128)S(1)}, f32[128,1024]{1,0:T(8,128)S(1)}, u32[]{:S(2)}, u32[]{:S(2)}) %collective-permute-start.10) | collective-permute-done | bytes 524320 | tf_op jit(solution)/shard_map/ppermute | solution.py:50
  93.3 3.7 %collective-permute-start.14 = (f32[128,1024]{1,0:T(8,128)S(1)}, f32[128,1024]{1,0:T(8,128)S(1)}, u32[]{:S(2)}, u32[]{:S(2)}) collective-permute-start(f32[128,1024]{1,0:T(8,128)S(1)} %collective-permute-done.10), channel_id=1, source_target_pairs={{0,7},{1,0},{2,1},{3,2},{4,3},{5,4},{6,5},{7,6},{8,15},{9,8},{10,9... | collective-permute-start | bytes 1572872 | tf_op jit(solution)/shard_map/ppermute | solution.py:55
  97.1 10.5 %collective-permute-done.13 = f32[128,1024]{1,0:T(8,128)S(1)} collective-permute-done((f32[128,1024]{1,0:T(8,128)S(1)}, f32[128,1024]{1,0:T(8,128)S(1)}, u32[]{:S(2)}, u32[]{:S(2)}) %collective-permute-start.13) | collective-permute-done | bytes 524320 | tf_op jit(solution)/shard_map/ppermute | solution.py:54
  107.8 1.8 %reduce-precision_convert_fusion.1 = (bf16[512,1024]{1,0:T(8,128)(2,1)}, bf16[512,1024]{1,0:T(8,128)(2,1)}) fusion(f32[512,1024]{1,0:T(8,128)S(1)} %constant_dynamic-update-slice_fusion.10), kind=kLoop, calls=%fused_computation.23 | loop fusion | flops 2097152 | bytes 4194304 | tf_op jit(solution)/shard_map/convert_element_type | solution.py:23
  109.8 5.2 %fusion = (bf16[1024,2048]{1,0:T(8,128)(2,1)S(1)}, bf16[1024,2048]{1,0:T(8,128)(2,1)S(1)}) fusion(f32[2,512,2048]{2,1,0:T(8,128)} %all-gather.2.cloned.1.call-done), kind=kLoop, calls=%fused_computation.2 | loop fusion | flops 8388608 | bytes 16777216 | tf_op jit(solution)/shard_map/convert_element_type | solution.py:23
  115.9 1.0 copy-done.2
  117.2 3.5 %fusion.7 = f32[1024,1024]{1,0:T(8,128)S(1)} fusion(bf16[1024,1536]{1,0:T(8,128)(2,1)S(1)} %get-tuple-element.19, bf16[512,1024]{1,0:T(8,128)(2,1)S(1)} %copy-done.3, bf16[512,1024]{1,0:T(8,128)(2,1)S(1)} %copy-done.2), kind=kOutput, calls=%fused_computation.10 | convolution fusion | flops 3230662656 | bytes 9437184 | tf_op jit(solution)/shard_map/dot_general | solution.py:84
  120.7 3.5 %fusion.1 = f32[1024,1024]{1,0:T(8,128)S(1)} fusion(bf16[1024,1536]{1,0:T(8,128)(2,1)S(1)} %get-tuple-element.17, bf16[512,1024]{1,0:T(8,128)(2,1)S(1)} %get-tuple-element.30, bf16[512,1024]{1,0:T(8,128)(2,1)S(1)} %get-tuple-element.29), kind=kOutput, calls=%fused_computation.4 | convolution fusion | flops 3230662656 | bytes 9437184 | tf_op jit(solution)/shard_map/dot_general | solution.py:84
  124.2 3.8 %fusion.13 = f32[1024,1024]{1,0:T(8,128)S(1)} fusion(bf16[1024,1536]{1,0:T(8,128)(2,1)S(1)} %get-tuple-element.18, bf16[512,1024]{1,0:T(8,128)(2,1)S(1)} %copy-done.5, bf16[512,1024]{1,0:T(8,128)(2,1)S(1)} %copy-done.4), kind=kOutput, calls=%fused_computation.16 | convolution fusion | flops 3230662656 | bytes 9437184 | tf_op jit(solution)/shard_map/dot_general | solution.py:84
  128.0 1.9 %fusion.22 = f32[1024,1024]{1,0:T(8,128)S(1)} fusion(bf16[256,1024]{1,0:T(8,128)(2,1)S(1)} %copy-done.8, bf16[256,1024]{1,0:T(8,128)(2,1)S(1)} %copy-done.7, bf16[1024,256]{1,0:T(8,128)(2,1)S(1)} %get-tuple-element.16, bf16[1024,256]{1,0:T(8,128)(2,1)S(1)} %get-tuple-element.11), kind=kOutput, calls=%fused_computation.31 | convolution fusion | flops 1620049920 | bytes 6291456 | tf_op jit(solution)/shard_map/dot_general | solution.py:84
  129.9 4.1 %add_add_fusion = f32[1024,1024]{1,0:T(8,128)} fusion(f32[1024,1024]{1,0:T(8,128)S(1)} %fusion.13, f32[1024,1024]{1,0:T(8,128)S(1)} %fusion.7, f32[1024,1024]{1,0:T(8,128)S(1)} %fusion.22, f32[1024,1024]{1,0:T(8,128)S(1)} %fusion.1, bf16[1024,256]{1,0:T(8,128)(2,1)S(1)} %get-tuple-element.12, bf16[256,1024]{1,0:T(8,128)(2,1)S(1)} %get-tuple-element.36, ...), kind=kOutput, calls=%fused_computation.3 | convolution fusion | flops 1624244224 | bytes 23068672 | tf_op jit(solution)/shard_map/dot_general | solution.py:84
  (67 shorter events, 3.9 us)
Async XLA Ops:
  6.5 0.7 copy-start
  6.5 103.3 %all-gather.2.cloned.1.call-start = ((), (), s32[]{:S(2)}) async-start(), calls=%async_computation | async-start | bytes 8912896 | tf_op jit(solution)/shard_map/all_gather | solution.py:70
  11.8 3.7 %copy-start.6 = (f32[128,1024]{1,0:T(8,128)S(1)}, f32[128,1024]{1,0:T(8,128)}, u32[]{:S(2)}) copy-start(f32[128,1024]{1,0:T(8,128)} %param.6) | copy-start | bytes 1572868
  15.5 15.3 %collective-permute-start = (f32[128,1024]{1,0:T(8,128)S(1)}, f32[128,1024]{1,0:T(8,128)S(1)}, u32[]{:S(2)}, u32[]{:S(2)}) collective-permute-start(f32[128,1024]{1,0:T(8,128)S(1)} %copy-done.6), channel_id=1, source_target_pairs={{0,8},{8,0},{1,9},{9,1},{2,10},{10,2},{3,11},{11,3},{4,12},{12,4},... | collective-permute-start | bytes 1572872 | tf_op jit(solution)/shard_map/ppermute | solution.py:41
  16.1 23.9 %collective-permute-start.1 = (f32[128,1024]{1,0:T(8,128)S(1)}, f32[128,1024]{1,0:T(8,128)S(1)}, u32[]{:S(2)}, u32[]{:S(2)}) collective-permute-start(f32[128,1024]{1,0:T(8,128)S(1)} %copy-done.6), channel_id=1, source_target_pairs={{0,7},{1,0},{2,1},{3,2},{4,3},{5,4},{6,5},{7,6},{8,15},{9,8},{10,9... | collective-permute-start | bytes 1572872 | tf_op jit(solution)/shard_map/ppermute | solution.py:48
  21.9 21.3 %collective-permute-start.3 = (f32[128,1024]{1,0:T(8,128)S(1)}, f32[128,1024]{1,0:T(8,128)S(1)}, u32[]{:S(2)}, u32[]{:S(2)}) collective-permute-start(f32[128,1024]{1,0:T(8,128)S(1)} %copy-done.6), channel_id=1, source_target_pairs={{0,1},{1,2},{2,3},{3,4},{4,5},{5,6},{6,7},{7,0},{8,9},{9,10},{10,1... | collective-permute-start | bytes 1572872 | tf_op jit(solution)/shard_map/ppermute | solution.py:47
  30.7 21.6 %collective-permute-start.2 = (f32[128,1024]{1,0:T(8,128)S(1)}, f32[128,1024]{1,0:T(8,128)S(1)}, u32[]{:S(2)}, u32[]{:S(2)}) collective-permute-start(f32[128,1024]{1,0:T(8,128)S(1)} %collective-permute-done), channel_id=1, source_target_pairs={{0,7},{1,0},{2,1},{3,2},{4,3},{5,4},{6,5},{7,6},{8,15},{9,8},{10,9... | collective-permute-start | bytes 1572872 | tf_op jit(solution)/shard_map/ppermute | solution.py:50
  40.0 16.0 %collective-permute-start.4 = (f32[128,1024]{1,0:T(8,128)S(1)}, f32[128,1024]{1,0:T(8,128)S(1)}, u32[]{:S(2)}, u32[]{:S(2)}) collective-permute-start(f32[128,1024]{1,0:T(8,128)S(1)} %collective-permute-done), channel_id=1, source_target_pairs={{0,1},{1,2},{2,3},{3,4},{4,5},{5,6},{6,7},{7,0},{8,9},{9,10},{10,1... | collective-permute-start | bytes 1572872 | tf_op jit(solution)/shard_map/ppermute | solution.py:49
  40.0 23.5 %collective-permute-start.5 = (f32[128,1024]{1,0:T(8,128)S(1)}, f32[128,1024]{1,0:T(8,128)S(1)}, u32[]{:S(2)}, u32[]{:S(2)}) collective-permute-start(f32[128,1024]{1,0:T(8,128)S(1)} %collective-permute-done.1), channel_id=1, source_target_pairs={{0,7},{1,0},{2,1},{3,2},{4,3},{5,4},{6,5},{7,6},{8,15},{9,8},{10,9... | collective-permute-start | bytes 1572872 | tf_op jit(solution)/shard_map/ppermute | solution.py:48
  43.2 24.0 %collective-permute-start.7 = (f32[128,1024]{1,0:T(8,128)S(1)}, f32[128,1024]{1,0:T(8,128)S(1)}, u32[]{:S(2)}, u32[]{:S(2)}) collective-permute-start(f32[128,1024]{1,0:T(8,128)S(1)} %collective-permute-done.3), channel_id=1, source_target_pairs={{0,1},{1,2},{2,3},{3,4},{4,5},{5,6},{6,7},{7,0},{8,9},{9,10},{10,1... | collective-permute-start | bytes 1572872 | tf_op jit(solution)/shard_map/ppermute | solution.py:47
  52.3 22.5 %collective-permute-start.6 = (f32[128,1024]{1,0:T(8,128)S(1)}, f32[128,1024]{1,0:T(8,128)S(1)}, u32[]{:S(2)}, u32[]{:S(2)}) collective-permute-start(f32[128,1024]{1,0:T(8,128)S(1)} %collective-permute-done.2), channel_id=1, source_target_pairs={{0,7},{1,0},{2,1},{3,2},{4,3},{5,4},{6,5},{7,6},{8,15},{9,8},{10,9... | collective-permute-start | bytes 1572872 | tf_op jit(solution)/shard_map/ppermute | solution.py:50
  56.0 22.5 %collective-permute-start.8 = (f32[128,1024]{1,0:T(8,128)S(1)}, f32[128,1024]{1,0:T(8,128)S(1)}, u32[]{:S(2)}, u32[]{:S(2)}) collective-permute-start(f32[128,1024]{1,0:T(8,128)S(1)} %collective-permute-done.4), channel_id=1, source_target_pairs={{0,1},{1,2},{2,3},{3,4},{4,5},{5,6},{6,7},{7,0},{8,9},{9,10},{10,1... | collective-permute-start | bytes 1572872 | tf_op jit(solution)/shard_map/ppermute | solution.py:49
  63.6 28.1 %collective-permute-start.9 = (f32[128,1024]{1,0:T(8,128)S(1)}, f32[128,1024]{1,0:T(8,128)S(1)}, u32[]{:S(2)}, u32[]{:S(2)}) collective-permute-start(f32[128,1024]{1,0:T(8,128)S(1)} %collective-permute-done.5), channel_id=1, source_target_pairs={{0,7},{1,0},{2,1},{3,2},{4,3},{5,4},{6,5},{7,6},{8,15},{9,8},{10,9... | collective-permute-start | bytes 1572872 | tf_op jit(solution)/shard_map/ppermute | solution.py:48
  67.2 22.5 %collective-permute-start.11 = (f32[128,1024]{1,0:T(8,128)S(1)}, f32[128,1024]{1,0:T(8,128)S(1)}, u32[]{:S(2)}, u32[]{:S(2)}) collective-permute-start(f32[128,1024]{1,0:T(8,128)S(1)} %collective-permute-done.7), channel_id=1, source_target_pairs={{0,1},{1,2},{2,3},{3,4},{4,5},{5,6},{6,7},{7,0},{8,9},{9,10},{10,1... | collective-permute-start | bytes 1572872 | tf_op jit(solution)/shard_map/ppermute | solution.py:47
  74.8 18.6 %collective-permute-start.10 = (f32[128,1024]{1,0:T(8,128)S(1)}, f32[128,1024]{1,0:T(8,128)S(1)}, u32[]{:S(2)}, u32[]{:S(2)}) collective-permute-start(f32[128,1024]{1,0:T(8,128)S(1)} %collective-permute-done.6), channel_id=1, source_target_pairs={{0,7},{1,0},{2,1},{3,2},{4,3},{5,4},{6,5},{7,6},{8,15},{9,8},{10,9... | collective-permute-start | bytes 1572872 | tf_op jit(solution)/shard_map/ppermute | solution.py:50
  78.5 29.2 %collective-permute-start.12 = (f32[128,1024]{1,0:T(8,128)S(1)}, f32[128,1024]{1,0:T(8,128)S(1)}, u32[]{:S(2)}, u32[]{:S(2)}) collective-permute-start(f32[128,1024]{1,0:T(8,128)S(1)} %collective-permute-done.8), channel_id=1, source_target_pairs={{0,1},{1,2},{2,3},{3,4},{4,5},{5,6},{6,7},{7,0},{8,9},{9,10},{10,1... | collective-permute-start | bytes 1572872 | tf_op jit(solution)/shard_map/ppermute | solution.py:49
  89.7 17.9 %collective-permute-start.13 = (f32[128,1024]{1,0:T(8,128)S(1)}, f32[128,1024]{1,0:T(8,128)S(1)}, u32[]{:S(2)}, u32[]{:S(2)}) collective-permute-start(f32[128,1024]{1,0:T(8,128)S(1)} %collective-permute-done.11), channel_id=1, source_target_pairs={{0,1},{1,2},{2,3},{3,4},{4,5},{5,6},{6,7},{7,0},{8,9},{9,10},{10,1... | collective-permute-start | bytes 1572872 | tf_op jit(solution)/shard_map/ppermute | solution.py:54
  93.3 16.2 %collective-permute-start.14 = (f32[128,1024]{1,0:T(8,128)S(1)}, f32[128,1024]{1,0:T(8,128)S(1)}, u32[]{:S(2)}, u32[]{:S(2)}) collective-permute-start(f32[128,1024]{1,0:T(8,128)S(1)} %collective-permute-done.10), channel_id=1, source_target_pairs={{0,7},{1,0},{2,1},{3,2},{4,3},{5,4},{6,5},{7,6},{8,15},{9,8},{10,9... | collective-permute-start | bytes 1572872 | tf_op jit(solution)/shard_map/ppermute | solution.py:55
  115.7 1.2 copy-start.2
  115.7 1.5 %copy-start.3 = (bf16[512,1024]{1,0:T(8,128)(2,1)S(1)}, bf16[512,1024]{1,0:T(8,128)(2,1)}, u32[]{:S(2)}) copy-start(bf16[512,1024]{1,0:T(8,128)(2,1)} %get-tuple-element.32) | copy-start | bytes 3145732
  120.7 3.5 %copy-start.4 = (bf16[512,1024]{1,0:T(8,128)(2,1)S(1)}, bf16[512,1024]{1,0:T(8,128)(2,1)}, u32[]{:S(2)}) copy-start(bf16[512,1024]{1,0:T(8,128)(2,1)} %get-tuple-element.33) | copy-start | bytes 3145732
  120.7 3.5 %copy-start.5 = (bf16[512,1024]{1,0:T(8,128)(2,1)S(1)}, bf16[512,1024]{1,0:T(8,128)(2,1)}, u32[]{:S(2)}) copy-start(bf16[512,1024]{1,0:T(8,128)(2,1)} %get-tuple-element.34) | copy-start | bytes 3145732
  124.2 3.8 %copy-start.7 = (bf16[256,1024]{1,0:T(8,128)(2,1)S(1)}, bf16[256,1024]{1,0:T(8,128)(2,1)}, u32[]{:S(2)}) copy-start(bf16[256,1024]{1,0:T(8,128)(2,1)} %get-tuple-element.37) | copy-start | bytes 1572868
  124.2 3.8 %copy-start.8 = (bf16[256,1024]{1,0:T(8,128)(2,1)S(1)}, bf16[256,1024]{1,0:T(8,128)(2,1)}, u32[]{:S(2)}) copy-start(bf16[256,1024]{1,0:T(8,128)(2,1)} %get-tuple-element.38) | copy-start | bytes 1572868
  129.9 4.1 %copy-start.1 = (f32[512]{0:T(512)S(1)}, f32[512]{0:T(512)}, u32[]{:S(2)}) copy-start(f32[512]{0:T(512)} %param.9) | copy-start | bytes 6148
Sparse Core Ops, SparseCore 0:
  15.6 56.9 all-gather.1

commit v4 on v3

--- a/solution.py
+++ b/solution.py
@@ -63,28 +63,26 @@
     b_energy = lax.dynamic_slice_in_dim(vir_energy, row * b_local, b_local)
     denominator = pair_energy[None, None, :] + b_energy[None, :, None] - j_energy[:, None, None]
     scaled = amps / denominator
-    s5 = scaled.reshape(j_local, b_local, nxhi, nz, blk)
-    s5 = jnp.where(xhi == 0, s5, s5[:, :, ::-1])
-    s5 = jnp.roll(s5, -z, axis=3)
-    s_perm = s5.transpose(0, 1, 3, 2, 4).reshape(j_local, b_local, ck)
-    s_full = lax.all_gather(s_perm, ROW, axis=1, tiled=True)
+    s_full = lax.all_gather(scaled, ROW, axis=1, tiled=True)
 
     s_cols = s_full.reshape(j_local * s_full.shape[1], ck)
     s_hi, s_lo = split_bf16(s_cols)
-    width = nxhi * blk
     out = None
     for group in ([0], [1, nz - 1], [2, nz - 2], [3, nz - 3], [half]):
         w_g = jnp.concatenate([blocks[d][t] for d in group for t in range(nxhi)], axis=0)
         w_hi, w_lo = split_bf16(w_g)
-        sl = [slice(d * width, (d + 1) * width) for d in group]
-        sh_g = jnp.concatenate([s_hi[:, c] for c in sl], axis=1)
-        sl_g = jnp.concatenate([s_lo[:, c] for c in sl], axis=1)
+        starts = [((xhi + t) % nxhi * nz + (z + d) % nz) * blk for d in group for t in range(nxhi)]
+        sh_g = jnp.concatenate([lax.dynamic_slice_in_dim(s_hi, c, blk, 1) for c in starts], 1)
+        sl_g = jnp.concatenate([lax.dynamic_slice_in_dim(s_lo, c, blk, 1) for c in starts], 1)
         lhs = jnp.concatenate([w_hi, w_hi, w_lo], axis=0)
         rhs = jnp.concatenate([sh_g, sl_g, sh_g], axis=1)
         part = lax.dot_general(
             lhs, rhs, (((0,), (1,)), ((), ())), preferred_element_type=jnp.float32
         )
-        out = part if out is None else out + part
+        if out is None:
+            out = part
+        else:
+            out = out + part
     return out
 
 

time: 141 us -> 143 us (1.014)
    ppermute x3, waiting for transfers between devices: 0.01 us -> 12.1 us  [layer(): f_oth = lax.ppermute(f_oth, 'z', fwd)]
    ppermute x4, waiting for transfers between devices: 21.8 us -> 10.5 us  [layer(): f_own = lax.ppermute(f_own, 'z', fwd)]
    unnamed x34 -> x67, local copies, waits for them, and re-layouts: 2.88 us -> 5.22 us
    reshape x2 -> x0, local copies, waits for them, and re-layouts: 1.51 us -> none  [the longest x1 1.24 us: layer(): s_perm = s5.transpose(0, 1, 3, 2, 4).reshape(j_local, b_local, ck)]
where the time goes in v4:
time: 143 us; the launch traced here: 142 us
  waiting for transfers between devices  54.5 us (38%)
  starting transfers between devices  34 us (24%)
  matrix products  19.8 us (14%)
  between operations  14 us (10%)
  other arithmetic  12.8 us (9%)
  local copies, waits for them, and re-layouts  7.04 us (5%)
    ppermute x4, starting transfers between devices, layer(): b_oth = lax.ppermute(b_oth, 'z', bwd)  20.6 us
    dot_general x5, matrix products, layer(): lax.dot_general(lhs, rhs, (((0,), (1,)), ((), ())), preferred_element_typ...  16.7 us
    ppermute x4, waiting for transfers between devices, layer(): b_oth = lax.ppermute(b_oth, 'z', bwd)  15.3 us
    ppermute x3, starting transfers between devices, layer(): b_own = lax.ppermute(b_own, 'z', bwd)  12.8 us
    ppermute x3, waiting for transfers between devices, layer(): f_oth = lax.ppermute(f_oth, 'z', fwd)  12.1 us
    convert_element_type x6, other arithmetic, split_bf16(): return (hi.astype(jnp.bfloat16), (x - hi).astype(jnp.bfloat16))  10.7 us
    ppermute x4, waiting for transfers between devices, layer(): f_own = lax.ppermute(f_own, 'z', fwd)  10.5 us
    ppermute x1, waiting for transfers between devices, layer(): w_other = lax.ppermute(w_cycle, 'xhi', [(0, 1), (1, 0)])  8.96 us
  transfers between devices with their start and end apart: 16, of which 7 were waited for; matrix products, arithmetic and copies ran while one was open for 4% of the time, Pallas kernels for 0%

profile of v4, /device:TPU:28, one launch (start us, length us, event | category | flops | bytes accessed | tf_op | source)
XLA Modules:
  0.0 142.1 jit_solution(1778875733473279243)
XLA Ops:
  6.5 0.7 copy-done
  7.2 1.3 fusion.38
  8.6 0.9 convolution_bitcast_fusion.1
  9.6 0.8 convolution_bitcast_fusion
  10.5 2.0 %subtract_divide_fusion = f32[2,32,2048]{2,1,0:T(8,128)} fusion(f32[2,32,2048]{2,1,0:T(8,128)} %param.7, f32[2]{0:T(128)S(1)} %convolution_bitcast_fusion, f32[32,2048]{1,0:T(8,128)S(1)} %broadcast_add_fusion), kind=kLoop, calls=%fused_computation.53 | loop fusion | flops 262144 | bytes 1310728 | tf_op jit(solution)/shard_map/div | solution.py:65
  12.5 0.6 collective-permute-start
  13.1 5.9 %collective-permute-start.1 = (f32[128,1024]{1,0:T(8,128)}, f32[128,1024]{1,0:T(8,128)S(1)}, u32[]{:S(2)}, u32[]{:S(2)}) collective-permute-start(f32[128,1024]{1,0:T(8,128)} %param.6), channel_id=1, source_target_pairs={{0,7},{1,0},{2,1},{3,2},{4,3},{5,4},{6,5},{7,6},{8,15},{9,8},{10,9... | collective-permute-start | bytes 1572872 | tf_op jit(solution)/shard_map/ppermute | solution.py:48
  19.0 9.0 %collective-permute-done = f32[128,1024]{1,0:T(8,128)S(1)} collective-permute-done((f32[128,1024]{1,0:T(8,128)}, f32[128,1024]{1,0:T(8,128)S(1)}, u32[]{:S(2)}, u32[]{:S(2)}) %collective-permute-start) | collective-permute-done | bytes 524320 | tf_op jit(solution)/shard_map/ppermute | solution.py:41
  28.0 9.5 %collective-permute-start.2 = (f32[128,1024]{1,0:T(8,128)S(1)}, f32[128,1024]{1,0:T(8,128)S(1)}, u32[]{:S(2)}, u32[]{:S(2)}) collective-permute-start(f32[128,1024]{1,0:T(8,128)S(1)} %collective-permute-done), channel_id=1, source_target_pairs={{0,7},{1,0},{2,1},{3,2},{4,3},{5,4},{6,5},{7,6},{8,15},{9,8},{10,9... | collective-permute-start | bytes 1572872 | tf_op jit(solution)/shard_map/ppermute | solution.py:50
  37.5 3.2 %collective-permute-start.5 = (f32[128,1024]{1,0:T(8,128)S(1)}, f32[128,1024]{1,0:T(8,128)S(1)}, u32[]{:S(2)}, u32[]{:S(2)}) collective-permute-start(f32[128,1024]{1,0:T(8,128)S(1)} %collective-permute-done.1), channel_id=1, source_target_pairs={{0,7},{1,0},{2,1},{3,2},{4,3},{5,4},{6,5},{7,6},{8,15},{9,8},{10,9... | collective-permute-start | bytes 1572872 | tf_op jit(solution)/shard_map/ppermute | solution.py:48
  40.8 1.2 reduce-precision_convert_fusion.5
  42.0 7.8 %collective-permute-done.2 = f32[128,1024]{1,0:T(8,128)S(1)} collective-permute-done((f32[128,1024]{1,0:T(8,128)S(1)}, f32[128,1024]{1,0:T(8,128)S(1)}, u32[]{:S(2)}, u32[]{:S(2)}) %collective-permute-start.2) | collective-permute-done | bytes 524320 | tf_op jit(solution)/shard_map/ppermute | solution.py:50
  49.8 3.7 %collective-permute-start.6 = (f32[128,1024]{1,0:T(8,128)S(1)}, f32[128,1024]{1,0:T(8,128)S(1)}, u32[]{:S(2)}, u32[]{:S(2)}) collective-permute-start(f32[128,1024]{1,0:T(8,128)S(1)} %collective-permute-done.2), channel_id=1, source_target_pairs={{0,7},{1,0},{2,1},{3,2},{4,3},{5,4},{6,5},{7,6},{8,15},{9,8},{10,9... | collective-permute-start | bytes 1572872 | tf_op jit(solution)/shard_map/ppermute | solution.py:50
  53.5 7.5 %collective-permute-done.5 = f32[128,1024]{1,0:T(8,128)S(1)} collective-permute-done((f32[128,1024]{1,0:T(8,128)S(1)}, f32[128,1024]{1,0:T(8,128)S(1)}, u32[]{:S(2)}, u32[]{:S(2)}) %collective-permute-start.5) | collective-permute-done | bytes 524320 | tf_op jit(solution)/shard_map/ppermute | solution.py:48
  61.0 3.7 %collective-permute-start.9 = (f32[128,1024]{1,0:T(8,128)S(1)}, f32[128,1024]{1,0:T(8,128)S(1)}, u32[]{:S(2)}, u32[]{:S(2)}) collective-permute-start(f32[128,1024]{1,0:T(8,128)S(1)} %collective-permute-done.5), channel_id=1, source_target_pairs={{0,7},{1,0},{2,1},{3,2},{4,3},{5,4},{6,5},{7,6},{8,15},{9,8},{10,9... | collective-permute-start | bytes 1572872 | tf_op jit(solution)/shard_map/ppermute | solution.py:48
  65.0 0.4 reduce-precision_convert_fusion.3
  65.4 6.8 %collective-permute-done.6 = f32[128,1024]{1,0:T(8,128)S(1)} collective-permute-done((f32[128,1024]{1,0:T(8,128)S(1)}, f32[128,1024]{1,0:T(8,128)S(1)}, u32[]{:S(2)}, u32[]{:S(2)}) %collective-permute-start.6) | collective-permute-done | bytes 524320 | tf_op jit(solution)/shard_map/ppermute | solution.py:50
  72.2 3.7 %collective-permute-start.10 = (f32[128,1024]{1,0:T(8,128)S(1)}, f32[128,1024]{1,0:T(8,128)S(1)}, u32[]{:S(2)}, u32[]{:S(2)}) collective-permute-start(f32[128,1024]{1,0:T(8,128)S(1)} %collective-permute-done.6), channel_id=1, source_target_pairs={{0,7},{1,0},{2,1},{3,2},{4,3},{5,4},{6,5},{7,6},{8,15},{9,8},{10,9... | collective-permute-start | bytes 1572872 | tf_op jit(solution)/shard_map/ppermute | solution.py:50
  75.9 12.1 %collective-permute-done.8 = f32[128,1024]{1,0:T(8,128)S(1)} collective-permute-done((f32[128,1024]{1,0:T(8,128)S(1)}, f32[128,1024]{1,0:T(8,128)S(1)}, u32[]{:S(2)}, u32[]{:S(2)}) %collective-permute-start.8) | collective-permute-done | bytes 524320 | tf_op jit(solution)/shard_map/ppermute | solution.py:49
  88.2 1.8 %reduce-precision_convert_fusion.2 = (bf16[512,1024]{1,0:T(8,128)(2,1)}, bf16[512,1024]{1,0:T(8,128)(2,1)}) fusion(f32[512,1024]{1,0:T(8,128)S(1)} %constant_dynamic-update-slice_fusion.6), kind=kLoop, calls=%fused_computation.25 | loop fusion | flops 2097152 | bytes 4194304 | tf_op jit(solution)/shard_map/convert_element_type | solution.py:23
  90.1 0.7 collective-permute-done.10
  90.8 3.7 %collective-permute-start.14 = (f32[128,1024]{1,0:T(8,128)S(1)}, f32[128,1024]{1,0:T(8,128)S(1)}, u32[]{:S(2)}, u32[]{:S(2)}) collective-permute-start(f32[128,1024]{1,0:T(8,128)S(1)} %collective-permute-done.10), channel_id=1, source_target_pairs={{0,7},{1,0},{2,1},{3,2},{4,3},{5,4},{6,5},{7,6},{8,15},{9,8},{10,9... | collective-permute-start | bytes 1572872 | tf_op jit(solution)/shard_map/ppermute | solution.py:55
  94.6 10.5 %collective-permute-done.13 = f32[128,1024]{1,0:T(8,128)S(1)} collective-permute-done((f32[128,1024]{1,0:T(8,128)S(1)}, f32[128,1024]{1,0:T(8,128)S(1)}, u32[]{:S(2)}, u32[]{:S(2)}) %collective-permute-start.13) | collective-permute-done | bytes 524320 | tf_op jit(solution)/shard_map/ppermute | solution.py:54
  105.2 1.8 %reduce-precision_convert_fusion.1 = (bf16[512,1024]{1,0:T(8,128)(2,1)}, bf16[512,1024]{1,0:T(8,128)(2,1)}) fusion(f32[512,1024]{1,0:T(8,128)S(1)} %constant_dynamic-update-slice_fusion.10), kind=kLoop, calls=%fused_computation.23 | loop fusion | flops 2097152 | bytes 4194304 | tf_op jit(solution)/shard_map/convert_element_type | solution.py:23
  107.3 5.2 %fusion = (bf16[1024,2048]{1,0:T(8,128)(2,1)S(1)}, bf16[1024,2048]{1,0:T(8,128)(2,1)S(1)}) fusion(f32[2,512,2048]{2,1,0:T(8,128)} %all-gather.2.cloned.1.call-done), kind=kLoop, calls=%fused_computation.2 | loop fusion | flops 8388608 | bytes 16777216 | tf_op jit(solution)/shard_map/convert_element_type | solution.py:23
  113.1 0.4 dynamic-slice_dynamic-update-slice_fusion.17
  114.7 0.5 dynamic-slice_dynamic-update-slice_fusion.37
  118.4 3.5 %fusion.13 = f32[1024,1024]{1,0:T(8,128)S(1)} fusion(bf16[1024,1536]{1,0:T(8,128)(2,1)S(1)} %dynamic-slice_dynamic-update-slice_fusion.21, bf16[512,1024]{1,0:T(8,128)(2,1)S(1)} %copy-done.5, bf16[512,1024]{1,0:T(8,128)(2,1)S(1)} %copy-done.4), kind=kOutput, calls=%fused_computation.16 | convolution fusion | flops 3230662656 | bytes 9437184 | tf_op jit(solution)/shard_map/dot_general | solution.py:79
  121.9 3.7 %fusion.7 = f32[1024,1024]{1,0:T(8,128)S(1)} fusion(bf16[1024,1536]{1,0:T(8,128)(2,1)S(1)} %get-tuple-element.19, bf16[512,1024]{1,0:T(8,128)(2,1)S(1)} %copy-done.3, bf16[512,1024]{1,0:T(8,128)(2,1)S(1)} %copy-done.2), kind=kOutput, calls=%fused_computation.10 | convolution fusion | flops 3230662656 | bytes 9437184 | tf_op jit(solution)/shard_map/dot_general | solution.py:79
  125.7 3.5 %fusion.1 = f32[1024,1024]{1,0:T(8,128)S(1)} fusion(bf16[1024,1536]{1,0:T(8,128)(2,1)S(1)} %copy-done.10, bf16[512,1024]{1,0:T(8,128)(2,1)S(1)} %get-tuple-element.22, bf16[512,1024]{1,0:T(8,128)(2,1)S(1)} %get-tuple-element.21), kind=kOutput, calls=%fused_computation.4 | convolution fusion | flops 3230662656 | bytes 9437184 | tf_op jit(solution)/shard_map/dot_general | solution.py:79
  129.2 1.9 %fusion.22 = f32[1024,1024]{1,0:T(8,128)S(1)} fusion(bf16[1024,768]{1,0:T(8,128)(2,1)S(1)} %get-tuple-element.16, bf16[256,1024]{1,0:T(8,128)(2,1)S(1)} %copy-done.8, bf16[256,1024]{1,0:T(8,128)(2,1)S(1)} %copy-done.7), kind=kOutput, calls=%fused_computation.31 | convolution fusion | flops 1615331328 | bytes 6815744 | tf_op jit(solution)/shard_map/dot_general | solution.py:79
  131.1 4.2 %add_add_fusion = f32[1024,1024]{1,0:T(8,128)} fusion(f32[1024,1024]{1,0:T(8,128)S(1)} %fusion.13, f32[1024,1024]{1,0:T(8,128)S(1)} %fusion.7, f32[1024,1024]{1,0:T(8,128)S(1)} %fusion.22, f32[1024,1024]{1,0:T(8,128)S(1)} %fusion.1, bf16[1024,768]{1,0:T(8,128)(2,1)S(1)} %get-tuple-element.7, bf16[256,1024]{1,0:T(8,128)(2,1)S(1)} %get-tuple-element.28, ...), kind=kOutput, calls=%fused_computation.3 | convolution fusion | flops 1619525632 | bytes 23592960 | tf_op jit(solution)/shard_map/dot_general | solution.py:79
  (97 shorter events, 6.0 us)
Async XLA Ops:
  6.5 0.7 copy-start
  6.5 12.4 %copy-start.6 = (f32[128,1024]{1,0:T(8,128)S(1)}, f32[128,1024]{1,0:T(8,128)}, u32[]{:S(2)}) copy-start(f32[128,1024]{1,0:T(8,128)} %param.6) | copy-start | bytes 1572868
  6.5 100.7 %all-gather.2.cloned.1.call-start = ((), (), s32[]{:S(2)}) async-start(), calls=%async_computation | async-start | bytes 8912896 | tf_op jit(solution)/shard_map/all_gather | solution.py:66
  12.5 15.5 %collective-permute-start = (f32[128,1024]{1,0:T(8,128)}, f32[128,1024]{1,0:T(8,128)S(1)}, u32[]{:S(2)}, u32[]{:S(2)}) collective-permute-start(f32[128,1024]{1,0:T(8,128)} %param.6), channel_id=1, source_target_pairs={{0,8},{8,0},{1,9},{9,1},{2,10},{10,2},{3,11},{11,3},{4,12},{12,4},... | collective-permute-start | bytes 1572872 | tf_op jit(solution)/shard_map/ppermute | solution.py:41
  13.1 24.4 %collective-permute-start.1 = (f32[128,1024]{1,0:T(8,128)}, f32[128,1024]{1,0:T(8,128)S(1)}, u32[]{:S(2)}, u32[]{:S(2)}) collective-permute-start(f32[128,1024]{1,0:T(8,128)} %param.6), channel_id=1, source_target_pairs={{0,7},{1,0},{2,1},{3,2},{4,3},{5,4},{6,5},{7,6},{8,15},{9,8},{10,9... | collective-permute-start | bytes 1572872 | tf_op jit(solution)/shard_map/ppermute | solution.py:48
  19.0 21.7 %collective-permute-start.3 = (f32[128,1024]{1,0:T(8,128)}, f32[128,1024]{1,0:T(8,128)S(1)}, u32[]{:S(2)}, u32[]{:S(2)}) collective-permute-start(f32[128,1024]{1,0:T(8,128)} %param.6), channel_id=1, source_target_pairs={{0,1},{1,2},{2,3},{3,4},{4,5},{5,6},{6,7},{7,0},{8,9},{9,10},{10,1... | collective-permute-start | bytes 1572872 | tf_op jit(solution)/shard_map/ppermute | solution.py:47
  28.0 21.8 %collective-permute-start.2 = (f32[128,1024]{1,0:T(8,128)S(1)}, f32[128,1024]{1,0:T(8,128)S(1)}, u32[]{:S(2)}, u32[]{:S(2)}) collective-permute-start(f32[128,1024]{1,0:T(8,128)S(1)} %collective-permute-done), channel_id=1, source_target_pairs={{0,7},{1,0},{2,1},{3,2},{4,3},{5,4},{6,5},{7,6},{8,15},{9,8},{10,9... | collective-permute-start | bytes 1572872 | tf_op jit(solution)/shard_map/ppermute | solution.py:50
  37.5 27.2 %collective-permute-start.4 = (f32[128,1024]{1,0:T(8,128)S(1)}, f32[128,1024]{1,0:T(8,128)S(1)}, u32[]{:S(2)}, u32[]{:S(2)}) collective-permute-start(f32[128,1024]{1,0:T(8,128)S(1)} %collective-permute-done), channel_id=1, source_target_pairs={{0,1},{1,2},{2,3},{3,4},{4,5},{5,6},{6,7},{7,0},{8,9},{9,10},{10,1... | collective-permute-start | bytes 1572872 | tf_op jit(solution)/shard_map/ppermute | solution.py:49
  37.5 23.5 %collective-permute-start.5 = (f32[128,1024]{1,0:T(8,128)S(1)}, f32[128,1024]{1,0:T(8,128)S(1)}, u32[]{:S(2)}, u32[]{:S(2)}) collective-permute-start(f32[128,1024]{1,0:T(8,128)S(1)} %collective-permute-done.1), channel_id=1, source_target_pairs={{0,7},{1,0},{2,1},{3,2},{4,3},{5,4},{6,5},{7,6},{8,15},{9,8},{10,9... | collective-permute-start | bytes 1572872 | tf_op jit(solution)/shard_map/ppermute | solution.py:48
  40.7 24.0 %collective-permute-start.7 = (f32[128,1024]{1,0:T(8,128)S(1)}, f32[128,1024]{1,0:T(8,128)S(1)}, u32[]{:S(2)}, u32[]{:S(2)}) collective-permute-start(f32[128,1024]{1,0:T(8,128)S(1)} %collective-permute-done.3), channel_id=1, source_target_pairs={{0,1},{1,2},{2,3},{3,4},{4,5},{5,6},{6,7},{7,0},{8,9},{9,10},{10,1... | collective-permute-start | bytes 1572872 | tf_op jit(solution)/shard_map/ppermute | solution.py:47
  49.8 22.5 %collective-permute-start.6 = (f32[128,1024]{1,0:T(8,128)S(1)}, f32[128,1024]{1,0:T(8,128)S(1)}, u32[]{:S(2)}, u32[]{:S(2)}) collective-permute-start(f32[128,1024]{1,0:T(8,128)S(1)} %collective-permute-done.2), channel_id=1, source_target_pairs={{0,7},{1,0},{2,1},{3,2},{4,3},{5,4},{6,5},{7,6},{8,15},{9,8},{10,9... | collective-permute-start | bytes 1572872 | tf_op jit(solution)/shard_map/ppermute | solution.py:50
  61.0 29.0 %collective-permute-start.9 = (f32[128,1024]{1,0:T(8,128)S(1)}, f32[128,1024]{1,0:T(8,128)S(1)}, u32[]{:S(2)}, u32[]{:S(2)}) collective-permute-start(f32[128,1024]{1,0:T(8,128)S(1)} %collective-permute-done.5), channel_id=1, source_target_pairs={{0,7},{1,0},{2,1},{3,2},{4,3},{5,4},{6,5},{7,6},{8,15},{9,8},{10,9... | collective-permute-start | bytes 1572872 | tf_op jit(solution)/shard_map/ppermute | solution.py:48
  64.7 23.3 %collective-permute-start.11 = (f32[128,1024]{1,0:T(8,128)S(1)}, f32[128,1024]{1,0:T(8,128)S(1)}, u32[]{:S(2)}, u32[]{:S(2)}) collective-permute-start(f32[128,1024]{1,0:T(8,128)S(1)} %collective-permute-done.7), channel_id=1, source_target_pairs={{0,1},{1,2},{2,3},{3,4},{4,5},{5,6},{6,7},{7,0},{8,9},{9,10},{10,1... | collective-permute-start | bytes 1572872 | tf_op jit(solution)/shard_map/ppermute | solution.py:47
  64.7 23.3 %collective-permute-start.8 = (f32[128,1024]{1,0:T(8,128)S(1)}, f32[128,1024]{1,0:T(8,128)S(1)}, u32[]{:S(2)}, u32[]{:S(2)}) collective-permute-start(f32[128,1024]{1,0:T(8,128)S(1)} %collective-permute-done.4), channel_id=1, source_target_pairs={{0,1},{1,2},{2,3},{3,4},{4,5},{5,6},{6,7},{7,0},{8,9},{9,10},{10,1... | collective-permute-start | bytes 1572872 | tf_op jit(solution)/shard_map/ppermute | solution.py:49
  72.2 18.6 %collective-permute-start.10 = (f32[128,1024]{1,0:T(8,128)S(1)}, f32[128,1024]{1,0:T(8,128)S(1)}, u32[]{:S(2)}, u32[]{:S(2)}) collective-permute-start(f32[128,1024]{1,0:T(8,128)S(1)} %collective-permute-done.6), channel_id=1, source_target_pairs={{0,7},{1,0},{2,1},{3,2},{4,3},{5,4},{6,5},{7,6},{8,15},{9,8},{10,9... | collective-permute-start | bytes 1572872 | tf_op jit(solution)/shard_map/ppermute | solution.py:50
  88.0 17.1 %collective-permute-start.12 = (f32[128,1024]{1,0:T(8,128)S(1)}, f32[128,1024]{1,0:T(8,128)S(1)}, u32[]{:S(2)}, u32[]{:S(2)}) collective-permute-start(f32[128,1024]{1,0:T(8,128)S(1)} %collective-permute-done.8), channel_id=1, source_target_pairs={{0,1},{1,2},{2,3},{3,4},{4,5},{5,6},{6,7},{7,0},{8,9},{9,10},{10,1... | collective-permute-start | bytes 1572872 | tf_op jit(solution)/shard_map/ppermute | solution.py:49
  88.0 17.1 %collective-permute-start.13 = (f32[128,1024]{1,0:T(8,128)S(1)}, f32[128,1024]{1,0:T(8,128)S(1)}, u32[]{:S(2)}, u32[]{:S(2)}) collective-permute-start(f32[128,1024]{1,0:T(8,128)S(1)} %collective-permute-done.11), channel_id=1, source_target_pairs={{0,1},{1,2},{2,3},{3,4},{4,5},{5,6},{6,7},{7,0},{8,9},{9,10},{10,1... | collective-permute-start | bytes 1572872 | tf_op jit(solution)/shard_map/ppermute | solution.py:54
  90.8 16.2 %collective-permute-start.14 = (f32[128,1024]{1,0:T(8,128)S(1)}, f32[128,1024]{1,0:T(8,128)S(1)}, u32[]{:S(2)}, u32[]{:S(2)}) collective-permute-start(f32[128,1024]{1,0:T(8,128)S(1)} %collective-permute-done.10), channel_id=1, source_target_pairs={{0,7},{1,0},{2,1},{3,2},{4,3},{5,4},{6,5},{7,6},{8,15},{9,8},{10,9... | collective-permute-start | bytes 1572872 | tf_op jit(solution)/shard_map/ppermute | solution.py:55
  115.2 1.7 %copy-start.9 = (bf16[1024,1536]{1,0:T(8,128)(2,1)}, bf16[1024,1536]{1,0:T(8,128)(2,1)S(1)}, u32[]{:S(2)}) copy-start(bf16[1024,1536]{1,0:T(8,128)(2,1)S(1)} %get-tuple-element.12) | copy-start | bytes 9437188
  116.9 1.4 %copy-start.4 = (bf16[512,1024]{1,0:T(8,128)(2,1)S(1)}, bf16[512,1024]{1,0:T(8,128)(2,1)}, u32[]{:S(2)}) copy-start(bf16[512,1024]{1,0:T(8,128)(2,1)} %get-tuple-element.25) | copy-start | bytes 3145732
  116.9 1.5 %copy-start.5 = (bf16[512,1024]{1,0:T(8,128)(2,1)S(1)}, bf16[512,1024]{1,0:T(8,128)(2,1)}, u32[]{:S(2)}) copy-start(bf16[512,1024]{1,0:T(8,128)(2,1)} %get-tuple-element.26) | copy-start | bytes 3145732
  118.4 3.5 %copy-start.2 = (bf16[512,1024]{1,0:T(8,128)(2,1)S(1)}, bf16[512,1024]{1,0:T(8,128)(2,1)}, u32[]{:S(2)}) copy-start(bf16[512,1024]{1,0:T(8,128)(2,1)} %get-tuple-element.23) | copy-start | bytes 3145732
  118.4 3.5 %copy-start.3 = (bf16[512,1024]{1,0:T(8,128)(2,1)S(1)}, bf16[512,1024]{1,0:T(8,128)(2,1)}, u32[]{:S(2)}) copy-start(bf16[512,1024]{1,0:T(8,128)(2,1)} %get-tuple-element.24) | copy-start | bytes 3145732
  121.9 3.8 %copy-start.10 = (bf16[1024,1536]{1,0:T(8,128)(2,1)S(1)}, bf16[1024,1536]{1,0:T(8,128)(2,1)}, u32[]{:S(2)}) copy-start(bf16[1024,1536]{1,0:T(8,128)(2,1)} %copy-done.9) | copy-start | bytes 9437188
  125.7 3.5 %copy-start.7 = (bf16[256,1024]{1,0:T(8,128)(2,1)S(1)}, bf16[256,1024]{1,0:T(8,128)(2,1)}, u32[]{:S(2)}) copy-start(bf16[256,1024]{1,0:T(8,128)(2,1)} %get-tuple-element.29) | copy-start | bytes 1572868
  125.7 3.5 %copy-start.8 = (bf16[256,1024]{1,0:T(8,128)(2,1)S(1)}, bf16[256,1024]{1,0:T(8,128)(2,1)}, u32[]{:S(2)}) copy-start(bf16[256,1024]{1,0:T(8,128)(2,1)} %get-tuple-element.30) | copy-start | bytes 1572868
  131.0 4.2 %copy-start.1 = (f32[512]{0:T(512)S(1)}, f32[512]{0:T(512)}, u32[]{:S(2)}) copy-start(f32[512]{0:T(512)} %param.9) | copy-start | bytes 6148
Sparse Core Ops, SparseCore 0:
  12.6 56.9 all-gather.1

commit v5 on v3

--- a/solution.py
+++ b/solution.py
@@ -76,15 +76,18 @@
     for group in ([0], [1, nz - 1], [2, nz - 2], [3, nz - 3], [half]):
         w_g = jnp.concatenate([blocks[d][t] for d in group for t in range(nxhi)], axis=0)
         w_hi, w_lo = split_bf16(w_g)
+        lhs = jnp.concatenate([w_hi, w_hi, w_lo], axis=0)
         sl = [slice(d * width, (d + 1) * width) for d in group]
         sh_g = jnp.concatenate([s_hi[:, c] for c in sl], axis=1)
         sl_g = jnp.concatenate([s_lo[:, c] for c in sl], axis=1)
-        lhs = jnp.concatenate([w_hi, w_hi, w_lo], axis=0)
         rhs = jnp.concatenate([sh_g, sl_g, sh_g], axis=1)
         part = lax.dot_general(
             lhs, rhs, (((0,), (1,)), ((), ())), preferred_element_type=jnp.float32
         )
-        out = part if out is None else out + part
+        if out is None:
+            out = part
+        else:
+            out = out + part
     return out
 
 

time: 141 us -> 141 us (level)
  no operation moved by 1% of the time
where the time goes in v5:
time: 141 us
  waiting for transfers between devices  54.4 us (39%)
  starting transfers between devices  33.7 us (24%)
  matrix products  19.7 us (14%)
  between operations  13.8 us (10%)
  other arithmetic  12.7 us (9%)
  local copies, waits for them, and re-layouts  6.45 us (5%)
    ppermute x4, waiting for transfers between devices, layer(): f_own = lax.ppermute(f_own, 'z', fwd)  21.8 us
    ppermute x4, starting transfers between devices, layer(): b_oth = lax.ppermute(b_oth, 'z', bwd)  20.3 us
    dot_general x5, matrix products, layer(): lax.dot_general(lhs, rhs, (((0,), (1,)), ((), ())), preferred_element_typ...  16.7 us
    ppermute x4, waiting for transfers between devices, layer(): b_oth = lax.ppermute(b_oth, 'z', bwd)  16.3 us
    ppermute x3, starting transfers between devices, layer(): b_own = lax.ppermute(b_own, 'z', bwd)  12.8 us
    convert_element_type x6, other arithmetic, split_bf16(): return (hi.astype(jnp.bfloat16), (x - hi).astype(jnp.bfloat16))  10.6 us
    ppermute x1, waiting for transfers between devices, layer(): w_other = lax.ppermute(w_cycle, 'xhi', [(0, 1), (1, 0)])  8.75 us
    ppermute x3, waiting for transfers between devices, layer(): b_own = lax.ppermute(b_own, 'z', bwd)  7.54 us
  transfers between devices with their start and end apart: 16, of which 7 were waited for; matrix products, arithmetic and copies ran while one was open for 4% of the time, Pallas kernels for 0%

profile of v5, /device:TPU:28, one launch (start us, length us, event | category | flops | bytes accessed | tf_op | source)
XLA Modules:
  0.0 140.9 jit_solution(3453443945678285630)
XLA Ops:
  6.5 0.7 copy-done
  7.2 1.3 fusion.50
  8.6 0.9 convolution_bitcast_fusion.1
  9.6 0.8 convolution_bitcast_fusion
  10.5 1.2 subtract_divide_fusion
  12.1 1.3 rev.3
  14.2 1.2 reshape.64
  15.5 0.6 collective-permute-start
  16.1 5.9 %collective-permute-start.1 = (f32[128,1024]{1,0:T(8,128)S(1)}, f32[128,1024]{1,0:T(8,128)S(1)}, u32[]{:S(2)}, u32[]{:S(2)}) collective-permute-start(f32[128,1024]{1,0:T(8,128)S(1)} %copy-done.6), channel_id=1, source_target_pairs={{0,7},{1,0},{2,1},{3,2},{4,3},{5,4},{6,5},{7,6},{8,15},{9,8},{10,9... | collective-permute-start | bytes 1572872 | tf_op jit(solution)/shard_map/ppermute | solution.py:48
  22.0 8.8 %collective-permute-done = f32[128,1024]{1,0:T(8,128)S(1)} collective-permute-done((f32[128,1024]{1,0:T(8,128)S(1)}, f32[128,1024]{1,0:T(8,128)S(1)}, u32[]{:S(2)}, u32[]{:S(2)}) %collective-permute-start) | collective-permute-done | bytes 524320 | tf_op jit(solution)/shard_map/ppermute | solution.py:41
  30.7 9.3 %collective-permute-start.2 = (f32[128,1024]{1,0:T(8,128)S(1)}, f32[128,1024]{1,0:T(8,128)S(1)}, u32[]{:S(2)}, u32[]{:S(2)}) collective-permute-start(f32[128,1024]{1,0:T(8,128)S(1)} %collective-permute-done), channel_id=1, source_target_pairs={{0,7},{1,0},{2,1},{3,2},{4,3},{5,4},{6,5},{7,6},{8,15},{9,8},{10,9... | collective-permute-start | bytes 1572872 | tf_op jit(solution)/shard_map/ppermute | solution.py:50
  40.0 3.2 %collective-permute-start.5 = (f32[128,1024]{1,0:T(8,128)S(1)}, f32[128,1024]{1,0:T(8,128)S(1)}, u32[]{:S(2)}, u32[]{:S(2)}) collective-permute-start(f32[128,1024]{1,0:T(8,128)S(1)} %collective-permute-done.1), channel_id=1, source_target_pairs={{0,7},{1,0},{2,1},{3,2},{4,3},{5,4},{6,5},{7,6},{8,15},{9,8},{10,9... | collective-permute-start | bytes 1572872 | tf_op jit(solution)/shard_map/ppermute | solution.py:48
  43.3 1.2 reduce-precision_convert_fusion.5
  44.6 7.8 %collective-permute-done.2 = f32[128,1024]{1,0:T(8,128)S(1)} collective-permute-done((f32[128,1024]{1,0:T(8,128)S(1)}, f32[128,1024]{1,0:T(8,128)S(1)}, u32[]{:S(2)}, u32[]{:S(2)}) %collective-permute-start.2) | collective-permute-done | bytes 524320 | tf_op jit(solution)/shard_map/ppermute | solution.py:50
  52.3 3.7 %collective-permute-start.6 = (f32[128,1024]{1,0:T(8,128)S(1)}, f32[128,1024]{1,0:T(8,128)S(1)}, u32[]{:S(2)}, u32[]{:S(2)}) collective-permute-start(f32[128,1024]{1,0:T(8,128)S(1)} %collective-permute-done.2), channel_id=1, source_target_pairs={{0,7},{1,0},{2,1},{3,2},{4,3},{5,4},{6,5},{7,6},{8,15},{9,8},{10,9... | collective-permute-start | bytes 1572872 | tf_op jit(solution)/shard_map/ppermute | solution.py:50
  56.0 7.5 %collective-permute-done.5 = f32[128,1024]{1,0:T(8,128)S(1)} collective-permute-done((f32[128,1024]{1,0:T(8,128)S(1)}, f32[128,1024]{1,0:T(8,128)S(1)}, u32[]{:S(2)}, u32[]{:S(2)}) %collective-permute-start.5) | collective-permute-done | bytes 524320 | tf_op jit(solution)/shard_map/ppermute | solution.py:48
  63.6 3.7 %collective-permute-start.9 = (f32[128,1024]{1,0:T(8,128)S(1)}, f32[128,1024]{1,0:T(8,128)S(1)}, u32[]{:S(2)}, u32[]{:S(2)}) collective-permute-start(f32[128,1024]{1,0:T(8,128)S(1)} %collective-permute-done.5), channel_id=1, source_target_pairs={{0,7},{1,0},{2,1},{3,2},{4,3},{5,4},{6,5},{7,6},{8,15},{9,8},{10,9... | collective-permute-start | bytes 1572872 | tf_op jit(solution)/shard_map/ppermute | solution.py:48
  67.9 6.9 %collective-permute-done.6 = f32[128,1024]{1,0:T(8,128)S(1)} collective-permute-done((f32[128,1024]{1,0:T(8,128)S(1)}, f32[128,1024]{1,0:T(8,128)S(1)}, u32[]{:S(2)}, u32[]{:S(2)}) %collective-permute-start.6) | collective-permute-done | bytes 524320 | tf_op jit(solution)/shard_map/ppermute | solution.py:50
  74.8 3.7 %collective-permute-start.10 = (f32[128,1024]{1,0:T(8,128)S(1)}, f32[128,1024]{1,0:T(8,128)S(1)}, u32[]{:S(2)}, u32[]{:S(2)}) collective-permute-start(f32[128,1024]{1,0:T(8,128)S(1)} %collective-permute-done.6), channel_id=1, source_target_pairs={{0,7},{1,0},{2,1},{3,2},{4,3},{5,4},{6,5},{7,6},{8,15},{9,8},{10,9... | collective-permute-start | bytes 1572872 | tf_op jit(solution)/shard_map/ppermute | solution.py:50
  78.5 11.2 %collective-permute-done.11 = f32[128,1024]{1,0:T(8,128)S(1)} collective-permute-done((f32[128,1024]{1,0:T(8,128)S(1)}, f32[128,1024]{1,0:T(8,128)S(1)}, u32[]{:S(2)}, u32[]{:S(2)}) %collective-permute-start.11) | collective-permute-done | bytes 524320 | tf_op jit(solution)/shard_map/ppermute | solution.py:47
  89.9 1.8 %reduce-precision_convert_fusion.2 = (bf16[512,1024]{1,0:T(8,128)(2,1)}, bf16[512,1024]{1,0:T(8,128)(2,1)}) fusion(f32[512,1024]{1,0:T(8,128)S(1)} %constant_dynamic-update-slice_fusion.6), kind=kLoop, calls=%fused_computation.25 | loop fusion | flops 2097152 | bytes 4194304 | tf_op jit(solution)/shard_map/convert_element_type | solution.py:23
  91.7 1.7 %collective-permute-done.10 = f32[128,1024]{1,0:T(8,128)S(1)} collective-permute-done((f32[128,1024]{1,0:T(8,128)S(1)}, f32[128,1024]{1,0:T(8,128)S(1)}, u32[]{:S(2)}, u32[]{:S(2)}) %collective-permute-start.10) | collective-permute-done | bytes 524320 | tf_op jit(solution)/shard_map/ppermute | solution.py:50
  93.3 3.7 %collective-permute-start.14 = (f32[128,1024]{1,0:T(8,128)S(1)}, f32[128,1024]{1,0:T(8,128)S(1)}, u32[]{:S(2)}, u32[]{:S(2)}) collective-permute-start(f32[128,1024]{1,0:T(8,128)S(1)} %collective-permute-done.10), channel_id=1, source_target_pairs={{0,7},{1,0},{2,1},{3,2},{4,3},{5,4},{6,5},{7,6},{8,15},{9,8},{10,9... | collective-permute-start | bytes 1572872 | tf_op jit(solution)/shard_map/ppermute | solution.py:55
  97.1 10.5 %collective-permute-done.13 = f32[128,1024]{1,0:T(8,128)S(1)} collective-permute-done((f32[128,1024]{1,0:T(8,128)S(1)}, f32[128,1024]{1,0:T(8,128)S(1)}, u32[]{:S(2)}, u32[]{:S(2)}) %collective-permute-start.13) | collective-permute-done | bytes 524320 | tf_op jit(solution)/shard_map/ppermute | solution.py:54
  107.8 1.8 %reduce-precision_convert_fusion.1 = (bf16[512,1024]{1,0:T(8,128)(2,1)}, bf16[512,1024]{1,0:T(8,128)(2,1)}) fusion(f32[512,1024]{1,0:T(8,128)S(1)} %constant_dynamic-update-slice_fusion.10), kind=kLoop, calls=%fused_computation.23 | loop fusion | flops 2097152 | bytes 4194304 | tf_op jit(solution)/shard_map/convert_element_type | solution.py:23
  109.8 5.2 %fusion = (bf16[1024,2048]{1,0:T(8,128)(2,1)S(1)}, bf16[1024,2048]{1,0:T(8,128)(2,1)S(1)}) fusion(f32[2,512,2048]{2,1,0:T(8,128)} %all-gather.2.cloned.1.call-done), kind=kLoop, calls=%fused_computation.2 | loop fusion | flops 8388608 | bytes 16777216 | tf_op jit(solution)/shard_map/convert_element_type | solution.py:23
  115.9 1.0 copy-done.2
  117.2 3.5 %fusion.7 = f32[1024,1024]{1,0:T(8,128)S(1)} fusion(bf16[1024,1536]{1,0:T(8,128)(2,1)S(1)} %get-tuple-element.19, bf16[512,1024]{1,0:T(8,128)(2,1)S(1)} %copy-done.3, bf16[512,1024]{1,0:T(8,128)(2,1)S(1)} %copy-done.2), kind=kOutput, calls=%fused_computation.10 | convolution fusion | flops 3230662656 | bytes 9437184 | tf_op jit(solution)/shard_map/dot_general | solution.py:84
  120.7 3.5 %fusion.1 = f32[1024,1024]{1,0:T(8,128)S(1)} fusion(bf16[1024,1536]{1,0:T(8,128)(2,1)S(1)} %get-tuple-element.17, bf16[512,1024]{1,0:T(8,128)(2,1)S(1)} %get-tuple-element.30, bf16[512,1024]{1,0:T(8,128)(2,1)S(1)} %get-tuple-element.29), kind=kOutput, calls=%fused_computation.4 | convolution fusion | flops 3230662656 | bytes 9437184 | tf_op jit(solution)/shard_map/dot_general | solution.py:84
  124.2 3.8 %fusion.13 = f32[1024,1024]{1,0:T(8,128)S(1)} fusion(bf16[1024,1536]{1,0:T(8,128)(2,1)S(1)} %get-tuple-element.18, bf16[512,1024]{1,0:T(8,128)(2,1)S(1)} %copy-done.5, bf16[512,1024]{1,0:T(8,128)(2,1)S(1)} %copy-done.4), kind=kOutput, calls=%fused_computation.16 | convolution fusion | flops 3230662656 | bytes 9437184 | tf_op jit(solution)/shard_map/dot_general | solution.py:84
  128.0 1.9 %fusion.22 = f32[1024,1024]{1,0:T(8,128)S(1)} fusion(bf16[256,1024]{1,0:T(8,128)(2,1)S(1)} %copy-done.8, bf16[256,1024]{1,0:T(8,128)(2,1)S(1)} %copy-done.7, bf16[1024,256]{1,0:T(8,128)(2,1)S(1)} %get-tuple-element.16, bf16[1024,256]{1,0:T(8,128)(2,1)S(1)} %get-tuple-element.11), kind=kOutput, calls=%fused_computation.31 | convolution fusion | flops 1620049920 | bytes 6291456 | tf_op jit(solution)/shard_map/dot_general | solution.py:84
  129.9 4.1 %add_add_fusion = f32[1024,1024]{1,0:T(8,128)} fusion(f32[1024,1024]{1,0:T(8,128)S(1)} %fusion.13, f32[1024,1024]{1,0:T(8,128)S(1)} %fusion.7, f32[1024,1024]{1,0:T(8,128)S(1)} %fusion.22, f32[1024,1024]{1,0:T(8,128)S(1)} %fusion.1, bf16[1024,256]{1,0:T(8,128)(2,1)S(1)} %get-tuple-element.12, bf16[256,1024]{1,0:T(8,128)(2,1)S(1)} %get-tuple-element.36, ...), kind=kOutput, calls=%fused_computation.3 | convolution fusion | flops 1624244224 | bytes 23068672 | tf_op jit(solution)/shard_map/dot_general | solution.py:84
  (67 shorter events, 3.9 us)
Async XLA Ops:
  6.5 0.7 copy-start
  6.5 103.3 %all-gather.2.cloned.1.call-start = ((), (), s32[]{:S(2)}) async-start(), calls=%async_computation | async-start | bytes 8912896 | tf_op jit(solution)/shard_map/all_gather | solution.py:70
  11.8 3.7 %copy-start.6 = (f32[128,1024]{1,0:T(8,128)S(1)}, f32[128,1024]{1,0:T(8,128)}, u32[]{:S(2)}) copy-start(f32[128,1024]{1,0:T(8,128)} %param.6) | copy-start | bytes 1572868
  15.5 15.3 %collective-permute-start = (f32[128,1024]{1,0:T(8,128)S(1)}, f32[128,1024]{1,0:T(8,128)S(1)}, u32[]{:S(2)}, u32[]{:S(2)}) collective-permute-start(f32[128,1024]{1,0:T(8,128)S(1)} %copy-done.6), channel_id=1, source_target_pairs={{0,8},{8,0},{1,9},{9,1},{2,10},{10,2},{3,11},{11,3},{4,12},{12,4},... | collective-permute-start | bytes 1572872 | tf_op jit(solution)/shard_map/ppermute | solution.py:41
  16.1 23.9 %collective-permute-start.1 = (f32[128,1024]{1,0:T(8,128)S(1)}, f32[128,1024]{1,0:T(8,128)S(1)}, u32[]{:S(2)}, u32[]{:S(2)}) collective-permute-start(f32[128,1024]{1,0:T(8,128)S(1)} %copy-done.6), channel_id=1, source_target_pairs={{0,7},{1,0},{2,1},{3,2},{4,3},{5,4},{6,5},{7,6},{8,15},{9,8},{10,9... | collective-permute-start | bytes 1572872 | tf_op jit(solution)/shard_map/ppermute | solution.py:48
  21.9 21.3 %collective-permute-start.3 = (f32[128,1024]{1,0:T(8,128)S(1)}, f32[128,1024]{1,0:T(8,128)S(1)}, u32[]{:S(2)}, u32[]{:S(2)}) collective-permute-start(f32[128,1024]{1,0:T(8,128)S(1)} %copy-done.6), channel_id=1, source_target_pairs={{0,1},{1,2},{2,3},{3,4},{4,5},{5,6},{6,7},{7,0},{8,9},{9,10},{10,1... | collective-permute-start | bytes 1572872 | tf_op jit(solution)/shard_map/ppermute | solution.py:47
  30.7 21.6 %collective-permute-start.2 = (f32[128,1024]{1,0:T(8,128)S(1)}, f32[128,1024]{1,0:T(8,128)S(1)}, u32[]{:S(2)}, u32[]{:S(2)}) collective-permute-start(f32[128,1024]{1,0:T(8,128)S(1)} %collective-permute-done), channel_id=1, source_target_pairs={{0,7},{1,0},{2,1},{3,2},{4,3},{5,4},{6,5},{7,6},{8,15},{9,8},{10,9... | collective-permute-start | bytes 1572872 | tf_op jit(solution)/shard_map/ppermute | solution.py:50
  40.0 16.0 %collective-permute-start.4 = (f32[128,1024]{1,0:T(8,128)S(1)}, f32[128,1024]{1,0:T(8,128)S(1)}, u32[]{:S(2)}, u32[]{:S(2)}) collective-permute-start(f32[128,1024]{1,0:T(8,128)S(1)} %collective-permute-done), channel_id=1, source_target_pairs={{0,1},{1,2},{2,3},{3,4},{4,5},{5,6},{6,7},{7,0},{8,9},{9,10},{10,1... | collective-permute-start | bytes 1572872 | tf_op jit(solution)/shard_map/ppermute | solution.py:49
  40.0 23.5 %collective-permute-start.5 = (f32[128,1024]{1,0:T(8,128)S(1)}, f32[128,1024]{1,0:T(8,128)S(1)}, u32[]{:S(2)}, u32[]{:S(2)}) collective-permute-start(f32[128,1024]{1,0:T(8,128)S(1)} %collective-permute-done.1), channel_id=1, source_target_pairs={{0,7},{1,0},{2,1},{3,2},{4,3},{5,4},{6,5},{7,6},{8,15},{9,8},{10,9... | collective-permute-start | bytes 1572872 | tf_op jit(solution)/shard_map/ppermute | solution.py:48
  43.2 24.0 %collective-permute-start.7 = (f32[128,1024]{1,0:T(8,128)S(1)}, f32[128,1024]{1,0:T(8,128)S(1)}, u32[]{:S(2)}, u32[]{:S(2)}) collective-permute-start(f32[128,1024]{1,0:T(8,128)S(1)} %collective-permute-done.3), channel_id=1, source_target_pairs={{0,1},{1,2},{2,3},{3,4},{4,5},{5,6},{6,7},{7,0},{8,9},{9,10},{10,1... | collective-permute-start | bytes 1572872 | tf_op jit(solution)/shard_map/ppermute | solution.py:47
  52.3 22.5 %collective-permute-start.6 = (f32[128,1024]{1,0:T(8,128)S(1)}, f32[128,1024]{1,0:T(8,128)S(1)}, u32[]{:S(2)}, u32[]{:S(2)}) collective-permute-start(f32[128,1024]{1,0:T(8,128)S(1)} %collective-permute-done.2), channel_id=1, source_target_pairs={{0,7},{1,0},{2,1},{3,2},{4,3},{5,4},{6,5},{7,6},{8,15},{9,8},{10,9... | collective-permute-start | bytes 1572872 | tf_op jit(solution)/shard_map/ppermute | solution.py:50
  56.0 22.5 %collective-permute-start.8 = (f32[128,1024]{1,0:T(8,128)S(1)}, f32[128,1024]{1,0:T(8,128)S(1)}, u32[]{:S(2)}, u32[]{:S(2)}) collective-permute-start(f32[128,1024]{1,0:T(8,128)S(1)} %collective-permute-done.4), channel_id=1, source_target_pairs={{0,1},{1,2},{2,3},{3,4},{4,5},{5,6},{6,7},{7,0},{8,9},{9,10},{10,1... | collective-permute-start | bytes 1572872 | tf_op jit(solution)/shard_map/ppermute | solution.py:49
  63.6 28.1 %collective-permute-start.9 = (f32[128,1024]{1,0:T(8,128)S(1)}, f32[128,1024]{1,0:T(8,128)S(1)}, u32[]{:S(2)}, u32[]{:S(2)}) collective-permute-start(f32[128,1024]{1,0:T(8,128)S(1)} %collective-permute-done.5), channel_id=1, source_target_pairs={{0,7},{1,0},{2,1},{3,2},{4,3},{5,4},{6,5},{7,6},{8,15},{9,8},{10,9... | collective-permute-start | bytes 1572872 | tf_op jit(solution)/shard_map/ppermute | solution.py:48
  67.2 22.5 %collective-permute-start.11 = (f32[128,1024]{1,0:T(8,128)S(1)}, f32[128,1024]{1,0:T(8,128)S(1)}, u32[]{:S(2)}, u32[]{:S(2)}) collective-permute-start(f32[128,1024]{1,0:T(8,128)S(1)} %collective-permute-done.7), channel_id=1, source_target_pairs={{0,1},{1,2},{2,3},{3,4},{4,5},{5,6},{6,7},{7,0},{8,9},{9,10},{10,1... | collective-permute-start | bytes 1572872 | tf_op jit(solution)/shard_map/ppermute | solution.py:47
  74.8 18.6 %collective-permute-start.10 = (f32[128,1024]{1,0:T(8,128)S(1)}, f32[128,1024]{1,0:T(8,128)S(1)}, u32[]{:S(2)}, u32[]{:S(2)}) collective-permute-start(f32[128,1024]{1,0:T(8,128)S(1)} %collective-permute-done.6), channel_id=1, source_target_pairs={{0,7},{1,0},{2,1},{3,2},{4,3},{5,4},{6,5},{7,6},{8,15},{9,8},{10,9... | collective-permute-start | bytes 1572872 | tf_op jit(solution)/shard_map/ppermute | solution.py:50
  78.5 29.2 %collective-permute-start.12 = (f32[128,1024]{1,0:T(8,128)S(1)}, f32[128,1024]{1,0:T(8,128)S(1)}, u32[]{:S(2)}, u32[]{:S(2)}) collective-permute-start(f32[128,1024]{1,0:T(8,128)S(1)} %collective-permute-done.8), channel_id=1, source_target_pairs={{0,1},{1,2},{2,3},{3,4},{4,5},{5,6},{6,7},{7,0},{8,9},{9,10},{10,1... | collective-permute-start | bytes 1572872 | tf_op jit(solution)/shard_map/ppermute | solution.py:49
  89.7 17.9 %collective-permute-start.13 = (f32[128,1024]{1,0:T(8,128)S(1)}, f32[128,1024]{1,0:T(8,128)S(1)}, u32[]{:S(2)}, u32[]{:S(2)}) collective-permute-start(f32[128,1024]{1,0:T(8,128)S(1)} %collective-permute-done.11), channel_id=1, source_target_pairs={{0,1},{1,2},{2,3},{3,4},{4,5},{5,6},{6,7},{7,0},{8,9},{9,10},{10,1... | collective-permute-start | bytes 1572872 | tf_op jit(solution)/shard_map/ppermute | solution.py:54
  93.3 16.2 %collective-permute-start.14 = (f32[128,1024]{1,0:T(8,128)S(1)}, f32[128,1024]{1,0:T(8,128)S(1)}, u32[]{:S(2)}, u32[]{:S(2)}) collective-permute-start(f32[128,1024]{1,0:T(8,128)S(1)} %collective-permute-done.10), channel_id=1, source_target_pairs={{0,7},{1,0},{2,1},{3,2},{4,3},{5,4},{6,5},{7,6},{8,15},{9,8},{10,9... | collective-permute-start | bytes 1572872 | tf_op jit(solution)/shard_map/ppermute | solution.py:55
  115.7 1.2 copy-start.2
  115.7 1.5 %copy-start.3 = (bf16[512,1024]{1,0:T(8,128)(2,1)S(1)}, bf16[512,1024]{1,0:T(8,128)(2,1)}, u32[]{:S(2)}) copy-start(bf16[512,1024]{1,0:T(8,128)(2,1)} %get-tuple-element.32) | copy-start | bytes 3145732
  120.7 3.5 %copy-start.4 = (bf16[512,1024]{1,0:T(8,128)(2,1)S(1)}, bf16[512,1024]{1,0:T(8,128)(2,1)}, u32[]{:S(2)}) copy-start(bf16[512,1024]{1,0:T(8,128)(2,1)} %get-tuple-element.33) | copy-start | bytes 3145732
  120.7 3.5 %copy-start.5 = (bf16[512,1024]{1,0:T(8,128)(2,1)S(1)}, bf16[512,1024]{1,0:T(8,128)(2,1)}, u32[]{:S(2)}) copy-start(bf16[512,1024]{1,0:T(8,128)(2,1)} %get-tuple-element.34) | copy-start | bytes 3145732
  124.2 3.8 %copy-start.7 = (bf16[256,1024]{1,0:T(8,128)(2,1)S(1)}, bf16[256,1024]{1,0:T(8,128)(2,1)}, u32[]{:S(2)}) copy-start(bf16[256,1024]{1,0:T(8,128)(2,1)} %get-tuple-element.37) | copy-start | bytes 1572868
  124.2 3.8 %copy-start.8 = (bf16[256,1024]{1,0:T(8,128)(2,1)S(1)}, bf16[256,1024]{1,0:T(8,128)(2,1)}, u32[]{:S(2)}) copy-start(bf16[256,1024]{1,0:T(8,128)(2,1)} %get-tuple-element.38) | copy-start | bytes 1572868
  129.9 4.1 %copy-start.1 = (f32[512]{0:T(512)S(1)}, f32[512]{0:T(512)}, u32[]{:S(2)}) copy-start(f32[512]{0:T(512)} %param.9) | copy-start | bytes 6148
Sparse Core Ops, SparseCore 0:
  15.6 56.9 all-gather.1

commit v6 on v5

--- a/solution.py
+++ b/solution.py
@@ -7,6 +7,7 @@
 
 ROW = ("y", "xlo", "core")
 COL = ("xhi", "z")
+ARRIVAL = (0, 1, 7, 2, 6, 3, 5, 4)
 
 
 def lookup(indices, table):
@@ -58,28 +59,37 @@
     vir_energy = lookup(vir_perm, eps_vir)
     occ_energy = lookup(occ_map, eps_occ)
     pair_energy = (vir_energy[None, :] - occ_energy[:, None]).reshape(-1)
-    j_index = jnp.arange(j_local, dtype=jnp.int32) + col * j_local
-    j_energy = lookup(j_index, eps_occ)
+    j_energy = lax.dynamic_slice_in_dim(eps_occ, col * j_local, j_local)
     b_energy = lax.dynamic_slice_in_dim(vir_energy, row * b_local, b_local)
     denominator = pair_energy[None, None, :] + b_energy[None, :, None] - j_energy[:, None, None]
     scaled = amps / denominator
     s5 = scaled.reshape(j_local, b_local, nxhi, nz, blk)
     s5 = jnp.where(xhi == 0, s5, s5[:, :, ::-1])
     s5 = jnp.roll(s5, -z, axis=3)
+    s5 = jnp.concatenate([s5[:, :, :, d : d + 1] for d in ARRIVAL], axis=3)
     s_perm = s5.transpose(0, 1, 3, 2, 4).reshape(j_local, b_local, ck)
-    s_full = lax.all_gather(s_perm, ROW, axis=1, tiled=True)
+    s_early = lax.all_gather(s_perm[:, :, : ck // 2], ROW, axis=1, tiled=True)
+    s_late = lax.all_gather(s_perm[:, :, ck // 2 :], ROW, axis=1, tiled=True)
 
-    s_cols = s_full.reshape(j_local * s_full.shape[1], ck)
-    s_hi, s_lo = split_bf16(s_cols)
+    rows = j_local * s_early.shape[1]
+    s_hi_a, s_lo_a = split_bf16(s_early.reshape(rows, ck // 2))
+    s_hi_b, s_lo_b = split_bf16(s_late.reshape(rows, ck // 2))
     width = nxhi * blk
+    per_half = nz // 2
+    where_of = {d: k for k, d in enumerate(ARRIVAL)}
+
+    def s_block(d, hi):
+        k = where_of[d]
+        src = (s_hi_a if hi else s_lo_a) if k < per_half else (s_hi_b if hi else s_lo_b)
+        k = k % per_half
+        return src[:, k * width : (k + 1) * width]
     out = None
     for group in ([0], [1, nz - 1], [2, nz - 2], [3, nz - 3], [half]):
         w_g = jnp.concatenate([blocks[d][t] for d in group for t in range(nxhi)], axis=0)
         w_hi, w_lo = split_bf16(w_g)
         lhs = jnp.concatenate([w_hi, w_hi, w_lo], axis=0)
-        sl = [slice(d * width, (d + 1) * width) for d in group]
-        sh_g = jnp.concatenate([s_hi[:, c] for c in sl], axis=1)
-        sl_g = jnp.concatenate([s_lo[:, c] for c in sl], axis=1)
+        sh_g = jnp.concatenate([s_block(d, True) for d in group], axis=1)
+        sl_g = jnp.concatenate([s_block(d, False) for d in group], axis=1)
         rhs = jnp.concatenate([sh_g, sl_g, sh_g], axis=1)
         part = lax.dot_general(
             lhs, rhs, (((0,), (1,)), ((), ())), preferred_element_type=jnp.float32

time: 141 us -> 149 us (1.057)
  local copies, waits for them, and re-layouts: 6.45 us -> 12.4 us
  other arithmetic: 12.7 us -> 15.1 us
    slice x2 -> x9, local copies, waits for them, and re-layouts: 0.34 us -> 4.56 us  [the longest x8 3.74 us: s_block(): return src[:, k * width:(k + 1) * width]]
    convert_element_type x6 -> x7, other arithmetic: 10.6 us -> 12.9 us  [split_bf16(): return (hi.astype(jnp.bfloat16), (x - hi).astype(jnp.bfloat16))]
    unnamed x34 -> x54, local copies, waits for them, and re-layouts: 2.88 us -> 4.66 us
    dot_general x3 -> x2, matrix products: 3.02 us -> 2.17 us  [lookup(): jnp.dot(onehot, table, precision=lax.Precision.HIGHEST, preferred_element...]
  transfers between devices with their start and end apart: 16 -> 17, of which waited for: 7 -> 7; matrix products, arithmetic and copies ran while one was open for 4% -> 9% of each run, Pallas kernels for 0% -> 0%
where the time goes in v6:
time: 149 us; the launch traced here: 148 us
  waiting for transfers between devices  54.7 us (37%)
  starting transfers between devices  33.6 us (23%)
  matrix products  18.8 us (13%)
  other arithmetic  15.1 us (10%)
  between operations  14 us (9%)
  local copies, waits for them, and re-layouts  12.4 us (8%)
    ppermute x4, waiting for transfers between devices, layer(): f_own = lax.ppermute(f_own, 'z', fwd)  21.7 us
    ppermute x4, starting transfers between devices, layer(): b_oth = lax.ppermute(b_oth, 'z', bwd)  20.1 us
    dot_general x5, matrix products, layer(): lax.dot_general(lhs, rhs, (((0,), (1,)), ((), ())), preferred_element_typ...  16.6 us
    ppermute x4, waiting for transfers between devices, layer(): b_oth = lax.ppermute(b_oth, 'z', bwd)  14.9 us
    convert_element_type x7, other arithmetic, split_bf16(): return (hi.astype(jnp.bfloat16), (x - hi).astype(jnp.bfloat16))  12.9 us
    ppermute x3, starting transfers between devices, layer(): b_own = lax.ppermute(b_own, 'z', bwd)  12.8 us
    ppermute x1, waiting for transfers between devices, layer(): w_other = lax.ppermute(w_cycle, 'xhi', [(0, 1), (1, 0)])  9.72 us
    ppermute x3, waiting for transfers between devices, layer(): b_own = lax.ppermute(b_own, 'z', bwd)  7.54 us
  transfers between devices with their start and end apart: 17, of which 7 were waited for; matrix products, arithmetic and copies ran while one was open for 9% of the time, Pallas kernels for 0%

profile of v6, /device:TPU:28, one launch (start us, length us, event | category | flops | bytes accessed | tf_op | source)
XLA Modules:
  0.0 148.4 jit_solution(8091751467010086460)
XLA Ops:
  7.2 1.3 fusion.61
  10.4 1.2 subtract_divide_fusion
  12.0 1.3 rev.3
  17.1 5.9 %collective-permute-start.1 = (f32[128,1024]{1,0:T(8,128)S(1)}, f32[128,1024]{1,0:T(8,128)S(1)}, u32[]{:S(2)}, u32[]{:S(2)}) collective-permute-start(f32[128,1024]{1,0:T(8,128)S(1)} %copy-done.12), channel_id=1, source_target_pairs={{0,7},{1,0},{2,1},{3,2},{4,3},{5,4},{6,5},{7,6},{8,15},{9,8},{10,9... | collective-permute-start | bytes 1572872 | tf_op jit(solution)/shard_map/ppermute | solution.py:49
  23.0 9.7 %collective-permute-done = f32[128,1024]{1,0:T(8,128)S(1)} collective-permute-done((f32[128,1024]{1,0:T(8,128)S(1)}, f32[128,1024]{1,0:T(8,128)S(1)}, u32[]{:S(2)}, u32[]{:S(2)}) %collective-permute-start) | collective-permute-done | bytes 524320 | tf_op jit(solution)/shard_map/ppermute | solution.py:42
  32.7 9.1 %collective-permute-start.2 = (f32[128,1024]{1,0:T(8,128)S(1)}, f32[128,1024]{1,0:T(8,128)S(1)}, u32[]{:S(2)}, u32[]{:S(2)}) collective-permute-start(f32[128,1024]{1,0:T(8,128)S(1)} %collective-permute-done), channel_id=1, source_target_pairs={{0,7},{1,0},{2,1},{3,2},{4,3},{5,4},{6,5},{7,6},{8,15},{9,8},{10,9... | collective-permute-start | bytes 1572872 | tf_op jit(solution)/shard_map/ppermute | solution.py:51
  41.8 3.2 %collective-permute-start.5 = (f32[128,1024]{1,0:T(8,128)S(1)}, f32[128,1024]{1,0:T(8,128)S(1)}, u32[]{:S(2)}, u32[]{:S(2)}) collective-permute-start(f32[128,1024]{1,0:T(8,128)S(1)} %collective-permute-done.1), channel_id=1, source_target_pairs={{0,7},{1,0},{2,1},{3,2},{4,3},{5,4},{6,5},{7,6},{8,15},{9,8},{10,9... | collective-permute-start | bytes 1572872 | tf_op jit(solution)/shard_map/ppermute | solution.py:49
  45.1 1.2 reduce-precision_convert_fusion.6
  46.3 7.8 %collective-permute-done.2 = f32[128,1024]{1,0:T(8,128)S(1)} collective-permute-done((f32[128,1024]{1,0:T(8,128)S(1)}, f32[128,1024]{1,0:T(8,128)S(1)}, u32[]{:S(2)}, u32[]{:S(2)}) %collective-permute-start.2) | collective-permute-done | bytes 524320 | tf_op jit(solution)/shard_map/ppermute | solution.py:51
  54.1 3.7 %collective-permute-start.6 = (f32[128,1024]{1,0:T(8,128)S(1)}, f32[128,1024]{1,0:T(8,128)S(1)}, u32[]{:S(2)}, u32[]{:S(2)}) collective-permute-start(f32[128,1024]{1,0:T(8,128)S(1)} %collective-permute-done.2), channel_id=1, source_target_pairs={{0,7},{1,0},{2,1},{3,2},{4,3},{5,4},{6,5},{7,6},{8,15},{9,8},{10,9... | collective-permute-start | bytes 1572872 | tf_op jit(solution)/shard_map/ppermute | solution.py:51
  57.8 7.5 %collective-permute-done.5 = f32[128,1024]{1,0:T(8,128)S(1)} collective-permute-done((f32[128,1024]{1,0:T(8,128)S(1)}, f32[128,1024]{1,0:T(8,128)S(1)}, u32[]{:S(2)}, u32[]{:S(2)}) %collective-permute-start.5) | collective-permute-done | bytes 524320 | tf_op jit(solution)/shard_map/ppermute | solution.py:49
  65.3 3.7 %collective-permute-start.9 = (f32[128,1024]{1,0:T(8,128)S(1)}, f32[128,1024]{1,0:T(8,128)S(1)}, u32[]{:S(2)}, u32[]{:S(2)}) collective-permute-start(f32[128,1024]{1,0:T(8,128)S(1)} %collective-permute-done.5), channel_id=1, source_target_pairs={{0,7},{1,0},{2,1},{3,2},{4,3},{5,4},{6,5},{7,6},{8,15},{9,8},{10,9... | collective-permute-start | bytes 1572872 | tf_op jit(solution)/shard_map/ppermute | solution.py:49
  69.2 1.9 %reduce-precision_convert_fusion.4 = (bf16[512,1024]{1,0:T(8,128)(2,1)}, bf16[512,1024]{1,0:T(8,128)(2,1)}) fusion(f32[512,1024]{1,0:T(8,128)S(1)} %constant_dynamic-update-slice_fusion.2), kind=kLoop, calls=%fused_computation.40 | loop fusion | flops 2097152 | bytes 4194304 | tf_op jit(solution)/shard_map/convert_element_type | solution.py:24
  71.1 5.5 %collective-permute-done.6 = f32[128,1024]{1,0:T(8,128)S(1)} collective-permute-done((f32[128,1024]{1,0:T(8,128)S(1)}, f32[128,1024]{1,0:T(8,128)S(1)}, u32[]{:S(2)}, u32[]{:S(2)}) %collective-permute-start.6) | collective-permute-done | bytes 524320 | tf_op jit(solution)/shard_map/ppermute | solution.py:51
  76.5 3.7 %collective-permute-start.10 = (f32[128,1024]{1,0:T(8,128)S(1)}, f32[128,1024]{1,0:T(8,128)S(1)}, u32[]{:S(2)}, u32[]{:S(2)}) collective-permute-start(f32[128,1024]{1,0:T(8,128)S(1)} %collective-permute-done.6), channel_id=1, source_target_pairs={{0,7},{1,0},{2,1},{3,2},{4,3},{5,4},{6,5},{7,6},{8,15},{9,8},{10,9... | collective-permute-start | bytes 1572872 | tf_op jit(solution)/shard_map/ppermute | solution.py:51
  80.2 11.2 %collective-permute-done.11 = f32[128,1024]{1,0:T(8,128)S(1)} collective-permute-done((f32[128,1024]{1,0:T(8,128)S(1)}, f32[128,1024]{1,0:T(8,128)S(1)}, u32[]{:S(2)}, u32[]{:S(2)}) %collective-permute-start.11) | collective-permute-done | bytes 524320 | tf_op jit(solution)/shard_map/ppermute | solution.py:48
  91.6 1.8 %reduce-precision_convert_fusion.3 = (bf16[512,1024]{1,0:T(8,128)(2,1)}, bf16[512,1024]{1,0:T(8,128)(2,1)}) fusion(f32[512,1024]{1,0:T(8,128)S(1)} %constant_dynamic-update-slice_fusion.6), kind=kLoop, calls=%fused_computation.38 | loop fusion | flops 2097152 | bytes 4194304 | tf_op jit(solution)/shard_map/convert_element_type | solution.py:24
  93.4 1.7 %collective-permute-done.10 = f32[128,1024]{1,0:T(8,128)S(1)} collective-permute-done((f32[128,1024]{1,0:T(8,128)S(1)}, f32[128,1024]{1,0:T(8,128)S(1)}, u32[]{:S(2)}, u32[]{:S(2)}) %collective-permute-start.10) | collective-permute-done | bytes 524320 | tf_op jit(solution)/shard_map/ppermute | solution.py:51
  95.1 3.7 %collective-permute-start.14 = (f32[128,1024]{1,0:T(8,128)S(1)}, f32[128,1024]{1,0:T(8,128)S(1)}, u32[]{:S(2)}, u32[]{:S(2)}) collective-permute-start(f32[128,1024]{1,0:T(8,128)S(1)} %collective-permute-done.10), channel_id=1, source_target_pairs={{0,7},{1,0},{2,1},{3,2},{4,3},{5,4},{6,5},{7,6},{8,15},{9,8},{10,9... | collective-permute-start | bytes 1572872 | tf_op jit(solution)/shard_map/ppermute | solution.py:56
  98.9 10.5 %collective-permute-done.13 = f32[128,1024]{1,0:T(8,128)S(1)} collective-permute-done((f32[128,1024]{1,0:T(8,128)S(1)}, f32[128,1024]{1,0:T(8,128)S(1)}, u32[]{:S(2)}, u32[]{:S(2)}) %collective-permute-start.13) | collective-permute-done | bytes 524320 | tf_op jit(solution)/shard_map/ppermute | solution.py:55
  109.5 1.8 %reduce-precision_convert_fusion.2 = (bf16[512,1024]{1,0:T(8,128)(2,1)}, bf16[512,1024]{1,0:T(8,128)(2,1)}) fusion(f32[512,1024]{1,0:T(8,128)S(1)} %constant_dynamic-update-slice_fusion.10), kind=kLoop, calls=%fused_computation.36 | loop fusion | flops 2097152 | bytes 4194304 | tf_op jit(solution)/shard_map/convert_element_type | solution.py:24
  111.6 2.9 %fusion = (bf16[1024,1024]{1,0:T(8,128)(2,1)S(1)}, bf16[1024,1024]{1,0:T(8,128)(2,1)S(1)}) fusion(f32[2,512,1024]{2,1,0:T(8,128)} %all-gather.3.cloned.1.call-done), kind=kLoop, calls=%fused_computation.4 | loop fusion | flops 4194304 | bytes 8388608 | tf_op jit(solution)/shard_map/convert_element_type | solution.py:24
  114.5 1.2 slice.106
  116.1 1.1 slice.107
  117.2 1.0 fusion.74
  118.3 3.3 %fusion.1 = (bf16[1024,1024]{1,0:T(8,128)(2,1)S(1)}, bf16[1024,1024]{1,0:T(8,128)(2,1)S(1)}) fusion(f32[2,512,1024]{2,1,0:T(8,128)} %all-gather.5.cloned.1.call-done), kind=kLoop, calls=%fused_computation.5 | loop fusion | flops 4194304 | bytes 8388608 | tf_op jit(solution)/shard_map/convert_element_type | solution.py:24
  121.8 1.4 copy-done.3
  124.8 3.5 %fusion.13 = f32[1024,1024]{1,0:T(8,128)S(1)} fusion(bf16[1024,1536]{1,0:T(8,128)(2,1)S(1)} %slice_dynamic-update-slice_fusion.3, bf16[512,1024]{1,0:T(8,128)(2,1)S(1)} %copy-done.9, bf16[512,1024]{1,0:T(8,128)(2,1)S(1)} %copy-done.8), kind=kOutput, calls=%fused_computation.18 | convolution fusion | flops 3230662656 | bytes 9437184 | tf_op jit(solution)/shard_map/dot_general | solution.py:94
  128.3 3.5 %fusion.2 = f32[1024,1024]{1,0:T(8,128)S(1)} fusion(bf16[512,1024]{1,0:T(8,128)(2,1)S(1)} %copy-done.7, bf16[512,1024]{1,0:T(8,128)(2,1)S(1)} %copy-done.6, bf16[1024,512]{1,0:T(8,128)(2,1)S(1)} %copy-done.4, bf16[1024,512]{1,0:T(8,128)(2,1)S(1)} %copy-done.5), kind=kOutput, calls=%fused_computation.7 | convolution fusion | flops 3240099840 | bytes 8388608 | tf_op jit(solution)/shard_map/dot_general | solution.py:94
  131.8 1.8 %fusion.33 = f32[1024,1024]{1,0:T(8,128)S(1)} fusion(bf16[256,1024]{1,0:T(8,128)(2,1)S(1)} %copy-done.14, bf16[256,1024]{1,0:T(8,128)(2,1)S(1)} %copy-done.13, bf16[1024,256]{1,0:T(8,128)(2,1)S(1)} %copy-done.15, bf16[1024,256]{1,0:T(8,128)(2,1)S(1)} %get-tuple-element.15), kind=kOutput, calls=%fused_computation.44 | convolution fusion | flops 1620049920 | bytes 6291456 | tf_op jit(solution)/shard_map/dot_general | solution.py:94
  133.7 3.7 %fusion.19 = f32[1024,1024]{1,0:T(8,128)S(1)} fusion(bf16[512,1024]{1,0:T(8,128)(2,1)S(1)} %copy-done.11, bf16[512,1024]{1,0:T(8,128)(2,1)S(1)} %copy-done.10, bf16[1024,512]{1,0:T(8,128)(2,1)S(1)} %slice.113, bf16[1024,512]{1,0:T(8,128)(2,1)S(1)} %slice.114), kind=kOutput, calls=%fused_computation.24 | convolution fusion | flops 3240099840 | bytes 8388608 | tf_op jit(solution)/shard_map/dot_general | solution.py:94
  137.4 4.1 %add_add_fusion = f32[1024,1024]{1,0:T(8,128)} fusion(f32[1024,1024]{1,0:T(8,128)S(1)} %fusion.19, f32[1024,1024]{1,0:T(8,128)S(1)} %fusion.13, f32[1024,1024]{1,0:T(8,128)S(1)} %fusion.33, f32[1024,1024]{1,0:T(8,128)S(1)} %fusion.2, bf16[1024,256]{1,0:T(8,128)(2,1)S(1)} %get-tuple-element.11, bf16[256,1024]{1,0:T(8,128)(2,1)S(1)} %get-tuple-element.24, ...), kind=kOutput, calls=%fused_computation.6 | convolution fusion | flops 1624244224 | bytes 23068672 | tf_op jit(solution)/shard_map/dot_general | solution.py:94
  (98 shorter events, 9.7 us)
Async XLA Ops:
  6.5 105.0 %all-gather.3.cloned.1.call-start = ((), (), s32[]{:S(2)}) async-start(), calls=%async_computation | async-start | bytes 4456448 | tf_op jit(solution)/shard_map/all_gather | solution.py:71
  13.3 3.2 %copy-start.12 = (f32[128,1024]{1,0:T(8,128)S(1)}, f32[128,1024]{1,0:T(8,128)}, u32[]{:S(2)}) copy-start(f32[128,1024]{1,0:T(8,128)} %param.6) | copy-start | bytes 1572868
  15.7 102.6 %all-gather.5.cloned.1.call-start = ((), (), s32[]{:S(2)}) async-start(), calls=%async_computation.1 | async-start | bytes 4456448 | tf_op jit(solution)/shard_map/all_gather | solution.py:72
  16.5 16.2 %collective-permute-start = (f32[128,1024]{1,0:T(8,128)S(1)}, f32[128,1024]{1,0:T(8,128)S(1)}, u32[]{:S(2)}, u32[]{:S(2)}) collective-permute-start(f32[128,1024]{1,0:T(8,128)S(1)} %copy-done.12), channel_id=1, source_target_pairs={{0,8},{8,0},{1,9},{9,1},{2,10},{10,2},{3,11},{11,3},{4,12},{12,4},... | collective-permute-start | bytes 1572872 | tf_op jit(solution)/shard_map/ppermute | solution.py:42
  17.1 24.7 %collective-permute-start.1 = (f32[128,1024]{1,0:T(8,128)S(1)}, f32[128,1024]{1,0:T(8,128)S(1)}, u32[]{:S(2)}, u32[]{:S(2)}) collective-permute-start(f32[128,1024]{1,0:T(8,128)S(1)} %copy-done.12), channel_id=1, source_target_pairs={{0,7},{1,0},{2,1},{3,2},{4,3},{5,4},{6,5},{7,6},{8,15},{9,8},{10,9... | collective-permute-start | bytes 1572872 | tf_op jit(solution)/shard_map/ppermute | solution.py:49
  22.9 22.1 %collective-permute-start.3 = (f32[128,1024]{1,0:T(8,128)S(1)}, f32[128,1024]{1,0:T(8,128)S(1)}, u32[]{:S(2)}, u32[]{:S(2)}) collective-permute-start(f32[128,1024]{1,0:T(8,128)S(1)} %copy-done.12), channel_id=1, source_target_pairs={{0,1},{1,2},{2,3},{3,4},{4,5},{5,6},{6,7},{7,0},{8,9},{9,10},{10,1... | collective-permute-start | bytes 1572872 | tf_op jit(solution)/shard_map/ppermute | solution.py:48
  32.7 21.4 %collective-permute-start.2 = (f32[128,1024]{1,0:T(8,128)S(1)}, f32[128,1024]{1,0:T(8,128)S(1)}, u32[]{:S(2)}, u32[]{:S(2)}) collective-permute-start(f32[128,1024]{1,0:T(8,128)S(1)} %collective-permute-done), channel_id=1, source_target_pairs={{0,7},{1,0},{2,1},{3,2},{4,3},{5,4},{6,5},{7,6},{8,15},{9,8},{10,9... | collective-permute-start | bytes 1572872 | tf_op jit(solution)/shard_map/ppermute | solution.py:51
  41.8 16.0 %collective-permute-start.4 = (f32[128,1024]{1,0:T(8,128)S(1)}, f32[128,1024]{1,0:T(8,128)S(1)}, u32[]{:S(2)}, u32[]{:S(2)}) collective-permute-start(f32[128,1024]{1,0:T(8,128)S(1)} %collective-permute-done), channel_id=1, source_target_pairs={{0,1},{1,2},{2,3},{3,4},{4,5},{5,6},{6,7},{7,0},{8,9},{9,10},{10,1... | collective-permute-start | bytes 1572872 | tf_op jit(solution)/shard_map/ppermute | solution.py:50
  41.8 23.5 %collective-permute-start.5 = (f32[128,1024]{1,0:T(8,128)S(1)}, f32[128,1024]{1,0:T(8,128)S(1)}, u32[]{:S(2)}, u32[]{:S(2)}) collective-permute-start(f32[128,1024]{1,0:T(8,128)S(1)} %collective-permute-done.1), channel_id=1, source_target_pairs={{0,7},{1,0},{2,1},{3,2},{4,3},{5,4},{6,5},{7,6},{8,15},{9,8},{10,9... | collective-permute-start | bytes 1572872 | tf_op jit(solution)/shard_map/ppermute | solution.py:49
  45.0 24.0 %collective-permute-start.7 = (f32[128,1024]{1,0:T(8,128)S(1)}, f32[128,1024]{1,0:T(8,128)S(1)}, u32[]{:S(2)}, u32[]{:S(2)}) collective-permute-start(f32[128,1024]{1,0:T(8,128)S(1)} %collective-permute-done.3), channel_id=1, source_target_pairs={{0,1},{1,2},{2,3},{3,4},{4,5},{5,6},{6,7},{7,0},{8,9},{9,10},{10,1... | collective-permute-start | bytes 1572872 | tf_op jit(solution)/shard_map/ppermute | solution.py:48
  54.1 22.5 %collective-permute-start.6 = (f32[128,1024]{1,0:T(8,128)S(1)}, f32[128,1024]{1,0:T(8,128)S(1)}, u32[]{:S(2)}, u32[]{:S(2)}) collective-permute-start(f32[128,1024]{1,0:T(8,128)S(1)} %collective-permute-done.2), channel_id=1, source_target_pairs={{0,7},{1,0},{2,1},{3,2},{4,3},{5,4},{6,5},{7,6},{8,15},{9,8},{10,9... | collective-permute-start | bytes 1572872 | tf_op jit(solution)/shard_map/ppermute | solution.py:51
  57.8 22.5 %collective-permute-start.8 = (f32[128,1024]{1,0:T(8,128)S(1)}, f32[128,1024]{1,0:T(8,128)S(1)}, u32[]{:S(2)}, u32[]{:S(2)}) collective-permute-start(f32[128,1024]{1,0:T(8,128)S(1)} %collective-permute-done.4), channel_id=1, source_target_pairs={{0,1},{1,2},{2,3},{3,4},{4,5},{5,6},{6,7},{7,0},{8,9},{9,10},{10,1... | collective-permute-start | bytes 1572872 | tf_op jit(solution)/shard_map/ppermute | solution.py:50
  65.3 28.1 %collective-permute-start.9 = (f32[128,1024]{1,0:T(8,128)S(1)}, f32[128,1024]{1,0:T(8,128)S(1)}, u32[]{:S(2)}, u32[]{:S(2)}) collective-permute-start(f32[128,1024]{1,0:T(8,128)S(1)} %collective-permute-done.5), channel_id=1, source_target_pairs={{0,7},{1,0},{2,1},{3,2},{4,3},{5,4},{6,5},{7,6},{8,15},{9,8},{10,9... | collective-permute-start | bytes 1572872 | tf_op jit(solution)/shard_map/ppermute | solution.py:49
  69.0 22.5 %collective-permute-start.11 = (f32[128,1024]{1,0:T(8,128)S(1)}, f32[128,1024]{1,0:T(8,128)S(1)}, u32[]{:S(2)}, u32[]{:S(2)}) collective-permute-start(f32[128,1024]{1,0:T(8,128)S(1)} %collective-permute-done.7), channel_id=1, source_target_pairs={{0,1},{1,2},{2,3},{3,4},{4,5},{5,6},{6,7},{7,0},{8,9},{9,10},{10,1... | collective-permute-start | bytes 1572872 | tf_op jit(solution)/shard_map/ppermute | solution.py:48
  76.5 18.6 %collective-permute-start.10 = (f32[128,1024]{1,0:T(8,128)S(1)}, f32[128,1024]{1,0:T(8,128)S(1)}, u32[]{:S(2)}, u32[]{:S(2)}) collective-permute-start(f32[128,1024]{1,0:T(8,128)S(1)} %collective-permute-done.6), channel_id=1, source_target_pairs={{0,7},{1,0},{2,1},{3,2},{4,3},{5,4},{6,5},{7,6},{8,15},{9,8},{10,9... | collective-permute-start | bytes 1572872 | tf_op jit(solution)/shard_map/ppermute | solution.py:51
  80.2 29.2 %collective-permute-start.12 = (f32[128,1024]{1,0:T(8,128)S(1)}, f32[128,1024]{1,0:T(8,128)S(1)}, u32[]{:S(2)}, u32[]{:S(2)}) collective-permute-start(f32[128,1024]{1,0:T(8,128)S(1)} %collective-permute-done.8), channel_id=1, source_target_pairs={{0,1},{1,2},{2,3},{3,4},{4,5},{5,6},{6,7},{7,0},{8,9},{9,10},{10,1... | collective-permute-start | bytes 1572872 | tf_op jit(solution)/shard_map/ppermute | solution.py:50
  91.5 17.9 %collective-permute-start.13 = (f32[128,1024]{1,0:T(8,128)S(1)}, f32[128,1024]{1,0:T(8,128)S(1)}, u32[]{:S(2)}, u32[]{:S(2)}) collective-permute-start(f32[128,1024]{1,0:T(8,128)S(1)} %collective-permute-done.11), channel_id=1, source_target_pairs={{0,1},{1,2},{2,3},{3,4},{4,5},{5,6},{6,7},{7,0},{8,9},{9,10},{10,1... | collective-permute-start | bytes 1572872 | tf_op jit(solution)/shard_map/ppermute | solution.py:55
  95.1 16.2 %collective-permute-start.14 = (f32[128,1024]{1,0:T(8,128)S(1)}, f32[128,1024]{1,0:T(8,128)S(1)}, u32[]{:S(2)}, u32[]{:S(2)}) collective-permute-start(f32[128,1024]{1,0:T(8,128)S(1)} %collective-permute-done.10), channel_id=1, source_target_pairs={{0,7},{1,0},{2,1},{3,2},{4,3},{5,4},{6,5},{7,6},{8,15},{9,8},{10,9... | collective-permute-start | bytes 1572872 | tf_op jit(solution)/shard_map/ppermute | solution.py:56
  114.5 1.6 %copy-start.2 = (bf16[1024,1024]{1,0:T(8,128)(2,1)}, bf16[1024,1024]{1,0:T(8,128)(2,1)S(1)}, u32[]{:S(2)}) copy-start(bf16[1024,1024]{1,0:T(8,128)(2,1)S(1)} %get-tuple-element.5) | copy-start | bytes 6291460
  118.3 3.4 %copy-start.16 = (bf16[1024,1536]{1,0:T(8,128)(2,1)S(1)}, bf16[1024,1536]{1,0:T(8,128)(2,1)}, u32[]{:S(2)}) copy-start(bf16[1024,1536]{1,0:T(8,128)(2,1)} %get-tuple-element.18) | copy-start | bytes 9437188
  121.6 1.6 %copy-start.3 = (bf16[1024,1024]{1,0:T(8,128)(2,1)S(1)}, bf16[1024,1024]{1,0:T(8,128)(2,1)}, u32[]{:S(2)}) copy-start(bf16[1024,1024]{1,0:T(8,128)(2,1)} %copy-done.2) | copy-start | bytes 6291460
  123.2 1.5 %copy-start.9 = (bf16[512,1024]{1,0:T(8,128)(2,1)S(1)}, bf16[512,1024]{1,0:T(8,128)(2,1)}, u32[]{:S(2)}) copy-start(bf16[512,1024]{1,0:T(8,128)(2,1)} %get-tuple-element.20) | copy-start | bytes 3145732
  124.8 3.5 %copy-start.4 = (bf16[1024,512]{1,0:T(8,128)(2,1)S(1)}, bf16[1024,512]{1,0:T(8,128)(2,1)}, u32[]{:S(2)}) copy-start(bf16[1024,512]{1,0:T(8,128)(2,1)} %slice.106) | copy-start | bytes 3145732
  124.8 3.5 %copy-start.5 = (bf16[1024,512]{1,0:T(8,128)(2,1)S(1)}, bf16[1024,512]{1,0:T(8,128)(2,1)}, u32[]{:S(2)}) copy-start(bf16[1024,512]{1,0:T(8,128)(2,1)} %slice.107) | copy-start | bytes 3145732
  124.8 3.5 %copy-start.6 = (bf16[512,1024]{1,0:T(8,128)(2,1)S(1)}, bf16[512,1024]{1,0:T(8,128)(2,1)}, u32[]{:S(2)}) copy-start(bf16[512,1024]{1,0:T(8,128)(2,1)} %get-tuple-element.13) | copy-start | bytes 3145732
  124.8 3.5 %copy-start.7 = (bf16[512,1024]{1,0:T(8,128)(2,1)S(1)}, bf16[512,1024]{1,0:T(8,128)(2,1)}, u32[]{:S(2)}) copy-start(bf16[512,1024]{1,0:T(8,128)(2,1)} %get-tuple-element.14) | copy-start | bytes 3145732
  128.3 3.5 %copy-start.13 = (bf16[256,1024]{1,0:T(8,128)(2,1)S(1)}, bf16[256,1024]{1,0:T(8,128)(2,1)}, u32[]{:S(2)}) copy-start(bf16[256,1024]{1,0:T(8,128)(2,1)} %get-tuple-element.25) | copy-start | bytes 1572868
  128.3 3.5 %copy-start.14 = (bf16[256,1024]{1,0:T(8,128)(2,1)S(1)}, bf16[256,1024]{1,0:T(8,128)(2,1)}, u32[]{:S(2)}) copy-start(bf16[256,1024]{1,0:T(8,128)(2,1)} %get-tuple-element.26) | copy-start | bytes 1572868
  128.3 3.5 %copy-start.15 = (bf16[1024,256]{1,0:T(8,128)(2,1)S(1)}, bf16[1024,256]{1,0:T(8,128)(2,1)}, u32[]{:S(2)}) copy-start(bf16[1024,256]{1,0:T(8,128)(2,1)} %get-tuple-element.17) | copy-start | bytes 1572868
  131.8 1.9 %copy-start.10 = (bf16[512,1024]{1,0:T(8,128)(2,1)S(1)}, bf16[512,1024]{1,0:T(8,128)(2,1)}, u32[]{:S(2)}) copy-start(bf16[512,1024]{1,0:T(8,128)(2,1)} %get-tuple-element.21) | copy-start | bytes 3145732
  131.8 1.9 %copy-start.11 = (bf16[512,1024]{1,0:T(8,128)(2,1)S(1)}, bf16[512,1024]{1,0:T(8,128)(2,1)}, u32[]{:S(2)}) copy-start(bf16[512,1024]{1,0:T(8,128)(2,1)} %get-tuple-element.22) | copy-start | bytes 3145732
  137.4 4.1 %copy-start.1 = (f32[512]{0:T(512)S(1)}, f32[512]{0:T(512)}, u32[]{:S(2)}) copy-start(f32[512]{0:T(512)} %param.9) | copy-start | bytes 6148
  (2 other events, 1.9 us)
Sparse Core Ops, SparseCore 0:
  15.8 41.1 all-gather.2
  58.8 39.9 all-gather.4

commit v7 on v5

--- a/solution.py
+++ b/solution.py
@@ -58,8 +58,7 @@
     vir_energy = lookup(vir_perm, eps_vir)
     occ_energy = lookup(occ_map, eps_occ)
     pair_energy = (vir_energy[None, :] - occ_energy[:, None]).reshape(-1)
-    j_index = jnp.arange(j_local, dtype=jnp.int32) + col * j_local
-    j_energy = lookup(j_index, eps_occ)
+    j_energy = lax.dynamic_slice_in_dim(eps_occ, col * j_local, j_local)
     b_energy = lax.dynamic_slice_in_dim(vir_energy, row * b_local, b_local)
     denominator = pair_energy[None, None, :] + b_energy[None, :, None] - j_energy[:, None, None]
     scaled = amps / denominator
@@ -67,9 +66,14 @@
     s5 = jnp.where(xhi == 0, s5, s5[:, :, ::-1])
     s5 = jnp.roll(s5, -z, axis=3)
     s_perm = s5.transpose(0, 1, 3, 2, 4).reshape(j_local, b_local, ck)
-    s_full = lax.all_gather(s_perm, ROW, axis=1, tiled=True)
+    s_rows = lax.all_gather(s_perm.reshape(j_local * b_local, ck), ROW, axis=0, tiled=True)
 
-    s_cols = s_full.reshape(j_local * s_full.shape[1], ck)
+    nrow = s_rows.shape[0] // (j_local * b_local)
+    s_cols = (
+        s_rows.reshape(nrow, j_local, b_local, ck)
+        .transpose(1, 0, 2, 3)
+        .reshape(nrow * j_local * b_local, ck)
+    )
     s_hi, s_lo = split_bf16(s_cols)
     width = nxhi * blk
     out = None

time: 141 us -> 146 us (1.035)
  local copies, waits for them, and re-layouts: 6.45 us -> 13.8 us
    reshape x1, local copies, waits for them, and re-layouts: 1.24 us -> 3.96 us  [layer(): s_rows.reshape(nrow, j_local, b_local, ck).transpose(1, 0, 2, 3)]
    unnamed x34 -> x42, local copies, waits for them, and re-layouts: 2.88 us -> 5.53 us
    dot_general x3 -> x2, matrix products: 3.02 us -> 2.17 us  [lookup(): jnp.dot(onehot, table, precision=lax.Precision.HIGHEST, preferred_element...]
  transfers between devices with their start and end apart: 16 -> 16, of which waited for: 7 -> 7; matrix products, arithmetic and copies ran while one was open for 4% -> 5% of each run, Pallas kernels for 0% -> 0%
where the time goes in v7:
time: 146 us
  waiting for transfers between devices  53.3 us (37%)
  starting transfers between devices  33.7 us (23%)
  matrix products  18.9 us (13%)
  local copies, waits for them, and re-layouts  13.8 us (9%)
  between operations  13.8 us (9%)
  other arithmetic  12.6 us (9%)
    ppermute x4, waiting for transfers between devices, layer(): f_own = lax.ppermute(f_own, 'z', fwd)  21.7 us
    ppermute x4, starting transfers between devices, layer(): b_oth = lax.ppermute(b_oth, 'z', bwd)  20.4 us
    dot_general x5, matrix products, layer(): lax.dot_general(lhs, rhs, (((0,), (1,)), ((), ())), preferred_element_typ...  16.7 us
    ppermute x4, waiting for transfers between devices, layer(): b_oth = lax.ppermute(b_oth, 'z', bwd)  15.2 us
    ppermute x3, starting transfers between devices, layer(): b_own = lax.ppermute(b_own, 'z', bwd)  12.8 us
    convert_element_type x6, other arithmetic, split_bf16(): return (hi.astype(jnp.bfloat16), (x - hi).astype(jnp.bfloat16))  10.5 us
    ppermute x1, waiting for transfers between devices, layer(): w_other = lax.ppermute(w_cycle, 'xhi', [(0, 1), (1, 0)])  8.75 us
    ppermute x3, waiting for transfers between devices, layer(): b_own = lax.ppermute(b_own, 'z', bwd)  7.54 us
  transfers between devices with their start and end apart: 16, of which 7 were waited for; matrix products, arithmetic and copies ran while one was open for 5% of the time, Pallas kernels for 0%

profile of v7, /device:TPU:28, one launch (start us, length us, event | category | flops | bytes accessed | tf_op | source)
XLA Modules:
  0.0 146.2 jit_solution(14255652976693685377)
XLA Ops:
  7.2 1.3 fusion.50
  8.6 0.9 convolution_bitcast_fusion
  10.4 1.2 subtract_divide_fusion
  12.0 1.3 rev.3
  14.1 1.2 reshape_reshape.3
  15.9 5.9 %collective-permute-start.1 = (f32[128,1024]{1,0:T(8,128)S(1)}, f32[128,1024]{1,0:T(8,128)S(1)}, u32[]{:S(2)}, u32[]{:S(2)}) collective-permute-start(f32[128,1024]{1,0:T(8,128)S(1)} %copy-done.9), channel_id=1, source_target_pairs={{0,7},{1,0},{2,1},{3,2},{4,3},{5,4},{6,5},{7,6},{8,15},{9,8},{10,9... | collective-permute-start | bytes 1572872 | tf_op jit(solution)/shard_map/ppermute | solution.py:48
  21.8 8.8 %collective-permute-done = f32[128,1024]{1,0:T(8,128)S(1)} collective-permute-done((f32[128,1024]{1,0:T(8,128)S(1)}, f32[128,1024]{1,0:T(8,128)S(1)}, u32[]{:S(2)}, u32[]{:S(2)}) %collective-permute-start) | collective-permute-done | bytes 524320 | tf_op jit(solution)/shard_map/ppermute | solution.py:41
  30.6 9.3 %collective-permute-start.2 = (f32[128,1024]{1,0:T(8,128)S(1)}, f32[128,1024]{1,0:T(8,128)S(1)}, u32[]{:S(2)}, u32[]{:S(2)}) collective-permute-start(f32[128,1024]{1,0:T(8,128)S(1)} %collective-permute-done), channel_id=1, source_target_pairs={{0,7},{1,0},{2,1},{3,2},{4,3},{5,4},{6,5},{7,6},{8,15},{9,8},{10,9... | collective-permute-start | bytes 1572872 | tf_op jit(solution)/shard_map/ppermute | solution.py:50
  39.9 3.2 %collective-permute-start.5 = (f32[128,1024]{1,0:T(8,128)S(1)}, f32[128,1024]{1,0:T(8,128)S(1)}, u32[]{:S(2)}, u32[]{:S(2)}) collective-permute-start(f32[128,1024]{1,0:T(8,128)S(1)} %collective-permute-done.1), channel_id=1, source_target_pairs={{0,7},{1,0},{2,1},{3,2},{4,3},{5,4},{6,5},{7,6},{8,15},{9,8},{10,9... | collective-permute-start | bytes 1572872 | tf_op jit(solution)/shard_map/ppermute | solution.py:48
  43.2 1.0 reduce-precision_convert_fusion.5
  44.2 8.0 %collective-permute-done.2 = f32[128,1024]{1,0:T(8,128)S(1)} collective-permute-done((f32[128,1024]{1,0:T(8,128)S(1)}, f32[128,1024]{1,0:T(8,128)S(1)}, u32[]{:S(2)}, u32[]{:S(2)}) %collective-permute-start.2) | collective-permute-done | bytes 524320 | tf_op jit(solution)/shard_map/ppermute | solution.py:50
  52.2 3.7 %collective-permute-start.6 = (f32[128,1024]{1,0:T(8,128)S(1)}, f32[128,1024]{1,0:T(8,128)S(1)}, u32[]{:S(2)}, u32[]{:S(2)}) collective-permute-start(f32[128,1024]{1,0:T(8,128)S(1)} %collective-permute-done.2), channel_id=1, source_target_pairs={{0,7},{1,0},{2,1},{3,2},{4,3},{5,4},{6,5},{7,6},{8,15},{9,8},{10,9... | collective-permute-start | bytes 1572872 | tf_op jit(solution)/shard_map/ppermute | solution.py:50
  55.9 7.5 %collective-permute-done.5 = f32[128,1024]{1,0:T(8,128)S(1)} collective-permute-done((f32[128,1024]{1,0:T(8,128)S(1)}, f32[128,1024]{1,0:T(8,128)S(1)}, u32[]{:S(2)}, u32[]{:S(2)}) %collective-permute-start.5) | collective-permute-done | bytes 524320 | tf_op jit(solution)/shard_map/ppermute | solution.py:48
  63.4 3.7 %collective-permute-start.9 = (f32[128,1024]{1,0:T(8,128)S(1)}, f32[128,1024]{1,0:T(8,128)S(1)}, u32[]{:S(2)}, u32[]{:S(2)}) collective-permute-start(f32[128,1024]{1,0:T(8,128)S(1)} %collective-permute-done.5), channel_id=1, source_target_pairs={{0,7},{1,0},{2,1},{3,2},{4,3},{5,4},{6,5},{7,6},{8,15},{9,8},{10,9... | collective-permute-start | bytes 1572872 | tf_op jit(solution)/shard_map/ppermute | solution.py:48
  67.3 1.8 %reduce-precision_convert_fusion.3 = (bf16[512,1024]{1,0:T(8,128)(2,1)}, bf16[512,1024]{1,0:T(8,128)(2,1)}) fusion(f32[512,1024]{1,0:T(8,128)S(1)} %constant_dynamic-update-slice_fusion.2), kind=kLoop, calls=%fused_computation.27 | loop fusion | flops 2097152 | bytes 4194304 | tf_op jit(solution)/shard_map/convert_element_type | solution.py:23
  69.1 5.5 %collective-permute-done.6 = f32[128,1024]{1,0:T(8,128)S(1)} collective-permute-done((f32[128,1024]{1,0:T(8,128)S(1)}, f32[128,1024]{1,0:T(8,128)S(1)}, u32[]{:S(2)}, u32[]{:S(2)}) %collective-permute-start.6) | collective-permute-done | bytes 524320 | tf_op jit(solution)/shard_map/ppermute | solution.py:50
  74.6 3.7 %collective-permute-start.10 = (f32[128,1024]{1,0:T(8,128)S(1)}, f32[128,1024]{1,0:T(8,128)S(1)}, u32[]{:S(2)}, u32[]{:S(2)}) collective-permute-start(f32[128,1024]{1,0:T(8,128)S(1)} %collective-permute-done.6), channel_id=1, source_target_pairs={{0,7},{1,0},{2,1},{3,2},{4,3},{5,4},{6,5},{7,6},{8,15},{9,8},{10,9... | collective-permute-start | bytes 1572872 | tf_op jit(solution)/shard_map/ppermute | solution.py:50
  78.3 11.2 %collective-permute-done.11 = f32[128,1024]{1,0:T(8,128)S(1)} collective-permute-done((f32[128,1024]{1,0:T(8,128)S(1)}, f32[128,1024]{1,0:T(8,128)S(1)}, u32[]{:S(2)}, u32[]{:S(2)}) %collective-permute-start.11) | collective-permute-done | bytes 524320 | tf_op jit(solution)/shard_map/ppermute | solution.py:47
  89.7 1.7 %reduce-precision_convert_fusion.2 = (bf16[512,1024]{1,0:T(8,128)(2,1)}, bf16[512,1024]{1,0:T(8,128)(2,1)}) fusion(f32[512,1024]{1,0:T(8,128)S(1)} %constant_dynamic-update-slice_fusion.6), kind=kLoop, calls=%fused_computation.25 | loop fusion | flops 2097152 | bytes 4194304 | tf_op jit(solution)/shard_map/convert_element_type | solution.py:23
  91.5 1.7 %collective-permute-done.10 = f32[128,1024]{1,0:T(8,128)S(1)} collective-permute-done((f32[128,1024]{1,0:T(8,128)S(1)}, f32[128,1024]{1,0:T(8,128)S(1)}, u32[]{:S(2)}, u32[]{:S(2)}) %collective-permute-start.10) | collective-permute-done | bytes 524320 | tf_op jit(solution)/shard_map/ppermute | solution.py:50
  93.2 3.7 %collective-permute-start.14 = (f32[128,1024]{1,0:T(8,128)S(1)}, f32[128,1024]{1,0:T(8,128)S(1)}, u32[]{:S(2)}, u32[]{:S(2)}) collective-permute-start(f32[128,1024]{1,0:T(8,128)S(1)} %collective-permute-done.10), channel_id=1, source_target_pairs={{0,7},{1,0},{2,1},{3,2},{4,3},{5,4},{6,5},{7,6},{8,15},{9,8},{10,9... | collective-permute-start | bytes 1572872 | tf_op jit(solution)/shard_map/ppermute | solution.py:55
  97.0 10.5 %collective-permute-done.13 = f32[128,1024]{1,0:T(8,128)S(1)} collective-permute-done((f32[128,1024]{1,0:T(8,128)S(1)}, f32[128,1024]{1,0:T(8,128)S(1)}, u32[]{:S(2)}, u32[]{:S(2)}) %collective-permute-start.13) | collective-permute-done | bytes 524320 | tf_op jit(solution)/shard_map/ppermute | solution.py:54
  107.6 1.8 %reduce-precision_convert_fusion.1 = (bf16[512,1024]{1,0:T(8,128)(2,1)}, bf16[512,1024]{1,0:T(8,128)(2,1)}) fusion(f32[512,1024]{1,0:T(8,128)S(1)} %constant_dynamic-update-slice_fusion.10), kind=kLoop, calls=%fused_computation.23 | loop fusion | flops 2097152 | bytes 4194304 | tf_op jit(solution)/shard_map/convert_element_type | solution.py:23
  109.7 4.0 %copy.9 = f32[16,2,32,2048]{3,2,0,1:T(8,128)S(1)} copy(f32[16,2,32,2048]{3,2,1,0:T(8,128)} %bitcast.27) | data formatting | bytes 16777216 | tf_op jit(solution)/shard_map/reshape | solution.py:73
  113.7 3.9 %fusion = (bf16[1024,2048]{1,0:T(8,128)(2,1)}, bf16[1024,2048]{1,0:T(8,128)(2,1)S(1)}) fusion(f32[16,2,32,2048]{3,2,0,1:T(8,128)S(1)} %copy.9), kind=kLoop, calls=%fused_computation.2 | loop fusion | flops 8388608 | bytes 16777216 | tf_op jit(solution)/shard_map/convert_element_type | solution.py:23
  117.9 1.8 %copy-done.2 = bf16[1024,2048]{1,0:T(8,128)(2,1)S(1)} copy-done((bf16[1024,2048]{1,0:T(8,128)(2,1)S(1)}, bf16[1024,2048]{1,0:T(8,128)(2,1)}, u32[]{:S(2)}) %copy-start.2) | copy-done | bytes 4194328
  120.4 1.7 %copy-done.11 = bf16[1024,1536]{1,0:T(8,128)(2,1)} copy-done((bf16[1024,1536]{1,0:T(8,128)(2,1)}, bf16[1024,1536]{1,0:T(8,128)(2,1)S(1)}, u32[]{:S(2)}) %copy-start.11) | copy-done | bytes 3145752
  122.5 3.5 %fusion.7 = f32[1024,1024]{1,0:T(8,128)S(1)} fusion(bf16[1024,1536]{1,0:T(8,128)(2,1)S(1)} %get-tuple-element.19, bf16[512,1024]{1,0:T(8,128)(2,1)S(1)} %copy-done.6, bf16[512,1024]{1,0:T(8,128)(2,1)S(1)} %copy-done.5), kind=kOutput, calls=%fused_computation.10 | convolution fusion | flops 3230662656 | bytes 9437184 | tf_op jit(solution)/shard_map/dot_general | solution.py:88
  126.0 3.5 %fusion.1 = f32[1024,1024]{1,0:T(8,128)S(1)} fusion(bf16[1024,1536]{1,0:T(8,128)(2,1)S(1)} %get-tuple-element.17, bf16[512,1024]{1,0:T(8,128)(2,1)S(1)} %copy-done.4, bf16[512,1024]{1,0:T(8,128)(2,1)S(1)} %copy-done.3), kind=kOutput, calls=%fused_computation.4 | convolution fusion | flops 3230662656 | bytes 9437184 | tf_op jit(solution)/shard_map/dot_general | solution.py:88
  129.5 3.8 %fusion.13 = f32[1024,1024]{1,0:T(8,128)S(1)} fusion(bf16[1024,1536]{1,0:T(8,128)(2,1)S(1)} %copy-done.12, bf16[512,1024]{1,0:T(8,128)(2,1)S(1)} %copy-done.8, bf16[512,1024]{1,0:T(8,128)(2,1)S(1)} %copy-done.7), kind=kOutput, calls=%fused_computation.16 | convolution fusion | flops 3230662656 | bytes 9437184 | tf_op jit(solution)/shard_map/dot_general | solution.py:88
  133.3 1.9 %fusion.22 = f32[1024,1024]{1,0:T(8,128)S(1)} fusion(bf16[256,1024]{1,0:T(8,128)(2,1)S(1)} %copy-done.10, bf16[256,1024]{1,0:T(8,128)(2,1)S(1)} %get-tuple-element.37, bf16[1024,256]{1,0:T(8,128)(2,1)S(1)} %get-tuple-element.16, bf16[1024,256]{1,0:T(8,128)(2,1)S(1)} %get-tuple-element.11), kind=kOutput, calls=%fused_computation.31 | convolution fusion | flops 1620049920 | bytes 6291456 | tf_op jit(solution)/shard_map/dot_general | solution.py:88
  135.2 4.1 %add_add_fusion = f32[1024,1024]{1,0:T(8,128)} fusion(f32[1024,1024]{1,0:T(8,128)S(1)} %fusion.13, f32[1024,1024]{1,0:T(8,128)S(1)} %fusion.7, f32[1024,1024]{1,0:T(8,128)S(1)} %fusion.22, f32[1024,1024]{1,0:T(8,128)S(1)} %fusion.1, bf16[1024,256]{1,0:T(8,128)(2,1)S(1)} %get-tuple-element.12, bf16[256,1024]{1,0:T(8,128)(2,1)S(1)} %get-tuple-element.36, ...), kind=kOutput, calls=%fused_computation.3 | convolution fusion | flops 1624244224 | bytes 23068672 | tf_op jit(solution)/shard_map/dot_general | solution.py:88
  (75 shorter events, 5.6 us)
Async XLA Ops:
  6.5 0.7 copy-start
  6.5 103.2 %all-gather.2.cloned.1.call-start = ((), (), s32[]{:S(2)}) async-start(), calls=%async_computation | async-start | bytes 8912896 | tf_op jit(solution)/shard_map/all_gather | solution.py:69
  11.7 3.6 %copy-start.9 = (f32[128,1024]{1,0:T(8,128)S(1)}, f32[128,1024]{1,0:T(8,128)}, u32[]{:S(2)}) copy-start(f32[128,1024]{1,0:T(8,128)} %param.6) | copy-start | bytes 1572868
  15.3 15.3 %collective-permute-start = (f32[128,1024]{1,0:T(8,128)S(1)}, f32[128,1024]{1,0:T(8,128)S(1)}, u32[]{:S(2)}, u32[]{:S(2)}) collective-permute-start(f32[128,1024]{1,0:T(8,128)S(1)} %copy-done.9), channel_id=1, source_target_pairs={{0,8},{8,0},{1,9},{9,1},{2,10},{10,2},{3,11},{11,3},{4,12},{12,4},... | collective-permute-start | bytes 1572872 | tf_op jit(solution)/shard_map/ppermute | solution.py:41
  15.9 23.9 %collective-permute-start.1 = (f32[128,1024]{1,0:T(8,128)S(1)}, f32[128,1024]{1,0:T(8,128)S(1)}, u32[]{:S(2)}, u32[]{:S(2)}) collective-permute-start(f32[128,1024]{1,0:T(8,128)S(1)} %copy-done.9), channel_id=1, source_target_pairs={{0,7},{1,0},{2,1},{3,2},{4,3},{5,4},{6,5},{7,6},{8,15},{9,8},{10,9... | collective-permute-start | bytes 1572872 | tf_op jit(solution)/shard_map/ppermute | solution.py:48
  21.8 21.3 %collective-permute-start.3 = (f32[128,1024]{1,0:T(8,128)S(1)}, f32[128,1024]{1,0:T(8,128)S(1)}, u32[]{:S(2)}, u32[]{:S(2)}) collective-permute-start(f32[128,1024]{1,0:T(8,128)S(1)} %copy-done.9), channel_id=1, source_target_pairs={{0,1},{1,2},{2,3},{3,4},{4,5},{5,6},{6,7},{7,0},{8,9},{9,10},{10,1... | collective-permute-start | bytes 1572872 | tf_op jit(solution)/shard_map/ppermute | solution.py:47
  30.6 21.6 %collective-permute-start.2 = (f32[128,1024]{1,0:T(8,128)S(1)}, f32[128,1024]{1,0:T(8,128)S(1)}, u32[]{:S(2)}, u32[]{:S(2)}) collective-permute-start(f32[128,1024]{1,0:T(8,128)S(1)} %collective-permute-done), channel_id=1, source_target_pairs={{0,7},{1,0},{2,1},{3,2},{4,3},{5,4},{6,5},{7,6},{8,15},{9,8},{10,9... | collective-permute-start | bytes 1572872 | tf_op jit(solution)/shard_map/ppermute | solution.py:50
  39.9 16.0 %collective-permute-start.4 = (f32[128,1024]{1,0:T(8,128)S(1)}, f32[128,1024]{1,0:T(8,128)S(1)}, u32[]{:S(2)}, u32[]{:S(2)}) collective-permute-start(f32[128,1024]{1,0:T(8,128)S(1)} %collective-permute-done), channel_id=1, source_target_pairs={{0,1},{1,2},{2,3},{3,4},{4,5},{5,6},{6,7},{7,0},{8,9},{9,10},{10,1... | collective-permute-start | bytes 1572872 | tf_op jit(solution)/shard_map/ppermute | solution.py:49
  39.9 23.5 %collective-permute-start.5 = (f32[128,1024]{1,0:T(8,128)S(1)}, f32[128,1024]{1,0:T(8,128)S(1)}, u32[]{:S(2)}, u32[]{:S(2)}) collective-permute-start(f32[128,1024]{1,0:T(8,128)S(1)} %collective-permute-done.1), channel_id=1, source_target_pairs={{0,7},{1,0},{2,1},{3,2},{4,3},{5,4},{6,5},{7,6},{8,15},{9,8},{10,9... | collective-permute-start | bytes 1572872 | tf_op jit(solution)/shard_map/ppermute | solution.py:48
  43.1 24.0 %collective-permute-start.7 = (f32[128,1024]{1,0:T(8,128)S(1)}, f32[128,1024]{1,0:T(8,128)S(1)}, u32[]{:S(2)}, u32[]{:S(2)}) collective-permute-start(f32[128,1024]{1,0:T(8,128)S(1)} %collective-permute-done.3), channel_id=1, source_target_pairs={{0,1},{1,2},{2,3},{3,4},{4,5},{5,6},{6,7},{7,0},{8,9},{9,10},{10,1... | collective-permute-start | bytes 1572872 | tf_op jit(solution)/shard_map/ppermute | solution.py:47
  52.2 22.5 %collective-permute-start.6 = (f32[128,1024]{1,0:T(8,128)S(1)}, f32[128,1024]{1,0:T(8,128)S(1)}, u32[]{:S(2)}, u32[]{:S(2)}) collective-permute-start(f32[128,1024]{1,0:T(8,128)S(1)} %collective-permute-done.2), channel_id=1, source_target_pairs={{0,7},{1,0},{2,1},{3,2},{4,3},{5,4},{6,5},{7,6},{8,15},{9,8},{10,9... | collective-permute-start | bytes 1572872 | tf_op jit(solution)/shard_map/ppermute | solution.py:50
  55.9 22.5 %collective-permute-start.8 = (f32[128,1024]{1,0:T(8,128)S(1)}, f32[128,1024]{1,0:T(8,128)S(1)}, u32[]{:S(2)}, u32[]{:S(2)}) collective-permute-start(f32[128,1024]{1,0:T(8,128)S(1)} %collective-permute-done.4), channel_id=1, source_target_pairs={{0,1},{1,2},{2,3},{3,4},{4,5},{5,6},{6,7},{7,0},{8,9},{9,10},{10,1... | collective-permute-start | bytes 1572872 | tf_op jit(solution)/shard_map/ppermute | solution.py:49
  63.4 28.1 %collective-permute-start.9 = (f32[128,1024]{1,0:T(8,128)S(1)}, f32[128,1024]{1,0:T(8,128)S(1)}, u32[]{:S(2)}, u32[]{:S(2)}) collective-permute-start(f32[128,1024]{1,0:T(8,128)S(1)} %collective-permute-done.5), channel_id=1, source_target_pairs={{0,7},{1,0},{2,1},{3,2},{4,3},{5,4},{6,5},{7,6},{8,15},{9,8},{10,9... | collective-permute-start | bytes 1572872 | tf_op jit(solution)/shard_map/ppermute | solution.py:48
  67.1 22.5 %collective-permute-start.11 = (f32[128,1024]{1,0:T(8,128)S(1)}, f32[128,1024]{1,0:T(8,128)S(1)}, u32[]{:S(2)}, u32[]{:S(2)}) collective-permute-start(f32[128,1024]{1,0:T(8,128)S(1)} %collective-permute-done.7), channel_id=1, source_target_pairs={{0,1},{1,2},{2,3},{3,4},{4,5},{5,6},{6,7},{7,0},{8,9},{9,10},{10,1... | collective-permute-start | bytes 1572872 | tf_op jit(solution)/shard_map/ppermute | solution.py:47
  74.6 18.6 %collective-permute-start.10 = (f32[128,1024]{1,0:T(8,128)S(1)}, f32[128,1024]{1,0:T(8,128)S(1)}, u32[]{:S(2)}, u32[]{:S(2)}) collective-permute-start(f32[128,1024]{1,0:T(8,128)S(1)} %collective-permute-done.6), channel_id=1, source_target_pairs={{0,7},{1,0},{2,1},{3,2},{4,3},{5,4},{6,5},{7,6},{8,15},{9,8},{10,9... | collective-permute-start | bytes 1572872 | tf_op jit(solution)/shard_map/ppermute | solution.py:50
  78.3 29.2 %collective-permute-start.12 = (f32[128,1024]{1,0:T(8,128)S(1)}, f32[128,1024]{1,0:T(8,128)S(1)}, u32[]{:S(2)}, u32[]{:S(2)}) collective-permute-start(f32[128,1024]{1,0:T(8,128)S(1)} %collective-permute-done.8), channel_id=1, source_target_pairs={{0,1},{1,2},{2,3},{3,4},{4,5},{5,6},{6,7},{7,0},{8,9},{9,10},{10,1... | collective-permute-start | bytes 1572872 | tf_op jit(solution)/shard_map/ppermute | solution.py:49
  89.6 17.9 %collective-permute-start.13 = (f32[128,1024]{1,0:T(8,128)S(1)}, f32[128,1024]{1,0:T(8,128)S(1)}, u32[]{:S(2)}, u32[]{:S(2)}) collective-permute-start(f32[128,1024]{1,0:T(8,128)S(1)} %collective-permute-done.11), channel_id=1, source_target_pairs={{0,1},{1,2},{2,3},{3,4},{4,5},{5,6},{6,7},{7,0},{8,9},{9,10},{10,1... | collective-permute-start | bytes 1572872 | tf_op jit(solution)/shard_map/ppermute | solution.py:54
  93.2 16.2 %collective-permute-start.14 = (f32[128,1024]{1,0:T(8,128)S(1)}, f32[128,1024]{1,0:T(8,128)S(1)}, u32[]{:S(2)}, u32[]{:S(2)}) collective-permute-start(f32[128,1024]{1,0:T(8,128)S(1)} %collective-permute-done.10), channel_id=1, source_target_pairs={{0,7},{1,0},{2,1},{3,2},{4,3},{5,4},{6,5},{7,6},{8,15},{9,8},{10,9... | collective-permute-start | bytes 1572872 | tf_op jit(solution)/shard_map/ppermute | solution.py:55
  117.6 2.2 %copy-start.2 = (bf16[1024,2048]{1,0:T(8,128)(2,1)S(1)}, bf16[1024,2048]{1,0:T(8,128)(2,1)}, u32[]{:S(2)}) copy-start(bf16[1024,2048]{1,0:T(8,128)(2,1)} %get-tuple-element.5) | copy-start | bytes 12582916
  120.1 2.0 %copy-start.5 = (bf16[512,1024]{1,0:T(8,128)(2,1)S(1)}, bf16[512,1024]{1,0:T(8,128)(2,1)}, u32[]{:S(2)}) copy-start(bf16[512,1024]{1,0:T(8,128)(2,1)} %get-tuple-element.31) | copy-start | bytes 3145732
  120.1 2.3 %copy-start.6 = (bf16[512,1024]{1,0:T(8,128)(2,1)S(1)}, bf16[512,1024]{1,0:T(8,128)(2,1)}, u32[]{:S(2)}) copy-start(bf16[512,1024]{1,0:T(8,128)(2,1)} %get-tuple-element.32) | copy-start | bytes 3145732
  120.4 1.7 %copy-start.11 = (bf16[1024,1536]{1,0:T(8,128)(2,1)}, bf16[1024,1536]{1,0:T(8,128)(2,1)S(1)}, u32[]{:S(2)}) copy-start(bf16[1024,1536]{1,0:T(8,128)(2,1)S(1)} %get-tuple-element.18) | copy-start | bytes 9437188
  122.4 3.5 %copy-start.3 = (bf16[512,1024]{1,0:T(8,128)(2,1)S(1)}, bf16[512,1024]{1,0:T(8,128)(2,1)}, u32[]{:S(2)}) copy-start(bf16[512,1024]{1,0:T(8,128)(2,1)} %get-tuple-element.29) | copy-start | bytes 3145732
  122.4 3.5 %copy-start.4 = (bf16[512,1024]{1,0:T(8,128)(2,1)S(1)}, bf16[512,1024]{1,0:T(8,128)(2,1)}, u32[]{:S(2)}) copy-start(bf16[512,1024]{1,0:T(8,128)(2,1)} %get-tuple-element.30) | copy-start | bytes 3145732
  126.0 3.5 %copy-start.7 = (bf16[512,1024]{1,0:T(8,128)(2,1)S(1)}, bf16[512,1024]{1,0:T(8,128)(2,1)}, u32[]{:S(2)}) copy-start(bf16[512,1024]{1,0:T(8,128)(2,1)} %get-tuple-element.33) | copy-start | bytes 3145732
  126.0 3.5 %copy-start.8 = (bf16[512,1024]{1,0:T(8,128)(2,1)S(1)}, bf16[512,1024]{1,0:T(8,128)(2,1)}, u32[]{:S(2)}) copy-start(bf16[512,1024]{1,0:T(8,128)(2,1)} %get-tuple-element.34) | copy-start | bytes 3145732
  126.0 3.5 %copy-start.12 = (bf16[1024,1536]{1,0:T(8,128)(2,1)S(1)}, bf16[1024,1536]{1,0:T(8,128)(2,1)}, u32[]{:S(2)}) copy-start(bf16[1024,1536]{1,0:T(8,128)(2,1)} %copy-done.11) | copy-start | bytes 9437188
  129.5 3.8 %copy-start.10 = (bf16[256,1024]{1,0:T(8,128)(2,1)S(1)}, bf16[256,1024]{1,0:T(8,128)(2,1)}, u32[]{:S(2)}) copy-start(bf16[256,1024]{1,0:T(8,128)(2,1)} %get-tuple-element.38) | copy-start | bytes 1572868
  135.2 4.1 %copy-start.1 = (f32[512]{0:T(512)S(1)}, f32[512]{0:T(512)}, u32[]{:S(2)}) copy-start(f32[512]{0:T(512)} %param.9) | copy-start | bytes 6148
Sparse Core Ops, SparseCore 0:
  15.4 56.9 all-gather.1

commit v8 on v5

--- a/solution.py
+++ b/solution.py
@@ -58,8 +58,7 @@
     vir_energy = lookup(vir_perm, eps_vir)
     occ_energy = lookup(occ_map, eps_occ)
     pair_energy = (vir_energy[None, :] - occ_energy[:, None]).reshape(-1)
-    j_index = jnp.arange(j_local, dtype=jnp.int32) + col * j_local
-    j_energy = lookup(j_index, eps_occ)
+    j_energy = lax.dynamic_slice_in_dim(eps_occ, col * j_local, j_local)
     b_energy = lax.dynamic_slice_in_dim(vir_energy, row * b_local, b_local)
     denominator = pair_energy[None, None, :] + b_energy[None, :, None] - j_energy[:, None, None]
     scaled = amps / denominator
@@ -73,7 +72,7 @@
     s_hi, s_lo = split_bf16(s_cols)
     width = nxhi * blk
     out = None
-    for group in ([0], [1, nz - 1], [2, nz - 2], [3, nz - 3], [half]):
+    for group in ([0], [1, nz - 1], [2, nz - 2], [3, nz - 3, half]):
         w_g = jnp.concatenate([blocks[d][t] for d in group for t in range(nxhi)], axis=0)
         w_hi, w_lo = split_bf16(w_g)
         lhs = jnp.concatenate([w_hi, w_hi, w_lo], axis=0)

time: 141 us -> 146 us (1.035)
  matrix products: 19.7 us -> 23.5 us
  local copies, waits for them, and re-layouts: 6.45 us -> 8.34 us
    dot_general x5 -> x4, matrix products: 16.7 us -> 21.3 us  [layer(): lax.dot_general(lhs, rhs, (((0,), (1,)), ((), ())), preferred_element_typ...]
    ppermute x4, waiting for transfers between devices: 21.8 us -> 17.9 us  [layer(): f_own = lax.ppermute(f_own, 'z', fwd)]
    ppermute x3, waiting for transfers between devices: 0.01 us -> 3.79 us  [layer(): f_oth = lax.ppermute(f_oth, 'z', fwd)]
    unnamed x34 -> x53, local copies, waits for them, and re-layouts: 2.88 us -> 4.21 us
    dot_general x3 -> x2, matrix products: 3.02 us -> 2.18 us  [lookup(): jnp.dot(onehot, table, precision=lax.Precision.HIGHEST, preferred_element...]
    convert_element_type x6 -> x5, other arithmetic: 10.6 us -> 10.7 us  [split_bf16(): return (hi.astype(jnp.bfloat16), (x - hi).astype(jnp.bfloat16))]
  transfers between devices with their start and end apart: 16 -> 16, of which waited for: 7 -> 8; matrix products, arithmetic and copies ran while one was open for 4% -> 4% of each run, Pallas kernels for 0% -> 0%
where the time goes in v8:
time: 146 us; the launch traced here: 145 us
  waiting for transfers between devices  53 us (36%)
  starting transfers between devices  33.7 us (23%)
  matrix products  23.5 us (16%)
  between operations  13.9 us (10%)
  other arithmetic  12.8 us (9%)
  local copies, waits for them, and re-layouts  8.34 us (6%)
    dot_general x4, matrix products, layer(): lax.dot_general(lhs, rhs, (((0,), (1,)), ((), ())), preferred_element_typ...  21.3 us
    ppermute x4, starting transfers between devices, layer(): b_oth = lax.ppermute(b_oth, 'z', bwd)  20.3 us
    ppermute x4, waiting for transfers between devices, layer(): f_own = lax.ppermute(f_own, 'z', fwd)  17.9 us
    ppermute x4, waiting for transfers between devices, layer(): b_oth = lax.ppermute(b_oth, 'z', bwd)  15 us
    ppermute x3, starting transfers between devices, layer(): b_own = lax.ppermute(b_own, 'z', bwd)  12.8 us
    convert_element_type x5, other arithmetic, split_bf16(): return (hi.astype(jnp.bfloat16), (x - hi).astype(jnp.bfloat16))  10.7 us
    ppermute x1, waiting for transfers between devices, layer(): w_other = lax.ppermute(w_cycle, 'xhi', [(0, 1), (1, 0)])  8.75 us
    ppermute x3, waiting for transfers between devices, layer(): b_own = lax.ppermute(b_own, 'z', bwd)  7.54 us
  transfers between devices with their start and end apart: 16, of which 8 were waited for; matrix products, arithmetic and copies ran while one was open for 4% of the time, Pallas kernels for 0%

profile of v8, /device:TPU:28, one launch (start us, length us, event | category | flops | bytes accessed | tf_op | source)
XLA Modules:
  0.0 145.2 jit_solution(9107681019527877508)
XLA Ops:
  6.5 0.7 dynamic_slice.11
  7.3 0.9 convolution_bitcast_fusion
  8.1 1.3 fusion.36
  9.7 1.2 subtract_divide_fusion
  11.3 1.3 rev.3
  13.4 1.2 reshape.60
  15.3 5.9 %collective-permute-start.1 = (f32[128,1024]{1,0:T(8,128)S(1)}, f32[128,1024]{1,0:T(8,128)S(1)}, u32[]{:S(2)}, u32[]{:S(2)}) collective-permute-start(f32[128,1024]{1,0:T(8,128)S(1)} %copy-done.6), channel_id=1, source_target_pairs={{0,7},{1,0},{2,1},{3,2},{4,3},{5,4},{6,5},{7,6},{8,15},{9,8},{10,9... | collective-permute-start | bytes 1572872 | tf_op jit(solution)/shard_map/ppermute | solution.py:48
  21.2 8.8 %collective-permute-done = f32[128,1024]{1,0:T(8,128)S(1)} collective-permute-done((f32[128,1024]{1,0:T(8,128)S(1)}, f32[128,1024]{1,0:T(8,128)S(1)}, u32[]{:S(2)}, u32[]{:S(2)}) %collective-permute-start) | collective-permute-done | bytes 524320 | tf_op jit(solution)/shard_map/ppermute | solution.py:41
  29.9 9.3 %collective-permute-start.2 = (f32[128,1024]{1,0:T(8,128)S(1)}, f32[128,1024]{1,0:T(8,128)S(1)}, u32[]{:S(2)}, u32[]{:S(2)}) collective-permute-start(f32[128,1024]{1,0:T(8,128)S(1)} %collective-permute-done), channel_id=1, source_target_pairs={{0,7},{1,0},{2,1},{3,2},{4,3},{5,4},{6,5},{7,6},{8,15},{9,8},{10,9... | collective-permute-start | bytes 1572872 | tf_op jit(solution)/shard_map/ppermute | solution.py:50
  39.2 3.2 %collective-permute-start.5 = (f32[128,1024]{1,0:T(8,128)S(1)}, f32[128,1024]{1,0:T(8,128)S(1)}, u32[]{:S(2)}, u32[]{:S(2)}) collective-permute-start(f32[128,1024]{1,0:T(8,128)S(1)} %collective-permute-done.1), channel_id=1, source_target_pairs={{0,7},{1,0},{2,1},{3,2},{4,3},{5,4},{6,5},{7,6},{8,15},{9,8},{10,9... | collective-permute-start | bytes 1572872 | tf_op jit(solution)/shard_map/ppermute | solution.py:48
  42.6 1.2 reduce-precision_convert_fusion.4
  43.8 7.8 %collective-permute-done.2 = f32[128,1024]{1,0:T(8,128)S(1)} collective-permute-done((f32[128,1024]{1,0:T(8,128)S(1)}, f32[128,1024]{1,0:T(8,128)S(1)}, u32[]{:S(2)}, u32[]{:S(2)}) %collective-permute-start.2) | collective-permute-done | bytes 524320 | tf_op jit(solution)/shard_map/ppermute | solution.py:50
  51.5 3.7 %collective-permute-start.6 = (f32[128,1024]{1,0:T(8,128)S(1)}, f32[128,1024]{1,0:T(8,128)S(1)}, u32[]{:S(2)}, u32[]{:S(2)}) collective-permute-start(f32[128,1024]{1,0:T(8,128)S(1)} %collective-permute-done.2), channel_id=1, source_target_pairs={{0,7},{1,0},{2,1},{3,2},{4,3},{5,4},{6,5},{7,6},{8,15},{9,8},{10,9... | collective-permute-start | bytes 1572872 | tf_op jit(solution)/shard_map/ppermute | solution.py:50
  55.2 7.5 %collective-permute-done.5 = f32[128,1024]{1,0:T(8,128)S(1)} collective-permute-done((f32[128,1024]{1,0:T(8,128)S(1)}, f32[128,1024]{1,0:T(8,128)S(1)}, u32[]{:S(2)}, u32[]{:S(2)}) %collective-permute-start.5) | collective-permute-done | bytes 524320 | tf_op jit(solution)/shard_map/ppermute | solution.py:48
  62.8 3.7 %collective-permute-start.9 = (f32[128,1024]{1,0:T(8,128)S(1)}, f32[128,1024]{1,0:T(8,128)S(1)}, u32[]{:S(2)}, u32[]{:S(2)}) collective-permute-start(f32[128,1024]{1,0:T(8,128)S(1)} %collective-permute-done.5), channel_id=1, source_target_pairs={{0,7},{1,0},{2,1},{3,2},{4,3},{5,4},{6,5},{7,6},{8,15},{9,8},{10,9... | collective-permute-start | bytes 1572872 | tf_op jit(solution)/shard_map/ppermute | solution.py:48
  66.7 1.8 %reduce-precision_convert_fusion.3 = (bf16[512,1024]{1,0:T(8,128)(2,1)}, bf16[512,1024]{1,0:T(8,128)(2,1)}) fusion(f32[512,1024]{1,0:T(8,128)S(1)} %constant_dynamic-update-slice_fusion.2), kind=kLoop, calls=%fused_computation.28 | loop fusion | flops 2097152 | bytes 4194304 | tf_op jit(solution)/shard_map/convert_element_type | solution.py:23
  68.5 5.5 %collective-permute-done.6 = f32[128,1024]{1,0:T(8,128)S(1)} collective-permute-done((f32[128,1024]{1,0:T(8,128)S(1)}, f32[128,1024]{1,0:T(8,128)S(1)}, u32[]{:S(2)}, u32[]{:S(2)}) %collective-permute-start.6) | collective-permute-done | bytes 524320 | tf_op jit(solution)/shard_map/ppermute | solution.py:50
  74.0 3.7 %collective-permute-start.10 = (f32[128,1024]{1,0:T(8,128)S(1)}, f32[128,1024]{1,0:T(8,128)S(1)}, u32[]{:S(2)}, u32[]{:S(2)}) collective-permute-start(f32[128,1024]{1,0:T(8,128)S(1)} %collective-permute-done.6), channel_id=1, source_target_pairs={{0,7},{1,0},{2,1},{3,2},{4,3},{5,4},{6,5},{7,6},{8,15},{9,8},{10,9... | collective-permute-start | bytes 1572872 | tf_op jit(solution)/shard_map/ppermute | solution.py:50
  77.7 11.2 %collective-permute-done.11 = f32[128,1024]{1,0:T(8,128)S(1)} collective-permute-done((f32[128,1024]{1,0:T(8,128)S(1)}, f32[128,1024]{1,0:T(8,128)S(1)}, u32[]{:S(2)}, u32[]{:S(2)}) %collective-permute-start.11) | collective-permute-done | bytes 524320 | tf_op jit(solution)/shard_map/ppermute | solution.py:47
  89.1 1.7 %reduce-precision_convert_fusion.2 = (bf16[512,1024]{1,0:T(8,128)(2,1)}, bf16[512,1024]{1,0:T(8,128)(2,1)}) fusion(f32[512,1024]{1,0:T(8,128)S(1)} %constant_dynamic-update-slice_fusion.6), kind=kLoop, calls=%fused_computation.26 | loop fusion | flops 2097152 | bytes 4194304 | tf_op jit(solution)/shard_map/convert_element_type | solution.py:23
  90.8 1.7 %collective-permute-done.10 = f32[128,1024]{1,0:T(8,128)S(1)} collective-permute-done((f32[128,1024]{1,0:T(8,128)S(1)}, f32[128,1024]{1,0:T(8,128)S(1)}, u32[]{:S(2)}, u32[]{:S(2)}) %collective-permute-start.10) | collective-permute-done | bytes 524320 | tf_op jit(solution)/shard_map/ppermute | solution.py:50
  92.6 3.7 %collective-permute-start.14 = (f32[128,1024]{1,0:T(8,128)S(1)}, f32[128,1024]{1,0:T(8,128)S(1)}, u32[]{:S(2)}, u32[]{:S(2)}) collective-permute-start(f32[128,1024]{1,0:T(8,128)S(1)} %collective-permute-done.10), channel_id=1, source_target_pairs={{0,7},{1,0},{2,1},{3,2},{4,3},{5,4},{6,5},{7,6},{8,15},{9,8},{10,9... | collective-permute-start | bytes 1572872 | tf_op jit(solution)/shard_map/ppermute | solution.py:55
  96.4 3.8 %collective-permute-done.12 = f32[128,1024]{1,0:T(8,128)S(1)} collective-permute-done((f32[128,1024]{1,0:T(8,128)S(1)}, f32[128,1024]{1,0:T(8,128)S(1)}, u32[]{:S(2)}, u32[]{:S(2)}) %collective-permute-start.12) | collective-permute-done | bytes 524320 | tf_op jit(solution)/shard_map/ppermute | solution.py:49
  100.2 6.7 %collective-permute-done.13 = f32[128,1024]{1,0:T(8,128)S(1)} collective-permute-done((f32[128,1024]{1,0:T(8,128)S(1)}, f32[128,1024]{1,0:T(8,128)S(1)}, u32[]{:S(2)}, u32[]{:S(2)}) %collective-permute-start.13) | collective-permute-done | bytes 524320 | tf_op jit(solution)/shard_map/ppermute | solution.py:54
  107.0 0.7 reduce-precision_convert_fusion.1
  107.7 5.2 %fusion = (bf16[1024,2048]{1,0:T(8,128)(2,1)S(1)}, bf16[1024,2048]{1,0:T(8,128)(2,1)S(1)}) fusion(f32[2,512,2048]{2,1,0:T(8,128)} %all-gather.2.cloned.1.call-done), kind=kLoop, calls=%fused_computation.2 | loop fusion | flops 8388608 | bytes 16777216 | tf_op jit(solution)/shard_map/convert_element_type | solution.py:23
  114.3 1.8 %copy-done.9 = bf16[1024,2304]{1,0:T(8,128)(2,1)} copy-done((bf16[1024,2304]{1,0:T(8,128)(2,1)}, bf16[1024,2304]{1,0:T(8,128)(2,1)S(1)}, u32[]{:S(2)}) %copy-start.9) | copy-done | bytes 4718616
  116.4 0.7 copy-done.5
  117.0 5.0 %fusion.14 = f32[1024,1024]{1,0:T(8,128)} fusion(bf16[1024,1536]{1,0:T(8,128)(2,1)S(1)} %slice_dynamic-update-slice_fusion.14, bf16[512,1024]{1,0:T(8,128)(2,1)S(1)} %copy-done.5, bf16[512,1024]{1,0:T(8,128)(2,1)S(1)} %copy-done.4), kind=kOutput, calls=%fused_computation.19 | convolution fusion | flops 3230662656 | bytes 9437184 | tf_op jit(solution)/shard_map/dot_general | solution.py:83
  122.1 5.1 %fusion.8 = f32[1024,1024]{1,0:T(8,128)} fusion(bf16[1024,1536]{1,0:T(8,128)(2,1)S(1)} %get-tuple-element.13, bf16[512,1024]{1,0:T(8,128)(2,1)S(1)} %copy-done.3, bf16[512,1024]{1,0:T(8,128)(2,1)S(1)} %copy-done.2), kind=kOutput, calls=%fused_computation.13 | convolution fusion | flops 3230662656 | bytes 9437184 | tf_op jit(solution)/shard_map/dot_general | solution.py:83
  127.2 1.8 %fusion.24 = f32[1024,1024]{1,0:T(8,128)S(1)} fusion(bf16[256,1024]{1,0:T(8,128)(2,1)S(1)} %copy-done.8, bf16[256,1024]{1,0:T(8,128)(2,1)S(1)} %copy-done.7, bf16[1024,256]{1,0:T(8,128)(2,1)S(1)} %get-tuple-element.10, bf16[1024,256]{1,0:T(8,128)(2,1)S(1)} %get-tuple-element.12), kind=kOutput, calls=%fused_computation.31 | convolution fusion | flops 1620049920 | bytes 6291456 | tf_op jit(solution)/shard_map/dot_general | solution.py:83
  129.1 9.3 %add_add_fusion = f32[1024,1024]{1,0:T(8,128)} fusion(f32[1024,1024]{1,0:T(8,128)} %fusion.14, f32[1024,1024]{1,0:T(8,128)S(1)} %fusion.24, f32[1024,1024]{1,0:T(8,128)} %fusion.8, bf16[1024,2304]{1,0:T(8,128)(2,1)S(1)} %bitcast.28, bf16[768,1024]{1,0:T(8,128)(2,1)S(1)} %get-tuple-element.16, bf16[768,1024]{1,0:T(8,128)(2,1)S(1)} %get-tuple-element.15), kind=kOutput, calls=%fused_computation.11 | convolution fusion | flops 4849139712 | bytes 24641536 | tf_op jit(solution)/shard_map/dot_general | solution.py:83
  (83 shorter events, 4.2 us)
Async XLA Ops:
  6.5 1.6 %copy-start = (f32[512]{0:T(512)S(1)}, f32[512]{0:T(512)}, u32[]{:S(2)}) copy-start(f32[512]{0:T(512)} %param.9) | copy-start | bytes 6148
  6.5 101.1 %all-gather.2.cloned.1.call-start = ((), (), s32[]{:S(2)}) async-start(), calls=%async_computation | async-start | bytes 8912896 | tf_op jit(solution)/shard_map/all_gather | solution.py:69
  11.0 3.7 %copy-start.6 = (f32[128,1024]{1,0:T(8,128)S(1)}, f32[128,1024]{1,0:T(8,128)}, u32[]{:S(2)}) copy-start(f32[128,1024]{1,0:T(8,128)} %param.6) | copy-start | bytes 1572868
  14.7 15.3 %collective-permute-start = (f32[128,1024]{1,0:T(8,128)S(1)}, f32[128,1024]{1,0:T(8,128)S(1)}, u32[]{:S(2)}, u32[]{:S(2)}) collective-permute-start(f32[128,1024]{1,0:T(8,128)S(1)} %copy-done.6), channel_id=1, source_target_pairs={{0,8},{8,0},{1,9},{9,1},{2,10},{10,2},{3,11},{11,3},{4,12},{12,4},... | collective-permute-start | bytes 1572872 | tf_op jit(solution)/shard_map/ppermute | solution.py:41
  15.3 23.9 %collective-permute-start.1 = (f32[128,1024]{1,0:T(8,128)S(1)}, f32[128,1024]{1,0:T(8,128)S(1)}, u32[]{:S(2)}, u32[]{:S(2)}) collective-permute-start(f32[128,1024]{1,0:T(8,128)S(1)} %copy-done.6), channel_id=1, source_target_pairs={{0,7},{1,0},{2,1},{3,2},{4,3},{5,4},{6,5},{7,6},{8,15},{9,8},{10,9... | collective-permute-start | bytes 1572872 | tf_op jit(solution)/shard_map/ppermute | solution.py:48
  21.1 21.3 %collective-permute-start.3 = (f32[128,1024]{1,0:T(8,128)S(1)}, f32[128,1024]{1,0:T(8,128)S(1)}, u32[]{:S(2)}, u32[]{:S(2)}) collective-permute-start(f32[128,1024]{1,0:T(8,128)S(1)} %copy-done.6), channel_id=1, source_target_pairs={{0,1},{1,2},{2,3},{3,4},{4,5},{5,6},{6,7},{7,0},{8,9},{9,10},{10,1... | collective-permute-start | bytes 1572872 | tf_op jit(solution)/shard_map/ppermute | solution.py:47
  29.9 21.6 %collective-permute-start.2 = (f32[128,1024]{1,0:T(8,128)S(1)}, f32[128,1024]{1,0:T(8,128)S(1)}, u32[]{:S(2)}, u32[]{:S(2)}) collective-permute-start(f32[128,1024]{1,0:T(8,128)S(1)} %collective-permute-done), channel_id=1, source_target_pairs={{0,7},{1,0},{2,1},{3,2},{4,3},{5,4},{6,5},{7,6},{8,15},{9,8},{10,9... | collective-permute-start | bytes 1572872 | tf_op jit(solution)/shard_map/ppermute | solution.py:50
  39.2 16.0 %collective-permute-start.4 = (f32[128,1024]{1,0:T(8,128)S(1)}, f32[128,1024]{1,0:T(8,128)S(1)}, u32[]{:S(2)}, u32[]{:S(2)}) collective-permute-start(f32[128,1024]{1,0:T(8,128)S(1)} %collective-permute-done), channel_id=1, source_target_pairs={{0,1},{1,2},{2,3},{3,4},{4,5},{5,6},{6,7},{7,0},{8,9},{9,10},{10,1... | collective-permute-start | bytes 1572872 | tf_op jit(solution)/shard_map/ppermute | solution.py:49
  39.2 23.5 %collective-permute-start.5 = (f32[128,1024]{1,0:T(8,128)S(1)}, f32[128,1024]{1,0:T(8,128)S(1)}, u32[]{:S(2)}, u32[]{:S(2)}) collective-permute-start(f32[128,1024]{1,0:T(8,128)S(1)} %collective-permute-done.1), channel_id=1, source_target_pairs={{0,7},{1,0},{2,1},{3,2},{4,3},{5,4},{6,5},{7,6},{8,15},{9,8},{10,9... | collective-permute-start | bytes 1572872 | tf_op jit(solution)/shard_map/ppermute | solution.py:48
  42.5 24.0 %collective-permute-start.7 = (f32[128,1024]{1,0:T(8,128)S(1)}, f32[128,1024]{1,0:T(8,128)S(1)}, u32[]{:S(2)}, u32[]{:S(2)}) collective-permute-start(f32[128,1024]{1,0:T(8,128)S(1)} %collective-permute-done.3), channel_id=1, source_target_pairs={{0,1},{1,2},{2,3},{3,4},{4,5},{5,6},{6,7},{7,0},{8,9},{9,10},{10,1... | collective-permute-start | bytes 1572872 | tf_op jit(solution)/shard_map/ppermute | solution.py:47
  51.5 22.5 %collective-permute-start.6 = (f32[128,1024]{1,0:T(8,128)S(1)}, f32[128,1024]{1,0:T(8,128)S(1)}, u32[]{:S(2)}, u32[]{:S(2)}) collective-permute-start(f32[128,1024]{1,0:T(8,128)S(1)} %collective-permute-done.2), channel_id=1, source_target_pairs={{0,7},{1,0},{2,1},{3,2},{4,3},{5,4},{6,5},{7,6},{8,15},{9,8},{10,9... | collective-permute-start | bytes 1572872 | tf_op jit(solution)/shard_map/ppermute | solution.py:50
  55.2 22.5 %collective-permute-start.8 = (f32[128,1024]{1,0:T(8,128)S(1)}, f32[128,1024]{1,0:T(8,128)S(1)}, u32[]{:S(2)}, u32[]{:S(2)}) collective-permute-start(f32[128,1024]{1,0:T(8,128)S(1)} %collective-permute-done.4), channel_id=1, source_target_pairs={{0,1},{1,2},{2,3},{3,4},{4,5},{5,6},{6,7},{7,0},{8,9},{9,10},{10,1... | collective-permute-start | bytes 1572872 | tf_op jit(solution)/shard_map/ppermute | solution.py:49
  62.8 33.5 %collective-permute-start.9 = (f32[128,1024]{1,0:T(8,128)S(1)}, f32[128,1024]{1,0:T(8,128)S(1)}, u32[]{:S(2)}, u32[]{:S(2)}) collective-permute-start(f32[128,1024]{1,0:T(8,128)S(1)} %collective-permute-done.5), channel_id=1, source_target_pairs={{0,7},{1,0},{2,1},{3,2},{4,3},{5,4},{6,5},{7,6},{8,15},{9,8},{10,9... | collective-permute-start | bytes 1572872 | tf_op jit(solution)/shard_map/ppermute | solution.py:48
  66.5 22.5 %collective-permute-start.11 = (f32[128,1024]{1,0:T(8,128)S(1)}, f32[128,1024]{1,0:T(8,128)S(1)}, u32[]{:S(2)}, u32[]{:S(2)}) collective-permute-start(f32[128,1024]{1,0:T(8,128)S(1)} %collective-permute-done.7), channel_id=1, source_target_pairs={{0,1},{1,2},{2,3},{3,4},{4,5},{5,6},{6,7},{7,0},{8,9},{9,10},{10,1... | collective-permute-start | bytes 1572872 | tf_op jit(solution)/shard_map/ppermute | solution.py:47
  74.0 18.6 %collective-permute-start.10 = (f32[128,1024]{1,0:T(8,128)S(1)}, f32[128,1024]{1,0:T(8,128)S(1)}, u32[]{:S(2)}, u32[]{:S(2)}) collective-permute-start(f32[128,1024]{1,0:T(8,128)S(1)} %collective-permute-done.6), channel_id=1, source_target_pairs={{0,7},{1,0},{2,1},{3,2},{4,3},{5,4},{6,5},{7,6},{8,15},{9,8},{10,9... | collective-permute-start | bytes 1572872 | tf_op jit(solution)/shard_map/ppermute | solution.py:50
  77.7 22.5 %collective-permute-start.12 = (f32[128,1024]{1,0:T(8,128)S(1)}, f32[128,1024]{1,0:T(8,128)S(1)}, u32[]{:S(2)}, u32[]{:S(2)}) collective-permute-start(f32[128,1024]{1,0:T(8,128)S(1)} %collective-permute-done.8), channel_id=1, source_target_pairs={{0,1},{1,2},{2,3},{3,4},{4,5},{5,6},{6,7},{7,0},{8,9},{9,10},{10,1... | collective-permute-start | bytes 1572872 | tf_op jit(solution)/shard_map/ppermute | solution.py:49
  88.9 17.9 %collective-permute-start.13 = (f32[128,1024]{1,0:T(8,128)S(1)}, f32[128,1024]{1,0:T(8,128)S(1)}, u32[]{:S(2)}, u32[]{:S(2)}) collective-permute-start(f32[128,1024]{1,0:T(8,128)S(1)} %collective-permute-done.11), channel_id=1, source_target_pairs={{0,1},{1,2},{2,3},{3,4},{4,5},{5,6},{6,7},{7,0},{8,9},{9,10},{10,1... | collective-permute-start | bytes 1572872 | tf_op jit(solution)/shard_map/ppermute | solution.py:54
  92.6 14.4 %collective-permute-start.14 = (f32[128,1024]{1,0:T(8,128)S(1)}, f32[128,1024]{1,0:T(8,128)S(1)}, u32[]{:S(2)}, u32[]{:S(2)}) collective-permute-start(f32[128,1024]{1,0:T(8,128)S(1)} %collective-permute-done.10), channel_id=1, source_target_pairs={{0,7},{1,0},{2,1},{3,2},{4,3},{5,4},{6,5},{7,6},{8,15},{9,8},{10,9... | collective-permute-start | bytes 1572872 | tf_op jit(solution)/shard_map/ppermute | solution.py:55
  113.8 2.2 %copy-start.9 = (bf16[1024,2304]{1,0:T(8,128)(2,1)}, bf16[1024,2304]{1,0:T(8,128)(2,1)S(1)}, u32[]{:S(2)}) copy-start(bf16[1024,2304]{1,0:T(8,128)(2,1)S(1)} %get-tuple-element.7) | copy-start | bytes 14155780
  114.1 2.2 %copy-start.4 = (bf16[512,1024]{1,0:T(8,128)(2,1)S(1)}, bf16[512,1024]{1,0:T(8,128)(2,1)}, u32[]{:S(2)}) copy-start(bf16[512,1024]{1,0:T(8,128)(2,1)} %get-tuple-element.19) | copy-start | bytes 3145732
  114.1 2.9 %copy-start.5 = (bf16[512,1024]{1,0:T(8,128)(2,1)S(1)}, bf16[512,1024]{1,0:T(8,128)(2,1)}, u32[]{:S(2)}) copy-start(bf16[512,1024]{1,0:T(8,128)(2,1)} %get-tuple-element.20) | copy-start | bytes 3145732
  117.0 5.0 %copy-start.2 = (bf16[512,1024]{1,0:T(8,128)(2,1)S(1)}, bf16[512,1024]{1,0:T(8,128)(2,1)}, u32[]{:S(2)}) copy-start(bf16[512,1024]{1,0:T(8,128)(2,1)} %get-tuple-element.17) | copy-start | bytes 3145732
  117.0 5.0 %copy-start.3 = (bf16[512,1024]{1,0:T(8,128)(2,1)S(1)}, bf16[512,1024]{1,0:T(8,128)(2,1)}, u32[]{:S(2)}) copy-start(bf16[512,1024]{1,0:T(8,128)(2,1)} %get-tuple-element.18) | copy-start | bytes 3145732
  117.0 12.0 %slice-start = ((s8[4718592]{0:T(1024)(128)(4,1)}), s8[4194304]{0:T(1024)(128)(4,1)S(1)}, s32[]{:S(2)}) async-start(s8[4718592]{0:T(1024)(128)(4,1)} %bitcast.27), calls=%async_computation.1 | async-start | bytes 8388608
  122.1 5.1 %copy-start.7 = (bf16[256,1024]{1,0:T(8,128)(2,1)S(1)}, bf16[256,1024]{1,0:T(8,128)(2,1)}, u32[]{:S(2)}) copy-start(bf16[256,1024]{1,0:T(8,128)(2,1)} %get-tuple-element.21) | copy-start | bytes 1572868
  122.1 5.1 %copy-start.8 = (bf16[256,1024]{1,0:T(8,128)(2,1)S(1)}, bf16[256,1024]{1,0:T(8,128)(2,1)}, u32[]{:S(2)}) copy-start(bf16[256,1024]{1,0:T(8,128)(2,1)} %get-tuple-element.22) | copy-start | bytes 1572868
  122.1 7.0 %slice-start.1 = ((s8[4718592]{0:T(1024)(128)(4,1)}), s8[524288]{0:T(1024)(128)(4,1)S(1)}, s32[]{:S(2)}) async-start(s8[4718592]{0:T(1024)(128)(4,1)} %bitcast.27), calls=%async_computation.2 | async-start | bytes 1048576
  129.1 9.3 %copy-start.1 = (f32[512]{0:T(512)S(1)}, f32[512]{0:T(512)}, u32[]{:S(2)}) copy-start(f32[512]{0:T(512)} %param.9) | copy-start | bytes 6148
Sparse Core Ops, SparseCore 0:
  14.8 56.9 all-gather.1
